TPU v7x, 256 devices: a whole 4x4x8 slice. The times are simulated.
256 devices in a mesh: tok: 64 (over y, z, core), head: 4 (over x).
Axes of the slice: x: 4, y: 4, z: 8, core: 2. Of those that a mesh axis runs over, the one named last changes fastest.
Arguments:
- hidden: bfloat16 [2048, 2048], P('tok', 'head'), may hold values from -24 to 24
- attn_gain: float32 [2048], replicated, may hold values from 0.1 to 1.9
- w_query: bfloat16 [2048, 3072], P(None, 'head'), may hold values from -0.125 to 0.125
- w_latent: bfloat16 [2048, 576], P('head'), may hold values from -0.125 to 0.125
- w_key_up: bfloat16 [16, 128, 512], P('head'), may hold values from -0.5 to 0.5
- w_value_up: bfloat16 [16, 512, 128], P('head'), may hold values from -1 to 1
- w_out: bfloat16 [2048, 2048], P('head'), may hold values from -0.125 to 0.125
- latent_cache: bfloat16 [638976, 576], P(('tok', 'head')), may hold values from -6 to 6
- cache_lengths: int32 [2048], P('tok'), may hold values from 144 to 2048, as said below
- request_slot: int32 [2048], P('tok'), may hold values from 0 to 2047, as said below
- ffn_gain: float32 [2048], P('head'), may hold values from 0.1 to 1.9
- w_router: bfloat16 [2048, 64], P('head'), may hold values from -0.25 to 0.25
- routes: int32 [2048, 6], P('tok'), may hold values from 0 to 63, all different within a row; in each aligned block of 32 rows (0 to 31, 32 to 63, ...) at most 6 rows name the same one
- expert_gate: bfloat16 [64, 2048, 1408], P('tok', None, 'head'), may hold values from -0.125 to 0.125
- expert_up: bfloat16 [64, 2048, 1408], P('tok', None, 'head'), may hold values from -0.125 to 0.125
- expert_down: bfloat16 [64, 1408, 2048], P('tok', 'head'), may hold values from -0.15625 to 0.15625
Outputs:
- new_entry: bfloat16 [2048, 576], P('tok')
- attended: bfloat16 [2048, 2048], P('tok', 'head')
- expert_mix: bfloat16 [2048, 2048], P('tok', 'head')
Inputs may be any that keep to these rules, and one draw needn't show every extreme that they name: `request_slot`: a permutation of the 2048 slots; slot s lies on owner s // 32, so every owner holds 32 slots; the requests of one device name at most 1 slots of one owner, and every device reaches that bound. `cache_lengths`: the caches of an owner's slots lie end to end in slot order at the start of that owner's 9984 rows of latent_cache; they fill at most 9984 rows, and some owner fills all of them. `routes`: each row names 6 different experts; in the rows of one device no expert is named more than 6 times.
All inputs are finite; a program needn't handle non-finite values.
Results may differ from a plain program's by a relative error of at most 0.028.
Values may be sent and summed in bfloat16 or wider, within the bound.
No kernel may reach another device: no remote copies, remote signals or barrier semaphores. Data moves between devices by JAX's collectives and lax.ppermute only.
A program may use at most 128 MiB of HBM per device.

v0:
```python
import jax
import jax.numpy as jnp
from jax import lax
from jax.sharding import PartitionSpec as P

D = 2048
NOPE = 128
ROPE = 64
LATENT = 512


NORM_EPS = 1e-06


def rotate_pairs(values, places):
    halfway = values.shape[-1] // 2
    freqs = 10000.0 ** (-jnp.arange(halfway, dtype=jnp.float32) / halfway)
    angles = places.astype(jnp.float32).reshape(places.shape + (1,) * (values.ndim - 1)) * freqs
    cosine = jnp.cos(angles)
    sine = jnp.sin(angles)
    first_half = values[..., :halfway]
    second_half = values[..., halfway:]
    return jnp.concatenate(
        [first_half * cosine - second_half * sine, first_half * sine + second_half * cosine],
        axis=-1,
    )


def owner_attend(all_heads, owner_lengths, latent_cache, head_index, factor):
    slot_rows = all_heads.shape[0]
    total_heads = all_heads.shape[1]
    probe_width = all_heads.shape[2]
    key_rows = latent_cache.shape[0]
    starts = jnp.cumsum(owner_lengths) - owner_lengths
    places = head_index * key_rows + jnp.arange(key_rows, dtype=jnp.int32)
    inside = (places[None, :] >= starts[:, None]) & (
        places[None, :] < (starts + owner_lengths)[:, None]
    )
    scores = factor * jnp.einsum(
        "qc,pc->qp",
        all_heads.reshape(slot_rows * total_heads, probe_width),
        latent_cache,
        preferred_element_type=jnp.float32,
    )
    scores = scores.reshape(slot_rows, total_heads, key_rows)
    weights = jnp.where(inside[:, None, :], jnp.exp(scores), 0.0).astype(jnp.bfloat16)
    numerator = jnp.einsum(
        "khp,pl->khl", weights, latent_cache[:, :LATENT], preferred_element_type=jnp.float32
    )
    denominator = jnp.sum(weights.astype(jnp.float32), axis=2)
    return (numerator, denominator)


def body(
    hidden,
    attn_gain,
    w_query,
    w_latent,
    w_key_up,
    w_value_up,
    w_out,
    latent_cache,
    cache_lengths,
    request_slot,
    ffn_gain,
    w_router,
    routes,
    expert_gate,
    expert_up,
    expert_down,
):
    local_rows = hidden.shape[0]
    quarter_width = hidden.shape[1]
    local_heads = w_key_up.shape[0]
    peer_count = lax.axis_size("tok")
    head_index = lax.axis_index("head")
    tok_index = lax.axis_index("tok")
    row_ids = jnp.arange(local_rows, dtype=jnp.int32)
    gathered = lax.all_gather(hidden, "head", axis=1, tiled=True)
    widened = gathered.astype(jnp.float32)
    inv_attn = lax.rsqrt(jnp.mean(widened * widened, axis=1, keepdims=True) + NORM_EPS)
    normed_attn = (widened * inv_attn * attn_gain).astype(jnp.bfloat16)
    normed_part = lax.dynamic_slice_in_dim(
        normed_attn, head_index * quarter_width, quarter_width, 1
    )
    compressed = lax.psum(
        jnp.dot(normed_part, w_latent, preferred_element_type=jnp.float32), "head"
    )
    latent_new = compressed[:, :LATENT]
    latent_new = latent_new * lax.rsqrt(
        jnp.mean(latent_new * latent_new, axis=1, keepdims=True) + NORM_EPS
    )
    new_entry = jnp.concatenate(
        [latent_new, rotate_pairs(compressed[:, LATENT:], cache_lengths)], axis=1
    ).astype(jnp.bfloat16)
    queries = jnp.dot(normed_attn, w_query, preferred_element_type=jnp.float32).astype(jnp.bfloat16)
    queries = queries.reshape(local_rows, local_heads, NOPE + ROPE)
    absorbed = jnp.einsum(
        "bhn,hnl->bhl", queries[:, :, :NOPE], w_key_up, preferred_element_type=jnp.float32
    ).astype(jnp.bfloat16)
    turned = rotate_pairs(queries[:, :, NOPE:].astype(jnp.float32), cache_lengths).astype(
        jnp.bfloat16
    )
    probes = jnp.concatenate([absorbed, turned], axis=2)
    factor = (NOPE + ROPE) ** (-0.5)
    self_score = factor * jnp.einsum(
        "bhc,bc->bh", probes, new_entry, preferred_element_type=jnp.float32
    )
    self_weight = jnp.exp(self_score).astype(jnp.bfloat16).astype(jnp.float32)
    per_owner = max(1, local_rows // peer_count)
    buffer_rows = peer_count * per_owner
    buffer_ids = jnp.arange(buffer_rows, dtype=jnp.int32)
    dest_owner = request_slot // local_rows
    earlier_same = (dest_owner[None, :] == dest_owner[:, None]) & (
        row_ids[None, :] < row_ids[:, None]
    )
    send_place = dest_owner * per_owner + jnp.sum(earlier_same.astype(jnp.int32), axis=1)
    all_probes, all_slots, all_lengths = (
        lax.all_gather(probes, "tok", axis=0, tiled=True),
        lax.all_gather(request_slot, "tok", axis=0, tiled=True),
        lax.all_gather(cache_lengths, "tok", axis=0, tiled=True),
    )
    total_rows = all_slots.shape[0]
    slot_hit = all_slots[None, :] == (tok_index * local_rows + row_ids)[:, None]
    request_at = jnp.sum(
        jnp.where(slot_hit, jnp.arange(total_rows, dtype=jnp.int32)[None, :], 0), axis=1
    )
    owner_probes = all_probes[request_at]
    owner_lengths = all_lengths[request_at]
    owned_here = (
        (all_slots // local_rows == tok_index).astype(jnp.int32).reshape(peer_count, local_rows)
    )
    prior_count = (jnp.cumsum(owned_here, axis=1) - owned_here).reshape(total_rows)
    back_index = request_at // local_rows * per_owner + prior_count[request_at]
    all_heads = lax.all_gather(owner_probes, "head", axis=1, tiled=True)
    numerator, denominator = owner_attend(
        all_heads, owner_lengths, latent_cache, head_index, factor
    )
    group_num, group_den = (
        lax.psum_scatter(numerator, "head", scatter_dimension=1, tiled=True),
        lax.psum_scatter(denominator, "head", scatter_dimension=1, tiled=True),
    )
    at_place = buffer_ids[:, None] == back_index[None, :]
    slot_of_place = jnp.sum(jnp.where(at_place, row_ids[None, :], 0), axis=1) + local_rows * (
        1 - jnp.max(at_place.astype(jnp.int32), axis=1)
    )
    padded_num = jnp.concatenate(
        [group_num, jnp.zeros((1, local_heads, LATENT), jnp.float32)], axis=0
    )
    padded_den = jnp.concatenate([group_den, jnp.zeros((1, local_heads), jnp.float32)], axis=0)
    got_num, got_den = (
        lax.all_to_all(
            padded_num[slot_of_place].reshape(peer_count, per_owner, local_heads, LATENT),
            "tok",
            split_axis=0,
            concat_axis=0,
            tiled=True,
        ),
        lax.all_to_all(
            padded_den[slot_of_place].reshape(peer_count, per_owner, local_heads),
            "tok",
            split_axis=0,
            concat_axis=0,
            tiled=True,
        ),
    )
    back_num = got_num.reshape(buffer_rows, local_heads, LATENT)
    back_den = got_den.reshape(buffer_rows, local_heads)
    total_num = back_num[send_place] + self_weight[:, :, None] * new_entry[:, None, :LATENT].astype(
        jnp.float32
    )
    total_den = back_den[send_place] + self_weight
    mixed_latent = (total_num / total_den[:, :, None]).astype(jnp.bfloat16)
    head_out = jnp.einsum(
        "bhl,hld->bhd", mixed_latent, w_value_up, preferred_element_type=jnp.float32
    ).astype(jnp.bfloat16)
    head_out = head_out.reshape(local_rows, local_heads * NOPE)
    attn_piece = lax.psum_scatter(
        jnp.dot(head_out, w_out, preferred_element_type=jnp.float32),
        "head",
        scatter_dimension=1,
        tiled=True,
    )
    attended = (hidden.astype(jnp.float32) + attn_piece).astype(jnp.bfloat16)
    attended_wide = attended.astype(jnp.float32)
    gained = (attended_wide * ffn_gain).astype(jnp.bfloat16)
    squares, logit_part = lax.psum(
        (
            jnp.sum(attended_wide * attended_wide, axis=1),
            jnp.dot(gained, w_router, preferred_element_type=jnp.float32),
        ),
        "head",
    )
    inv_ffn = lax.rsqrt(squares / D + NORM_EPS)
    logits = logit_part * inv_ffn[:, None]
    normed_ffn = (attended_wide * ffn_gain * inv_ffn[:, None]).astype(jnp.bfloat16)
    expert_count = w_router.shape[1]
    route_count = routes.shape[1]
    expert_ids = jnp.arange(expert_count, dtype=jnp.int32)
    named = routes[:, :, None] == expert_ids[None, None, :]
    picked = jnp.sum(jnp.where(named, logits[:, None, :], 0.0), axis=2)
    lifted = jnp.exp(picked)
    route_weight = lifted / jnp.sum(lifted, axis=1, keepdims=True)
    struck = jnp.max(named.astype(jnp.int32), axis=1)
    earlier_hits = jnp.cumsum(struck, axis=0) - struck
    capacity = min(local_rows, max(2, 2 * local_rows * route_count // expert_count))
    route_place = routes * capacity + jnp.take_along_axis(earlier_hits, routes, axis=1)
    slot_total = expert_count * capacity
    slot_ids = jnp.arange(slot_total, dtype=jnp.int32)
    filled = route_place[None, :, :] == slot_ids[:, None, None]
    source_token = jnp.sum(
        jnp.where(filled, row_ids[None, :, None], 0), axis=(1, 2)
    ) + local_rows * (1 - jnp.max(filled.astype(jnp.int32), axis=(1, 2)))
    full_rows = lax.all_gather(normed_ffn, "head", axis=1, tiled=True)
    padded_rows = jnp.concatenate(
        [full_rows, jnp.zeros((1, full_rows.shape[1]), jnp.bfloat16)], axis=0
    )
    arrived = lax.all_to_all(
        padded_rows[source_token].reshape(expert_count, capacity, full_rows.shape[1]),
        "tok",
        split_axis=0,
        concat_axis=0,
        tiled=True,
    )
    expert_in = arrived.reshape(peer_count * capacity, full_rows.shape[1])
    gate_value = jnp.dot(expert_in, expert_gate[0], preferred_element_type=jnp.float32)
    up_value = jnp.dot(expert_in, expert_up[0], preferred_element_type=jnp.float32)
    activity = (jax.nn.silu(gate_value) * up_value).astype(jnp.bfloat16)
    expert_share = lax.psum_scatter(
        jnp.dot(activity, expert_down[0], preferred_element_type=jnp.float32).astype(jnp.bfloat16),
        "head",
        scatter_dimension=1,
        tiled=True,
    )
    returned = lax.all_to_all(
        expert_share.reshape(peer_count, capacity, quarter_width),
        "tok",
        split_axis=0,
        concat_axis=0,
        tiled=True,
    )
    chosen_rows = returned.reshape(slot_total, quarter_width)[route_place]
    expert_mix = jnp.sum(route_weight[:, :, None] * chosen_rows.astype(jnp.float32), axis=1).astype(
        jnp.bfloat16
    )
    return (new_entry, attended, expert_mix)


def solution(mesh):
    in_specs = (
        P("tok", "head"),
        P(),
        P(None, "head"),
        P("head", None),
        P("head", None, None),
        P("head", None, None),
        P("head", None),
        P(("tok", "head"), None),
        P("tok"),
        P("tok"),
        P("head"),
        P("head", None),
        P("tok", None),
        P("tok", None, "head"),
        P("tok", None, "head"),
        P("tok", "head", None),
    )
    out_specs = (P("tok", None), P("tok", "head"), P("tok", "head"))
    return jax.shard_map(body, mesh=mesh, in_specs=in_specs, out_specs=out_specs, check_vma=False)
```

profile of v0, /device:TPU:1, one launch (start us, length us, event | category | flops | bytes accessed | tf_op | source)
XLA Modules:
  0.0 640.7 jit_solution(2848119772154112607)
XLA Ops:
  7.2 10.6 %all_gather.18 = bf16[32,2048]{1,0:T(8,128)(2,1)S(1)} all-gather(bf16[32,512]{1,0:T(8,128)(2,1)} %param.16), channel_id=1, replica_groups=mesh['tok'=64,'head'=4] {'head'}, dimensions={1}, use_global_device_ids=true | all-gather | bytes 163840 | tf_op jit(solution)/shard_map/all_gather | solution.py:79
  18.0 0.8 fusion.28
  18.8 2.0 fusion.45
  21.8 1.2 fusion.16
  23.0 46.7 %all-reduce.10.cloned.1.call-done = f32[32,576]{1,0:T(8,128)} async-done(((f32[32,576]{1,0:T(8,128)}), f32[32,576]{1,0:T(8,128)}) %all-reduce.10.cloned.1.call-update) | async-done | bytes 73744 | tf_op jit(solution)/shard_map/psum | solution.py:86
  69.7 1.5 multiply_cosine_fusion
  74.0 246.6 %all-reduce.6 = (s32[2048]{0:T(1024)S(1)}, s32[2048]{0:T(1024)S(1)}) all-reduce(s32[2048]{0:T(1024)S(1)} %dynamic-update-slice.1, s32[2048]{0:T(1024)S(1)} %dynamic-update-slice), channel_id=1, replica_groups=mesh['tok'=64,'head'=4] {'tok'}, use_global_device_ids=true, to_apply=%add.4 | all-reduce | flops 4096 | bytes 32768
  322.4 2.4 copy.92
  324.8 14.7 %copy.84 = bf16[2048,4,576]{2,1,0:T(4,128)(2,1)} copy(bf16[2048,4,576]{2,0,1:T(8,128)(2,1)} %all-gather.3.cloned.1.call-done) | data formatting | bytes 18874368 | tf_op jit(solution)/shard_map/all_gather | solution.py:119
  339.5 4.7 gather_fusion.1
  344.3 10.5 %all-gather = bf16[32,16,576]{2,0,1:T(8,128)(2,1)S(1)} all-gather(bf16[32,4,576]{2,0,1:T(8,128)(2,1)S(1)} %copy.85), channel_id=2, replica_groups=mesh['tok'=64,'head'=4] {'head'}, dimensions={1}, use_global_device_ids=true | all-gather | bytes 737280 | tf_op jit(solution)/shard_map/all_gather | solution.py:135
  355.0 6.3 convert_reduce_fusion
  361.3 4.4 copy.87
  365.7 4.1 fusion
  369.8 1.6 copy.89
  374.4 13.0 %all-reduce.5 = f32[32,16]{1,0:T(8,128)S(1)} all-reduce(f32[32,16]{1,0:T(8,128)S(1)} %reduce_sum.110), channel_id=4, replica_groups=mesh['tok'=64,'head'=4] {'head'}, use_global_device_ids=true, to_apply=%region_11.12.clone | all-reduce | flops 512 | bytes 4096
  387.5 1.2 gather_fusion.5
  388.7 16.3 %all-to-all-start.1 = ((f32[64,1,4]{2,1,0:T(1,128)}), f32[64,1,4]{2,1,0:T(1,128)S(1)}, u32[]{:S(2)}, u32[]{:S(2)}) async-start(f32[64,1,4]{2,1,0:T(1,128)} %bitcast.18), calls=%async_computation.2 | async-start | bytes 65536 | tf_op jit(solution)/shard_map/all_to_all | solution.py:159
  405.8 1.6 gather_fusion.9
  408.1 1.1 copy.90
  409.3 1.8 gather_fusion.3
  411.1 3.3 all-to-all-done.1
  414.4 7.3 %all-to-all-start = ((f32[64,1,4,512]{3,2,1,0:T(4,128)}), f32[64,1,4,512]{3,2,1,0:T(4,128)}, u32[]{:S(2)}, u32[]{:S(2)}) async-start(f32[64,1,4,512]{3,2,1,0:T(4,128)} %bitcast.72), calls=%async_computation.1 | async-start | bytes 1048576 | tf_op jit(solution)/shard_map/all_to_all | solution.py:152
  423.2 0.8 fusion.73
  424.0 1.2 fusion.30
  426.5 12.4 %all-to-all-done = f32[64,1,4,512]{3,2,1,0:T(4,128)} async-done(((f32[64,1,4,512]{3,2,1,0:T(4,128)}), f32[64,1,4,512]{3,2,1,0:T(4,128)}, u32[]{:S(2)}, u32[]{:S(2)}) %all-to-all-start) | async-done | bytes 524320 | tf_op jit(solution)/shard_map/all_to_all | solution.py:152
  438.9 1.9 gather_fusion.4
  440.8 1.0 fusion.29
  441.9 1.2 fusion.17
  443.2 2.8 fusion.40
  447.0 14.9 %reduce-scatter.7.cloned.1.call-done = f32[32,512]{1,0:T(8,128)} async-done(((f32[32,2048]{1,0:T(8,128)}), f32[32,512]{1,0:T(8,128)}) %reduce-scatter.7.cloned.1.call-update) | async-done | bytes 65552 | tf_op jit(solution)/shard_map/reduce_scatter | solution.py:178
  461.9 1.0 fusion.37
  463.1 11.8 %all-reduce.7 = (f32[32]{0:T(128)S(1)}, f32[32,64]{1,0:T(8,128)S(1)}) all-reduce(f32[32]{0:T(128)S(1)} %get-tuple-element.13, f32[32,64]{1,0:T(8,128)S(1)} %fusion.38), channel_id=1, replica_groups=mesh['tok'=64,'head'=4] {'head'}, use_global_device_ids=true, to_apply=%region_15.16 | all-reduce | flops 2080 | bytes 16640 | tf_op jit(solution)/shard_map/psum | solution.py:187
  474.9 9.3 %all_gather.23 = bf16[32,2048]{1,0:T(8,128)(2,1)S(1)} all-gather(bf16[32,512]{1,0:T(8,128)(2,1)S(1)} %fusion.36), channel_id=1, replica_groups=mesh['tok'=64,'head'=4] {'head'}, dimensions={1}, use_global_device_ids=true | all-gather | bytes 163840 | tf_op jit(solution)/shard_map/all_gather | solution.py:214
  484.3 3.1 gather_fusion.7
  487.4 3.7 reshape.358
  491.1 70.4 %all_to_all.20 = bf16[64,6,2048]{2,1,0:T(8,128)(2,1)} all-to-all(bf16[64,6,2048]{2,1,0:T(8,128)(2,1)} %reshape.358), channel_id=1, replica_groups=mesh['tok'=64,'head'=4] {'tok'}, dimensions={0} | all-to-all | bytes 3145728 | tf_op jit(solution)/shard_map/all_to_all | solution.py:218
  561.5 3.7 reshape.359
  565.3 3.6 fusion.8
  568.8 5.5 convolution_convert_fusion
  574.5 22.3 %reduce-scatter.9.cloned.1.call-done = bf16[384,512]{1,0:T(8,128)(2,1)} async-done(((bf16[384,2048]{1,0:T(8,128)(2,1)}), bf16[384,512]{1,0:T(8,128)(2,1)}) %reduce-scatter.9.cloned.1.call-update) | async-done | bytes 393232 | tf_op jit(solution)/shard_map/reduce_scatter | solution.py:229
  596.8 1.9 reshape.360
  598.7 11.7 %all-to-all-start.3 = ((bf16[64,6,512]{2,1,0:T(8,128)(2,1)}), bf16[64,6,512]{2,1,0:T(8,128)(2,1)}, u32[]{:S(2)}, u32[]{:S(2)}) async-start(bf16[64,6,512]{2,1,0:T(8,128)(2,1)} %reshape.360), calls=%async_computation.6 | async-start | bytes 1048576 | tf_op jit(solution)/shard_map/all_to_all | solution.py:235
  612.1 15.5 %all-to-all-done.3 = bf16[64,6,512]{2,1,0:T(8,128)(2,1)} async-done(((bf16[64,6,512]{2,1,0:T(8,128)(2,1)}), bf16[64,6,512]{2,1,0:T(8,128)(2,1)}, u32[]{:S(2)}, u32[]{:S(2)}) %all-to-all-start.3) | async-done | bytes 393248 | tf_op jit(solution)/shard_map/all_to_all | solution.py:235
  627.6 1.2 reshape.361
  628.8 1.7 gather_fusion.8
  630.5 1.8 reshape.445
  632.2 1.9 multiply_reduce_fusion
  (127 shorter events, 14.8 us)
Async XLA Ops:
  7.2 13.8 %copy-start = (bf16[2048,768]{1,0:T(8,128)(2,1)S(1)}, bf16[2048,768]{1,0:T(8,128)(2,1)}, u32[]{:S(2)}) copy-start(bf16[2048,768]{1,0:T(8,128)(2,1)} %param.18) | copy-start | bytes 9437188
  7.2 62.6 %all-reduce.10.cloned.1.call-start = ((), (), s32[]{:S(2)}) async-start(), calls=%async_computation.7 | async-start | bytes 163840 | tf_op jit(solution)/shard_map/psum | solution.py:86
  18.8 2.9 copy-start.14
  20.8 51.4 %copy-start.17 = (u32[256]{0:T(256)S(1)}, u32[256]{0:T(256)}, u32[]{:S(2)}) copy-start(u32[256]{0:T(256)} %constant.148) | copy-start | bytes 3076
  20.9 52.9 %copy-start.15 = (s32[32]{0:T(128)S(1)}, s32[32]{0:T(128)}, u32[]{:S(2)}) copy-start(s32[32]{0:T(128)} %param.25) | copy-start | bytes 388
  20.9 303.9 %all-gather.3.cloned.1.call-start = ((), (), s32[]{:S(2)}) async-start(), calls=%async_computation.8 | async-start | bytes 10649600 | tf_op jit(solution)/shard_map/all_gather | solution.py:119
  72.1 336.0 %reduce-scatter.5.cloned.1.call-start = ((), (), s32[]{:S(2)}) async-start(), calls=%async_computation.9 | async-start | bytes 1310720 | tf_op jit(solution)/shard_map/reduce_scatter | solution.py:140
  344.2 10.7 %copy-start.1 = (pred[512,2496]{0,1:T(32,128)(4,1)S(1)}, pred[512,2496]{0,1:T(32,128)(4,1)}, u32[]{:S(2)}) copy-start(pred[512,2496]{0,1:T(32,128)(4,1)} %copy.92) | copy-start | bytes 3833860
  369.8 1.7 copy-start.9
  369.8 2.8 copy-start.16
  374.0 31.8 %copy-start.13 = (s32[1024]{0:T(1024)}, s32[1024]{0:T(1024)S(1)}, u32[]{:S(2)}) copy-start(s32[1024]{0:T(1024)S(1)} %pad_clamp_fusion.3) | copy-start | bytes 12292
  388.7 25.7 %all-to-all-start.1 = ((f32[64,1,4]{2,1,0:T(1,128)}), f32[64,1,4]{2,1,0:T(1,128)S(1)}, u32[]{:S(2)}, u32[]{:S(2)}) async-start(f32[64,1,4]{2,1,0:T(1,128)} %bitcast.18), calls=%async_computation.2 | async-start | bytes 65536 | tf_op jit(solution)/shard_map/all_to_all | solution.py:159
  407.4 14.4 %copy-start.2 = (f32[32,576]{1,0:T(8,128)S(1)}, f32[32,576]{1,0:T(8,128)}, u32[]{:S(2)}) copy-start(f32[32,576]{1,0:T(8,128)} %all-reduce.10.cloned.1.call-done) | copy-start | bytes 221188
  414.4 24.5 %all-to-all-start = ((f32[64,1,4,512]{3,2,1,0:T(4,128)}), f32[64,1,4,512]{3,2,1,0:T(4,128)}, u32[]{:S(2)}, u32[]{:S(2)}) async-start(f32[64,1,4,512]{3,2,1,0:T(4,128)} %bitcast.72), calls=%async_computation.1 | async-start | bytes 1048576 | tf_op jit(solution)/shard_map/all_to_all | solution.py:152
  421.7 40.2 %reduce-scatter.7.cloned.1.call-start = ((), (), s32[]{:S(2)}) async-start(), calls=%async_computation.10 | async-start | bytes 327680 | tf_op jit(solution)/shard_map/reduce_scatter | solution.py:178
  422.6 0.6 copy-start.4
  440.8 21.1 %copy-start.6 = (bf16[32,512]{1,0:T(8,128)(2,1)S(1)}, bf16[32,512]{1,0:T(8,128)(2,1)}, u32[]{:S(2)}) copy-start(bf16[32,512]{1,0:T(8,128)(2,1)} %param.16) | copy-start | bytes 98308
  440.8 22.1 %copy-start.8 = (bf16[512,64]{0,1:T(8,128)(2,1)S(1)}, bf16[512,64]{0,1:T(8,128)(2,1)}, u32[]{:S(2)}) copy-start(bf16[512,64]{0,1:T(8,128)(2,1)} %param.27) | copy-start | bytes 196612
  440.8 22.1 %copy-start.11 = (f32[512]{0:T(512)S(1)}, f32[512]{0:T(512)}, u32[]{:S(2)}) copy-start(f32[512]{0:T(512)} %param.26) | copy-start | bytes 6148
  441.9 33.0 %copy-start.12 = (f32[512]{0:T(512)S(1)}, f32[512]{0:T(512)}, u32[]{:S(2)}) copy-start(f32[512]{0:T(512)} %param.26) | copy-start | bytes 6148
  445.9 150.9 %reduce-scatter.9.cloned.1.call-start = ((), (), s32[]{:S(2)}) async-start(), calls=%async_computation.11 | async-start | bytes 1966080 | tf_op jit(solution)/shard_map/reduce_scatter | solution.py:229
  462.9 12.0 %copy-start.3 = (bf16[32,512]{1,0:T(8,128)(2,1)}, bf16[32,512]{1,0:T(8,128)(2,1)S(1)}, u32[]{:S(2)}) copy-start(bf16[32,512]{1,0:T(8,128)(2,1)S(1)} %get-tuple-element.14) | copy-start | bytes 98308
  574.3 36.1 %copy-start.5 = (bf16[32,512]{1,0:T(8,128)(2,1)S(1)}, bf16[32,512]{1,0:T(8,128)(2,1)}, u32[]{:S(2)}) copy-start(bf16[32,512]{1,0:T(8,128)(2,1)} %copy-done.4) | copy-start | bytes 98308
  574.3 36.1 %copy-start.7 = (bf16[32,32]{1,0:T(8,128)(2,1)S(1)}, bf16[32,32]{1,0:T(8,128)(2,1)}, u32[]{:S(2)}) copy-start(bf16[32,32]{1,0:T(8,128)(2,1)} %get-tuple-element.26) | copy-start | bytes 6148
  574.3 36.9 %copy-start.10 = (s32[32,6]{0,1:T(8,128)S(1)}, s32[32,6]{0,1:T(8,128)}, u32[]{:S(2)}) copy-start(s32[32,6]{0,1:T(8,128)} %param.28) | copy-start | bytes 2308
  598.7 28.9 %all-to-all-start.3 = ((bf16[64,6,512]{2,1,0:T(8,128)(2,1)}), bf16[64,6,512]{2,1,0:T(8,128)(2,1)}, u32[]{:S(2)}, u32[]{:S(2)}) async-start(bf16[64,6,512]{2,1,0:T(8,128)(2,1)} %reshape.360), calls=%async_computation.6 | async-start | bytes 1048576 | tf_op jit(solution)/shard_map/all_to_all | solution.py:235
Sparse Core Ops, SparseCore 0:
  21.0 48.7 all-reduce.9
  72.5 89.3 all-gather.2
  371.5 25.9 reduce-scatter.4
  446.1 15.8 reduce-scatter.6
  574.5 22.2 reduce-scatter.8
where the time goes:
time: 642 us; the launch traced here: 641 us
  blocking collectives  372 us (58%)
  waiting for transfers between devices  115 us (18%)
  local copies, waits for them, and re-layouts  60 us (9%)
  starting transfers between devices  35.5 us (6%)
  matrix products  28.6 us (4%)
  between operations  15.6 us (2%)
  other arithmetic  13.3 us (2%)
    unnamed x2, blocking collectives  260 us
    all_to_all x1, blocking collectives, body(): lax.all_to_all(padded_rows[source_token].reshape(expert_count, capacity,...  70.4 us
    psum x1, waiting for transfers between devices, body(): lax.psum(jnp.dot(normed_part, w_latent, preferred_element_type=jnp.float3...  46.7 us
    reduce_scatter x1, waiting for transfers between devices, body(): lax.psum_scatter(jnp.dot(activity, expert_down[0], preferred_element_type...  22.3 us
    all_to_all x1, starting transfers between devices, body(): lax.all_to_all(padded_den[slot_of_place].reshape(peer_count, per_owner, l...  16.3 us
    all_to_all x1, waiting for transfers between devices, body(): lax.all_to_all(expert_share.reshape(peer_count, capacity, quarter_width),...  15.5 us
    reduce_scatter x1, waiting for transfers between devices, body(): lax.psum_scatter(jnp.dot(head_out, w_out, preferred_element_type=jnp.floa...  14.9 us
    all_gather x1, local copies, waits for them, and re-layouts, body(): lax.all_gather(probes, 'tok', axis=0, tiled=True)  14.7 us
  transfers between devices with their start and end apart: 8, of which 6 were waited for; matrix products, arithmetic and copies ran while one was open for 4% of the time, Pallas kernels for 0%

commit v1 on v0

--- a/solution.py
+++ b/solution.py
@@ -103,77 +103,64 @@
     )
     probes = jnp.concatenate([absorbed, turned], axis=2)
     factor = (NOPE + ROPE) ** (-0.5)
-    self_score = factor * jnp.einsum(
-        "bhc,bc->bh", probes, new_entry, preferred_element_type=jnp.float32
-    )
-    self_weight = jnp.exp(self_score).astype(jnp.bfloat16).astype(jnp.float32)
-    per_owner = max(1, local_rows // peer_count)
-    buffer_rows = peer_count * per_owner
-    buffer_ids = jnp.arange(buffer_rows, dtype=jnp.int32)
+    owner_ids = jnp.arange(peer_count, dtype=jnp.int32)
     dest_owner = request_slot // local_rows
-    earlier_same = (dest_owner[None, :] == dest_owner[:, None]) & (
-        row_ids[None, :] < row_ids[:, None]
-    )
-    send_place = dest_owner * per_owner + jnp.sum(earlier_same.astype(jnp.int32), axis=1)
-    all_probes, all_slots, all_lengths = (
-        lax.all_gather(probes, "tok", axis=0, tiled=True),
-        lax.all_gather(request_slot, "tok", axis=0, tiled=True),
-        lax.all_gather(cache_lengths, "tok", axis=0, tiled=True),
-    )
-    total_rows = all_slots.shape[0]
-    slot_hit = all_slots[None, :] == (tok_index * local_rows + row_ids)[:, None]
-    request_at = jnp.sum(
-        jnp.where(slot_hit, jnp.arange(total_rows, dtype=jnp.int32)[None, :], 0), axis=1
-    )
-    owner_probes = all_probes[request_at]
-    owner_lengths = all_lengths[request_at]
-    owned_here = (
-        (all_slots // local_rows == tok_index).astype(jnp.int32).reshape(peer_count, local_rows)
-    )
-    prior_count = (jnp.cumsum(owned_here, axis=1) - owned_here).reshape(total_rows)
-    back_index = request_at // local_rows * per_owner + prior_count[request_at]
+    goes_to = dest_owner[None, :] == owner_ids[:, None]
+    sent_any = jnp.max(goes_to.astype(jnp.int32), axis=1)
+    sent_row = jnp.sum(jnp.where(goes_to, row_ids[None, :], 0), axis=1) + local_rows * (1 - sent_any)
+    packed = jnp.concatenate([probes, new_entry[:, None, :]], axis=1)
+    packed = jnp.concatenate(
+        [packed, jnp.zeros((1,) + packed.shape[1:], jnp.bfloat16)], axis=0
+    )
+    send_ints = jnp.stack(
+        [
+            jnp.where(sent_any > 0, request_slot[jnp.minimum(sent_row, local_rows - 1)], -1),
+            cache_lengths[jnp.minimum(sent_row, local_rows - 1)],
+        ],
+        axis=1,
+    )
+    got_packed = lax.all_to_all(packed[sent_row], "tok", 0, 0, tiled=True)
+    got_ints = lax.all_to_all(send_ints, "tok", 0, 0, tiled=True)
+    got_slot = got_ints[:, 0]
+    local_slot = got_slot - tok_index * local_rows
+    slot_sel = local_slot[None, :] == row_ids[:, None]
+    src_of_slot = jnp.sum(jnp.where(slot_sel, owner_ids[None, :], 0), axis=1)
+    owner_packed = got_packed[src_of_slot]
+    owner_probes = owner_packed[:, :local_heads]
+    owner_new = owner_packed[:, local_heads]
+    owner_lengths = got_ints[src_of_slot, 1]
     all_heads = lax.all_gather(owner_probes, "head", axis=1, tiled=True)
     numerator, denominator = owner_attend(
         all_heads, owner_lengths, latent_cache, head_index, factor
     )
-    group_num, group_den = (
-        lax.psum_scatter(numerator, "head", scatter_dimension=1, tiled=True),
-        lax.psum_scatter(denominator, "head", scatter_dimension=1, tiled=True),
-    )
-    at_place = buffer_ids[:, None] == back_index[None, :]
-    slot_of_place = jnp.sum(jnp.where(at_place, row_ids[None, :], 0), axis=1) + local_rows * (
-        1 - jnp.max(at_place.astype(jnp.int32), axis=1)
-    )
-    padded_num = jnp.concatenate(
-        [group_num, jnp.zeros((1, local_heads, LATENT), jnp.float32)], axis=0
-    )
-    padded_den = jnp.concatenate([group_den, jnp.zeros((1, local_heads), jnp.float32)], axis=0)
-    got_num, got_den = (
-        lax.all_to_all(
-            padded_num[slot_of_place].reshape(peer_count, per_owner, local_heads, LATENT),
-            "tok",
-            split_axis=0,
-            concat_axis=0,
-            tiled=True,
-        ),
-        lax.all_to_all(
-            padded_den[slot_of_place].reshape(peer_count, per_owner, local_heads),
-            "tok",
-            split_axis=0,
-            concat_axis=0,
-            tiled=True,
-        ),
-    )
-    back_num = got_num.reshape(buffer_rows, local_heads, LATENT)
-    back_den = got_den.reshape(buffer_rows, local_heads)
-    total_num = back_num[send_place] + self_weight[:, :, None] * new_entry[:, None, :LATENT].astype(
+    joined = lax.psum_scatter(
+        jnp.concatenate([numerator, denominator[:, :, None]], axis=2),
+        "head",
+        scatter_dimension=1,
+        tiled=True,
+    )
+    group_num = joined[:, :, :LATENT]
+    group_den = joined[:, :, LATENT]
+    self_score = factor * jnp.einsum(
+        "bhc,bc->bh", owner_probes, owner_new, preferred_element_type=jnp.float32
+    )
+    self_weight = jnp.exp(self_score).astype(jnp.bfloat16).astype(jnp.float32)
+    total_num = group_num + self_weight[:, :, None] * owner_new[:, None, :LATENT].astype(
         jnp.float32
     )
-    total_den = back_den[send_place] + self_weight
+    total_den = group_den + self_weight
     mixed_latent = (total_num / total_den[:, :, None]).astype(jnp.bfloat16)
-    head_out = jnp.einsum(
+    owner_out = jnp.einsum(
         "bhl,hld->bhd", mixed_latent, w_value_up, preferred_element_type=jnp.float32
     ).astype(jnp.bfloat16)
+    owner_out = owner_out.reshape(local_rows, local_heads * NOPE)
+    owner_out = jnp.concatenate(
+        [owner_out, jnp.zeros((1, local_heads * NOPE), jnp.bfloat16)], axis=0
+    )
+    back_valid = (local_slot >= 0) & (local_slot < local_rows)
+    back_row = jnp.where(back_valid, local_slot, local_rows)
+    returned_out = lax.all_to_all(owner_out[back_row], "tok", 0, 0, tiled=True)
+    head_out = returned_out[dest_owner]
     head_out = head_out.reshape(local_rows, local_heads * NOPE)
     attn_piece = lax.psum_scatter(
         jnp.dot(head_out, w_out, preferred_element_type=jnp.float32),

time: 642 us -> 404 us (0.63)
  blocking collectives: 372 us -> 113 us
  waiting for transfers between devices: 115 us -> 136 us
  local copies, waits for them, and re-layouts: 60 us -> 43.6 us
  starting transfers between devices: 35.5 us -> 50.9 us
    unnamed x2 -> x0, blocking collectives: 260 us -> none
    reduce_scatter x1, waiting for transfers between devices: 0.01 us -> 21 us  [body(): lax.psum_scatter(jnp.concatenate([numerator, denominator[:, :, None]], ax...]
    all_to_all x2 -> x3, starting transfers between devices: 23.7 us -> 39.1 us  [the longest x1 13.1 us: body(): got_ints = lax.all_to_all(send_ints, 'tok', 0, 0, tiled=True)]
    all_gather x1 -> x0, local copies, waits for them, and re-layouts: 14.7 us -> none  [body(): lax.all_gather(probes, 'tok', axis=0, tiled=True)]
    all_to_all x2 -> x3, waiting for transfers between devices: 15.7 us -> 23.4 us  [the longest x1 15.7 us: body(): got_packed = lax.all_to_all(packed[sent_row], 'tok', 0, 0, tiled=True)]
  transfers between devices with their start and end apart: 8 -> 8, of which waited for: 6 -> 7; matrix products, arithmetic and copies ran while one was open for 4% -> 5% of each run, Pallas kernels for 0% -> 0%
where the time goes in v1:
time: 404 us; the launch traced here: 403 us
  waiting for transfers between devices  136 us (34%)
  blocking collectives  113 us (28%)
  starting transfers between devices  50.9 us (13%)
  local copies, waits for them, and re-layouts  43.6 us (11%)
  matrix products  30 us (7%)
  other arithmetic  14.6 us (4%)
  between operations  14.4 us (4%)
    all_to_all x1, blocking collectives, body(): lax.all_to_all(padded_rows[source_token].reshape(expert_count, capacity,...  70.4 us
    psum x1, waiting for transfers between devices, body(): lax.psum(jnp.dot(normed_part, w_latent, preferred_element_type=jnp.float3...  40.8 us
    reduce_scatter x1, waiting for transfers between devices, body(): lax.psum_scatter(jnp.dot(activity, expert_down[0], preferred_element_type...  21.5 us
    reduce_scatter x1, waiting for transfers between devices, body(): lax.psum_scatter(jnp.concatenate([numerator, denominator[:, :, None]], ax...  21 us
    all_to_all x1, waiting for transfers between devices, body(): got_packed = lax.all_to_all(packed[sent_row], 'tok', 0, 0, tiled=True)  15.7 us
    all_to_all x1, waiting for transfers between devices, body(): lax.all_to_all(expert_share.reshape(peer_count, capacity, quarter_width),...  15.5 us
    reduce_scatter x1, waiting for transfers between devices, body(): lax.psum_scatter(jnp.dot(head_out, w_out, preferred_element_type=jnp.floa...  14 us
    all_to_all x1, starting transfers between devices, body(): got_ints = lax.all_to_all(send_ints, 'tok', 0, 0, tiled=True)  13.1 us
  transfers between devices with their start and end apart: 8, of which 7 were waited for; matrix products, arithmetic and copies ran while one was open for 5% of the time, Pallas kernels for 0%

profile of v1, /device:TPU:1, one launch (start us, length us, event | category | flops | bytes accessed | tf_op | source)
XLA Modules:
  0.0 402.8 jit_solution(13905377801501472798)
XLA Ops:
  7.2 1.4 compare_select_fusion.3
  8.7 1.4 gather_fusion
  10.1 1.4 gather_fusion.1
  12.3 13.1 %all-to-all-start = ((s32[64,1,2]{2,1,0:T(1,128)}), s32[64,1,2]{2,1,0:T(1,128)S(1)}, u32[]{:S(2)}, u32[]{:S(2)}) async-start(s32[64,1,2]{2,1,0:T(1,128)} %copy.107), calls=%async_computation | async-start | bytes 65536 | tf_op jit(solution)/shard_map/all_to_all | solution.py:123
  25.5 10.3 %all_gather.9 = bf16[32,2048]{1,0:T(8,128)(2,1)S(1)} all-gather(bf16[32,512]{1,0:T(8,128)(2,1)} %param.16), channel_id=1, replica_groups=mesh['tok'=64,'head'=4] {'head'}, dimensions={1}, use_global_device_ids=true | all-gather | bytes 163840 | tf_op jit(solution)/shard_map/all_gather | solution.py:79
  36.7 2.0 fusion.45
  40.2 1.2 fusion.16
  44.3 40.8 %all-reduce.7.cloned.1.call-done = f32[32,576]{1,0:T(8,128)} async-done(((f32[32,576]{1,0:T(8,128)}), f32[32,576]{1,0:T(8,128)}) %all-reduce.7.cloned.1.call-update) | async-done | bytes 73744 | tf_op jit(solution)/shard_map/psum | solution.py:86
  85.1 1.0 multiply_reduce_fusion.1
  86.0 0.9 multiply_cosine_fusion
  87.1 0.9 fusion.76
  88.3 1.5 gather_fusion.3
  89.8 13.0 %all-to-all-start.1 = ((bf16[64,5,576]{2,1,0:T(8,128)(2,1)}), bf16[64,5,576]{2,1,0:T(8,128)(2,1)}, u32[]{:S(2)}, u32[]{:S(2)}) async-start(bf16[64,5,576]{2,1,0:T(8,128)(2,1)} %gather_fusion.3), calls=%async_computation.1 | async-start | bytes 1310720 | tf_op jit(solution)/shard_map/all_to_all | solution.py:122
  104.0 2.5 copy.117
  107.1 15.7 %all-to-all-done.1 = bf16[64,5,576]{2,1,0:T(8,128)(2,1)} async-done(((bf16[64,5,576]{2,1,0:T(8,128)(2,1)}), bf16[64,5,576]{2,1,0:T(8,128)(2,1)}, u32[]{:S(2)}, u32[]{:S(2)}) %all-to-all-start.1) | async-done | bytes 368672 | tf_op jit(solution)/shard_map/all_to_all | solution.py:122
  122.8 1.8 gather_fusion.4
  125.4 11.3 %all_gather.10 = bf16[32,16,576]{2,0,1:T(8,128)(2,1)S(1)} all-gather(bf16[32,4,576]{2,0,1:T(8,128)(2,1)S(1)} %copy.113), channel_id=1, replica_groups=mesh['tok'=64,'head'=4] {'head'}, dimensions={1}, use_global_device_ids=true | all-gather | bytes 737280 | tf_op jit(solution)/shard_map/all_gather | solution.py:132
  136.9 6.9 %convert_reduce_fusion = (f32[512]{0:T(512)}, bf16[512,2496]{0,1:T(8,128)(2,1)}) fusion(pred[512,2496]{0,1:T(32,128)(4,1)S(1)} %copy-done.2, bf16[512,576]{1,0:T(8,128)(2,1)S(1)} %bitcast.106, bf16[2496,576]{0,1:T(8,128)(2,1)} %param.23), kind=kOutput, calls=%fused_computation.11 | convolution fusion | flops 1478589952 | bytes 7301120 | tf_op jit(solution)/shard_map/qc,pc->qp/dot_general | solution.py:39
  143.8 0.9 broadcast_in_dim.142
  144.7 4.4 %copy.115 = bf16[512,2496]{1,0:T(8,128)(2,1)} copy(bf16[512,2496]{0,1:T(8,128)(2,1)} %get-tuple-element.32) | data formatting | bytes 5111808 | tf_op jit(solution)/shard_map/exp | solution.py:46
  149.1 4.1 %fusion = f32[32,16,512]{2,1,0:T(8,128)S(1)} fusion(bf16[32,16,2496]{2,1,0:T(8,128)(2,1)} %bitcast.104, bf16[2496,576]{0,1:T(8,128)(2,1)} %param.23, pred[32,2496]{1,0:T(8,128)(4,1)S(1)} %compare_and_fusion), kind=kOutput, calls=%fused_computation.15 | convolution fusion | flops 1309900800 | bytes 6371328 | tf_op jit(solution)/shard_map/khp,pl->khl/dot_general | solution.py:47
  153.4 1.5 copy.119
  155.1 1.8 fusion.35
  157.8 21.0 %reduce-scatter.4.cloned.1.call-done = f32[32,4,513]{2,0,1:T(8,128)} async-done(((f32[32,16,513]{2,0,1:T(8,128)}), f32[32,4,513]{2,0,1:T(8,128)}) %reduce-scatter.4.cloned.1.call-update) | async-done | bytes 262672 | tf_op jit(solution)/shard_map/reduce_scatter | solution.py:136
  178.8 0.9 slice_reduce_fusion
  179.7 1.4 fusion.17
  183.7 13.0 %all-to-all-start.2 = ((bf16[64,2,256]{2,1,0:T(2,128)(2,1)}), bf16[64,2,256]{2,1,0:T(2,128)(2,1)S(1)}, u32[]{:S(2)}, u32[]{:S(2)}) async-start(bf16[64,2,256]{2,1,0:T(2,128)(2,1)} %reshape.501), calls=%async_computation.3 | async-start | bytes 131072 | tf_op jit(solution)/shard_map/all_to_all | solution.py:162
  197.0 1.6 gather_fusion.9
  198.7 7.7 %all-to-all-done.2 = bf16[64,2,256]{2,1,0:T(2,128)(2,1)S(1)} async-done(((bf16[64,2,256]{2,1,0:T(2,128)(2,1)}), bf16[64,2,256]{2,1,0:T(2,128)(2,1)S(1)}, u32[]{:S(2)}, u32[]{:S(2)}) %all-to-all-start.2) | async-done | bytes 65568 | tf_op jit(solution)/shard_map/all_to_all | solution.py:162
  207.2 2.8 fusion.62
  210.3 14.0 %reduce-scatter.6.cloned.1.call-done = f32[32,512]{1,0:T(8,128)} async-done(((f32[32,2048]{1,0:T(8,128)}), f32[32,512]{1,0:T(8,128)}) %reduce-scatter.6.cloned.1.call-update) | async-done | bytes 65552 | tf_op jit(solution)/shard_map/reduce_scatter | solution.py:165
  224.3 1.0 fusion.40
  225.4 11.8 %all-reduce.4 = (f32[32]{0:T(128)S(1)}, f32[32,64]{1,0:T(8,128)S(1)}) all-reduce(f32[32]{0:T(128)S(1)} %get-tuple-element.11, f32[32,64]{1,0:T(8,128)S(1)} %fusion.41), channel_id=1, replica_groups=mesh['tok'=64,'head'=4] {'head'}, use_global_device_ids=true, to_apply=%region_12.13 | all-reduce | flops 2080 | bytes 16640 | tf_op jit(solution)/shard_map/psum | solution.py:174
  237.3 9.1 %all_gather.11 = bf16[32,2048]{1,0:T(8,128)(2,1)S(1)} all-gather(bf16[32,512]{1,0:T(8,128)(2,1)S(1)} %fusion.39), channel_id=1, replica_groups=mesh['tok'=64,'head'=4] {'head'}, dimensions={1}, use_global_device_ids=true | all-gather | bytes 163840 | tf_op jit(solution)/shard_map/all_gather | solution.py:201
  246.4 3.1 gather_fusion.7
  249.6 3.7 reshape.405
  253.2 70.4 %all_to_all.39 = bf16[64,6,2048]{2,1,0:T(8,128)(2,1)} all-to-all(bf16[64,6,2048]{2,1,0:T(8,128)(2,1)} %reshape.405), channel_id=1, replica_groups=mesh['tok'=64,'head'=4] {'tok'}, dimensions={0} | all-to-all | bytes 3145728 | tf_op jit(solution)/shard_map/all_to_all | solution.py:205
  323.7 3.7 reshape.406
  327.4 3.6 fusion.8
  331.0 5.5 %convolution_convert_fusion = bf16[384,2048]{1,0:T(8,128)(2,1)} fusion(bf16[1,352,2048]{2,1,0:T(8,128)(2,1)} %param.31, bf16[384,2048]{1,0:T(8,128)(2,1)} %reshape.406, bf16[1,2048,352]{1,2,0:T(8,128)(2,1)} %param.30, f32[384,352]{0,1:T(8,128)} %fusion.8), kind=kOutput, calls=%fused_computation.14 | convolution fusion | flops 1108893696 | bytes 6569984 | tf_op jit(solution)/shard_map/dot_general | solution.py:217
  337.4 21.5 %reduce-scatter.8.cloned.1.call-done = bf16[384,512]{1,0:T(8,128)(2,1)} async-done(((bf16[384,2048]{1,0:T(8,128)(2,1)}), bf16[384,512]{1,0:T(8,128)(2,1)}) %reduce-scatter.8.cloned.1.call-update) | async-done | bytes 393232 | tf_op jit(solution)/shard_map/reduce_scatter | solution.py:216
  359.0 1.9 reshape.407
  360.9 11.7 %all-to-all-start.4 = ((bf16[64,6,512]{2,1,0:T(8,128)(2,1)}), bf16[64,6,512]{2,1,0:T(8,128)(2,1)}, u32[]{:S(2)}, u32[]{:S(2)}) async-start(bf16[64,6,512]{2,1,0:T(8,128)(2,1)} %reshape.407), calls=%async_computation.7 | async-start | bytes 1048576 | tf_op jit(solution)/shard_map/all_to_all | solution.py:222
  374.3 15.5 %all-to-all-done.4 = bf16[64,6,512]{2,1,0:T(8,128)(2,1)} async-done(((bf16[64,6,512]{2,1,0:T(8,128)(2,1)}), bf16[64,6,512]{2,1,0:T(8,128)(2,1)}, u32[]{:S(2)}, u32[]{:S(2)}) %all-to-all-start.4) | async-done | bytes 393248 | tf_op jit(solution)/shard_map/all_to_all | solution.py:222
  389.8 1.2 reshape.408
  390.9 1.7 gather_fusion.8
  392.6 1.8 reshape.488
  394.4 1.9 multiply_reduce_fusion
  (134 shorter events, 17.2 us)
Async XLA Ops:
  7.2 31.6 %copy-start = (bf16[2048,768]{1,0:T(8,128)(2,1)S(1)}, bf16[2048,768]{1,0:T(8,128)(2,1)}, u32[]{:S(2)}) copy-start(bf16[2048,768]{1,0:T(8,128)(2,1)} %param.18) | copy-start | bytes 9437188
  12.3 29.2 %all-to-all-start = ((s32[64,1,2]{2,1,0:T(1,128)}), s32[64,1,2]{2,1,0:T(1,128)S(1)}, u32[]{:S(2)}, u32[]{:S(2)}) async-start(s32[64,1,2]{2,1,0:T(1,128)} %copy.107), calls=%async_computation | async-start | bytes 65536 | tf_op jit(solution)/shard_map/all_to_all | solution.py:123
  25.5 59.6 %all-reduce.7.cloned.1.call-start = ((), (), s32[]{:S(2)}) async-start(), calls=%async_computation.8 | async-start | bytes 163840 | tf_op jit(solution)/shard_map/psum | solution.py:86
  38.7 2.7 copy-start.1
  43.7 44.4 %copy-start.18 = (s32[32]{0:T(128)}, s32[32]{0:T(128)S(1)}, u32[]{:S(2)}) copy-start(s32[32]{0:T(128)S(1)} %reduce.1) | copy-start | bytes 388
  86.0 2.1 copy-start.16
  87.0 1.0 copy-start.9
  87.0 1.0 copy-start.11
  89.8 33.0 %all-to-all-start.1 = ((bf16[64,5,576]{2,1,0:T(8,128)(2,1)}), bf16[64,5,576]{2,1,0:T(8,128)(2,1)}, u32[]{:S(2)}, u32[]{:S(2)}) async-start(bf16[64,5,576]{2,1,0:T(8,128)(2,1)} %gather_fusion.3), calls=%async_computation.1 | async-start | bytes 1310720 | tf_op jit(solution)/shard_map/all_to_all | solution.py:122
  102.7 76.0 %reduce-scatter.4.cloned.1.call-start = ((), (), s32[]{:S(2)}) async-start(), calls=%async_computation.9 | async-start | bytes 1638400 | tf_op jit(solution)/shard_map/reduce_scatter | solution.py:136
  104.0 2.5 copy-start.21
  124.6 19.2 %copy-start.3 = (bf16[32,5,576]{2,1,0:T(8,128)(2,1)}, bf16[32,5,576]{2,1,0:T(8,128)(2,1)S(1)}, u32[]{:S(2)}) copy-start(bf16[32,5,576]{2,1,0:T(8,128)(2,1)S(1)} %gather_fusion.4) | copy-start | bytes 552964
  124.6 12.3 %copy-start.2 = (pred[512,2496]{0,1:T(32,128)(4,1)S(1)}, pred[512,2496]{0,1:T(32,128)(4,1)}, u32[]{:S(2)}) copy-start(pred[512,2496]{0,1:T(32,128)(4,1)} %copy.117) | copy-start | bytes 3833860
  124.7 0.7 copy-start.5
  153.4 1.5 copy-start.14
  153.4 1.6 copy-start.19
  153.4 1.6 copy-start.4
  183.7 22.8 %all-to-all-start.2 = ((bf16[64,2,256]{2,1,0:T(2,128)(2,1)}), bf16[64,2,256]{2,1,0:T(2,128)(2,1)S(1)}, u32[]{:S(2)}, u32[]{:S(2)}) async-start(bf16[64,2,256]{2,1,0:T(2,128)(2,1)} %reshape.501), calls=%async_computation.3 | async-start | bytes 131072 | tf_op jit(solution)/shard_map/all_to_all | solution.py:162
  196.7 27.7 %reduce-scatter.6.cloned.1.call-start = ((), (), s32[]{:S(2)}) async-start(), calls=%async_computation.10 | async-start | bytes 327680 | tf_op jit(solution)/shard_map/reduce_scatter | solution.py:165
  197.0 1.7 copy-start.20
  206.5 17.8 %copy-start.8 = (bf16[32,512]{1,0:T(8,128)(2,1)S(1)}, bf16[32,512]{1,0:T(8,128)(2,1)}, u32[]{:S(2)}) copy-start(bf16[32,512]{1,0:T(8,128)(2,1)} %param.16) | copy-start | bytes 98308
  206.5 18.8 %copy-start.13 = (bf16[512,64]{0,1:T(8,128)(2,1)S(1)}, bf16[512,64]{0,1:T(8,128)(2,1)}, u32[]{:S(2)}) copy-start(bf16[512,64]{0,1:T(8,128)(2,1)} %param.27) | copy-start | bytes 196612
  206.5 18.8 %copy-start.15 = (f32[512]{0:T(512)S(1)}, f32[512]{0:T(512)}, u32[]{:S(2)}) copy-start(f32[512]{0:T(512)} %param.26) | copy-start | bytes 6148
  210.0 149.0 %reduce-scatter.8.cloned.1.call-start = ((), (), s32[]{:S(2)}) async-start(), calls=%async_computation.11 | async-start | bytes 1966080 | tf_op jit(solution)/shard_map/reduce_scatter | solution.py:216
  225.3 12.1 %copy-start.7 = (bf16[32,512]{1,0:T(8,128)(2,1)}, bf16[32,512]{1,0:T(8,128)(2,1)S(1)}, u32[]{:S(2)}) copy-start(bf16[32,512]{1,0:T(8,128)(2,1)S(1)} %get-tuple-element.12) | copy-start | bytes 98308
  336.5 0.9 copy-start.6
  336.5 0.9 copy-start.17
  336.5 36.1 %copy-start.10 = (bf16[32,32]{1,0:T(8,128)(2,1)S(1)}, bf16[32,32]{1,0:T(8,128)(2,1)}, u32[]{:S(2)}) copy-start(bf16[32,32]{1,0:T(8,128)(2,1)} %copy-done.9) | copy-start | bytes 6148
  336.5 36.1 %copy-start.12 = (bf16[32,32]{1,0:T(8,128)(2,1)S(1)}, bf16[32,32]{1,0:T(8,128)(2,1)}, u32[]{:S(2)}) copy-start(bf16[32,32]{1,0:T(8,128)(2,1)} %copy-done.11) | copy-start | bytes 6148
  360.9 28.9 %all-to-all-start.4 = ((bf16[64,6,512]{2,1,0:T(8,128)(2,1)}), bf16[64,6,512]{2,1,0:T(8,128)(2,1)}, u32[]{:S(2)}, u32[]{:S(2)}) async-start(bf16[64,6,512]{2,1,0:T(8,128)(2,1)} %reshape.407), calls=%async_computation.7 | async-start | bytes 1048576 | tf_op jit(solution)/shard_map/all_to_all | solution.py:222
Sparse Core Ops, SparseCore 0:
  38.9 46.1 all-reduce.6
  155.0 23.7 reduce-scatter.3
  210.1 14.1 reduce-scatter.5
  336.6 22.2 reduce-scatter.7

commit v2 on v1

--- a/solution.py
+++ b/solution.py
@@ -76,16 +76,39 @@
     head_index = lax.axis_index("head")
     tok_index = lax.axis_index("tok")
     row_ids = jnp.arange(local_rows, dtype=jnp.int32)
-    gathered = lax.all_gather(hidden, "head", axis=1, tiled=True)
+    latent_width = w_latent.shape[1]
+    gain_part = lax.dynamic_slice_in_dim(attn_gain, head_index * quarter_width, quarter_width, 0)
+    raw_part = jnp.dot(
+        (hidden.astype(jnp.float32) * gain_part).astype(jnp.bfloat16),
+        w_latent,
+        preferred_element_type=jnp.float32,
+    )
+    part_hi = lax.reduce_precision(raw_part, exponent_bits=8, mantissa_bits=7)
+    rest = raw_part - part_hi
+    part_mid = lax.reduce_precision(rest, exponent_bits=8, mantissa_bits=7)
+    part_lo = rest - part_mid
+    send_rows = jnp.concatenate(
+        [
+            hidden,
+            part_hi.astype(jnp.bfloat16),
+            part_mid.astype(jnp.bfloat16),
+            part_lo.astype(jnp.bfloat16),
+        ],
+        axis=1,
+    )
+    piece_width = send_rows.shape[1]
+    got_rows = lax.all_gather(send_rows, "head", axis=1, tiled=True).reshape(
+        local_rows, -1, piece_width
+    )
+    gathered = got_rows[:, :, :quarter_width].reshape(local_rows, -1)
+    got_parts = got_rows[:, :, quarter_width:].reshape(local_rows, -1, 3, latent_width).astype(
+        jnp.float32
+    )
+    part_sums = (got_parts[:, :, 0] + got_parts[:, :, 1]) + got_parts[:, :, 2]
     widened = gathered.astype(jnp.float32)
     inv_attn = lax.rsqrt(jnp.mean(widened * widened, axis=1, keepdims=True) + NORM_EPS)
     normed_attn = (widened * inv_attn * attn_gain).astype(jnp.bfloat16)
-    normed_part = lax.dynamic_slice_in_dim(
-        normed_attn, head_index * quarter_width, quarter_width, 1
-    )
-    compressed = lax.psum(
-        jnp.dot(normed_part, w_latent, preferred_element_type=jnp.float32), "head"
-    )
+    compressed = jnp.sum(part_sums, axis=1) * inv_attn
     latent_new = compressed[:, :LATENT]
     latent_new = latent_new * lax.rsqrt(
         jnp.mean(latent_new * latent_new, axis=1, keepdims=True) + NORM_EPS
@@ -103,32 +126,32 @@
     )
     probes = jnp.concatenate([absorbed, turned], axis=2)
     factor = (NOPE + ROPE) ** (-0.5)
+    self_score = factor * jnp.einsum(
+        "bhc,bc->bh", probes, new_entry, preferred_element_type=jnp.float32
+    )
+    self_weight = jnp.exp(self_score).astype(jnp.bfloat16).astype(jnp.float32)
     owner_ids = jnp.arange(peer_count, dtype=jnp.int32)
     dest_owner = request_slot // local_rows
     goes_to = dest_owner[None, :] == owner_ids[:, None]
     sent_any = jnp.max(goes_to.astype(jnp.int32), axis=1)
-    sent_row = jnp.sum(jnp.where(goes_to, row_ids[None, :], 0), axis=1) + local_rows * (1 - sent_any)
-    packed = jnp.concatenate([probes, new_entry[:, None, :]], axis=1)
-    packed = jnp.concatenate(
-        [packed, jnp.zeros((1,) + packed.shape[1:], jnp.bfloat16)], axis=0
-    )
-    send_ints = jnp.stack(
-        [
-            jnp.where(sent_any > 0, request_slot[jnp.minimum(sent_row, local_rows - 1)], -1),
-            cache_lengths[jnp.minimum(sent_row, local_rows - 1)],
-        ],
-        axis=1,
-    )
-    got_packed = lax.all_to_all(packed[sent_row], "tok", 0, 0, tiled=True)
-    got_ints = lax.all_to_all(send_ints, "tok", 0, 0, tiled=True)
-    got_slot = got_ints[:, 0]
+    sent_row = jnp.sum(jnp.where(goes_to, row_ids[None, :], 0), axis=1)
+    sent_slot = request_slot[sent_row]
+    sent_len = cache_lengths[sent_row]
+    code = jnp.stack(
+        [sent_any, sent_slot // 64, sent_slot % 64, sent_len // 64, sent_len % 64], axis=1
+    ) * sent_any[:, None]
+    code_row = jnp.zeros((peer_count, probes.shape[2]), jnp.float32)
+    code_row = code_row.at[:, :5].set(code.astype(jnp.float32)).astype(jnp.bfloat16)
+    packed = jnp.concatenate([probes[sent_row], code_row[:, None, :]], axis=1)
+    got_packed = lax.all_to_all(packed, "tok", 0, 0, tiled=True)
+    got_code = got_packed[:, local_heads, :5].astype(jnp.float32).astype(jnp.int32)
+    got_slot = jnp.where(got_code[:, 0] > 0, got_code[:, 1] * 64 + got_code[:, 2], -1)
+    got_len = got_code[:, 3] * 64 + got_code[:, 4]
     local_slot = got_slot - tok_index * local_rows
     slot_sel = local_slot[None, :] == row_ids[:, None]
     src_of_slot = jnp.sum(jnp.where(slot_sel, owner_ids[None, :], 0), axis=1)
-    owner_packed = got_packed[src_of_slot]
-    owner_probes = owner_packed[:, :local_heads]
-    owner_new = owner_packed[:, local_heads]
-    owner_lengths = got_ints[src_of_slot, 1]
+    owner_probes = got_packed[src_of_slot, :local_heads]
+    owner_lengths = got_len[src_of_slot]
     all_heads = lax.all_gather(owner_probes, "head", axis=1, tiled=True)
     numerator, denominator = owner_attend(
         all_heads, owner_lengths, latent_cache, head_index, factor
@@ -139,28 +162,18 @@
         scatter_dimension=1,
         tiled=True,
     )
-    group_num = joined[:, :, :LATENT]
-    group_den = joined[:, :, LATENT]
-    self_score = factor * jnp.einsum(
-        "bhc,bc->bh", owner_probes, owner_new, preferred_element_type=jnp.float32
-    )
-    self_weight = jnp.exp(self_score).astype(jnp.bfloat16).astype(jnp.float32)
-    total_num = group_num + self_weight[:, :, None] * owner_new[:, None, :LATENT].astype(
+    joined = jnp.concatenate([joined, jnp.zeros((1,) + joined.shape[1:], jnp.float32)], axis=0)
+    back_valid = (local_slot >= 0) & (local_slot < local_rows)
+    back_row = jnp.where(back_valid, local_slot, local_rows)
+    returned = lax.all_to_all(joined[back_row], "tok", 0, 0, tiled=True)[dest_owner]
+    total_num = returned[:, :, :LATENT] + self_weight[:, :, None] * new_entry[:, None, :LATENT].astype(
         jnp.float32
     )
-    total_den = group_den + self_weight
+    total_den = returned[:, :, LATENT] + self_weight
     mixed_latent = (total_num / total_den[:, :, None]).astype(jnp.bfloat16)
-    owner_out = jnp.einsum(
+    head_out = jnp.einsum(
         "bhl,hld->bhd", mixed_latent, w_value_up, preferred_element_type=jnp.float32
     ).astype(jnp.bfloat16)
-    owner_out = owner_out.reshape(local_rows, local_heads * NOPE)
-    owner_out = jnp.concatenate(
-        [owner_out, jnp.zeros((1, local_heads * NOPE), jnp.bfloat16)], axis=0
-    )
-    back_valid = (local_slot >= 0) & (local_slot < local_rows)
-    back_row = jnp.where(back_valid, local_slot, local_rows)
-    returned_out = lax.all_to_all(owner_out[back_row], "tok", 0, 0, tiled=True)
-    head_out = returned_out[dest_owner]
     head_out = head_out.reshape(local_rows, local_heads * NOPE)
     attn_piece = lax.psum_scatter(
         jnp.dot(head_out, w_out, preferred_element_type=jnp.float32),
@@ -198,18 +211,19 @@
     source_token = jnp.sum(
         jnp.where(filled, row_ids[None, :, None], 0), axis=(1, 2)
     ) + local_rows * (1 - jnp.max(filled.astype(jnp.int32), axis=(1, 2)))
-    full_rows = lax.all_gather(normed_ffn, "head", axis=1, tiled=True)
     padded_rows = jnp.concatenate(
-        [full_rows, jnp.zeros((1, full_rows.shape[1]), jnp.bfloat16)], axis=0
+        [normed_ffn, jnp.zeros((1, normed_ffn.shape[1]), jnp.bfloat16)], axis=0
     )
     arrived = lax.all_to_all(
-        padded_rows[source_token].reshape(expert_count, capacity, full_rows.shape[1]),
+        padded_rows[source_token].reshape(expert_count, capacity, quarter_width),
         "tok",
         split_axis=0,
         concat_axis=0,
         tiled=True,
     )
-    expert_in = arrived.reshape(peer_count * capacity, full_rows.shape[1])
+    expert_in = lax.all_gather(
+        arrived.reshape(peer_count * capacity, quarter_width), "head", axis=1, tiled=True
+    )
     gate_value = jnp.dot(expert_in, expert_gate[0], preferred_element_type=jnp.float32)
     up_value = jnp.dot(expert_in, expert_up[0], preferred_element_type=jnp.float32)
     activity = (jax.nn.silu(gate_value) * up_value).astype(jnp.bfloat16)

time: 404 us -> 374 us (0.926)
  blocking collectives: 113 us -> 70 us
  local copies, waits for them, and re-layouts: 43.6 us -> 57.8 us
  starting transfers between devices: 50.9 us -> 39.3 us
  other arithmetic: 14.6 us -> 22.4 us
  waiting for transfers between devices: 136 us -> 142 us
    psum x1 -> x0, waiting for transfers between devices: 40.8 us -> none  [body(): lax.psum(jnp.dot(normed_part, w_latent, preferred_element_type=jnp.float3...]
    all_to_all x1, blocking collectives: 70.4 us -> 33.6 us  [body(): lax.all_to_all(padded_rows[source_token].reshape(expert_count, capacity,...]
    all_gather x0 -> x1, waiting for transfers between devices: none -> 24.3 us  [body(): lax.all_gather(arrived.reshape(peer_count * capacity, quarter_width), 'he...]
    all_to_all x3 -> x2, waiting for transfers between devices: 23.4 us -> 35.2 us  [the longest x1 20 us: body(): got_packed = lax.all_to_all(packed, 'tok', 0, 0, tiled=True)]
    all_to_all x3 -> x2, starting transfers between devices: 39.1 us -> 27.5 us  [the longest x1 14.2 us: body(): got_packed = lax.all_to_all(packed, 'tok', 0, 0, tiled=True)]
    all_gather x2 -> x1, blocking collectives: 19.4 us -> 12.4 us  [body(): lax.all_gather(send_rows, 'head', axis=1, tiled=True)]
    convert_element_type x2 -> x5, other arithmetic: 0.81 us -> 6.47 us  [the longest x1 2.05 us: body(): got_rows[:, :, quarter_width:].reshape(local_rows, -1, 3, latent_width)]
    reduce_scatter x1, waiting for transfers between devices: 21.5 us -> 26.9 us  [body(): lax.psum_scatter(jnp.dot(activity, expert_down[0], preferred_element_type...]
  transfers between devices with their start and end apart: 8 -> 7, of which waited for: 7 -> 7; matrix products, arithmetic and copies ran while one was open for 5% -> 2% of each run, Pallas kernels for 0% -> 0%
where the time goes in v2:
time: 374 us; the launch traced here: 373 us
  waiting for transfers between devices  142 us (38%)
  blocking collectives  70 us (19%)
  local copies, waits for them, and re-layouts  57.8 us (15%)
  starting transfers between devices  39.3 us (11%)
  matrix products  26.5 us (7%)
  other arithmetic  22.4 us (6%)
  between operations  14.3 us (4%)
    all_to_all x1, blocking collectives, body(): lax.all_to_all(padded_rows[source_token].reshape(expert_count, capacity,...  33.6 us
    reduce_scatter x1, waiting for transfers between devices, body(): lax.psum_scatter(jnp.dot(activity, expert_down[0], preferred_element_type...  26.9 us
    all_gather x1, waiting for transfers between devices, body(): lax.all_gather(arrived.reshape(peer_count * capacity, quarter_width), 'he...  24.3 us
    reduce_scatter x1, waiting for transfers between devices, body(): lax.psum_scatter(jnp.concatenate([numerator, denominator[:, :, None]], ax...  23.5 us
    all_to_all x1, waiting for transfers between devices, body(): got_packed = lax.all_to_all(packed, 'tok', 0, 0, tiled=True)  20 us
    all_to_all x1, waiting for transfers between devices, body(): lax.all_to_all(expert_share.reshape(peer_count, capacity, quarter_width),...  16.2 us
    reduce_scatter x1, waiting for transfers between devices, body(): lax.psum_scatter(jnp.dot(head_out, w_out, preferred_element_type=jnp.floa...  16.2 us
    all_to_all x1, waiting for transfers between devices, body(): lax.all_to_all(joined[back_row], 'tok', 0, 0, tiled=True)[dest_owner]  15.3 us
  transfers between devices with their start and end apart: 7, of which 7 were waited for; matrix products, arithmetic and copies ran while one was open for 2% of the time, Pallas kernels for 0%

profile of v2, /device:TPU:1, one launch (start us, length us, event | category | flops | bytes accessed | tf_op | source)
XLA Modules:
  0.0 372.7 jit_solution(18207986420326165914)
XLA Ops:
  8.1 1.4 fusion.32
  10.4 12.4 %all-gather = bf16[4,2240,32]{1,2,0:T(8,128)(2,1)S(1)} all-gather(bf16[1,2240,32]{1,2,0:T(8,128)(2,1)S(1)} %bitcast.94), channel_id=1, replica_groups=mesh['tok'=64,'head'=4] {'head'}, dimensions={0}, use_global_device_ids=true | all-gather | bytes 716800 | tf_op jit(solution)/shard_map/all_gather | solution.py:100
  22.8 1.3 copy.239
  24.0 2.4 reshape.600
  26.4 2.6 reshape.501
  30.2 2.0 slice.127
  36.7 2.1 copy_convert_fusion
  38.7 2.5 reshape.512
  41.2 3.2 fusion.25
  46.3 1.6 gather_fusion
  49.8 1.8 copy.260
  51.5 2.2 pad_maximum_fusion.1
  53.7 14.2 %all-to-all-start = ((bf16[64,5,576]{2,1,0:T(8,128)(2,1)}), bf16[64,5,576]{2,1,0:T(8,128)(2,1)}, u32[]{:S(2)}, u32[]{:S(2)}) async-start(bf16[64,5,576]{2,1,0:T(8,128)(2,1)} %pad_maximum_fusion.1), calls=%async_computation | async-start | bytes 1310720 | tf_op jit(solution)/shard_map/all_to_all | solution.py:146
  68.0 20.0 %all-to-all-done = bf16[64,5,576]{2,1,0:T(8,128)(2,1)} async-done(((bf16[64,5,576]{2,1,0:T(8,128)(2,1)}), bf16[64,5,576]{2,1,0:T(8,128)(2,1)}, u32[]{:S(2)}, u32[]{:S(2)}) %all-to-all-start) | async-done | bytes 368672 | tf_op jit(solution)/shard_map/all_to_all | solution.py:146
  89.3 1.9 copy.262
  91.2 2.1 gather_fusion.4
  93.3 12.1 %all_gather.10 = bf16[32,16,576]{2,0,1:T(8,128)(2,1)S(1)} all-gather(bf16[32,4,576]{2,0,1:T(8,128)(2,1)S(1)} %gather_fusion.4), channel_id=1, replica_groups=mesh['tok'=64,'head'=4] {'head'}, dimensions={1}, use_global_device_ids=true | all-gather | bytes 737280 | tf_op jit(solution)/shard_map/all_gather | solution.py:155
  108.0 1.4 copy.266
  109.6 4.5 %convert_reduce_fusion = (f32[512]{0:T(512)S(1)}, bf16[512,2496]{0,1:T(8,128)(2,1)}) fusion(pred[512,2496]{0,1:T(32,128)(4,1)S(1)} %copy.266, bf16[512,576]{1,0:T(8,128)(2,1)S(1)} %bitcast.93, bf16[2496,576]{0,1:T(8,128)(2,1)S(1)} %copy-done.15), kind=kOutput, calls=%fused_computation.11 | convolution fusion | flops 1478589952 | bytes 7301120 | tf_op jit(solution)/shard_map/qc,pc->qp/dot_general | solution.py:39
  114.2 4.4 %copy.264 = bf16[512,2496]{1,0:T(8,128)(2,1)} copy(bf16[512,2496]{0,1:T(8,128)(2,1)} %get-tuple-element.53) | data formatting | bytes 5111808 | tf_op jit(solution)/shard_map/exp | solution.py:46
  118.5 5.1 %fusion = f32[32,16,512]{2,1,0:T(8,128)} fusion(bf16[32,16,2496]{2,1,0:T(8,128)(2,1)} %bitcast.88, bf16[2496,576]{0,1:T(8,128)(2,1)} %param.25, pred[32,2496]{1,0:T(8,128)(4,1)S(1)} %compare_and_fusion), kind=kOutput, calls=%fused_computation.15 | convolution fusion | flops 1309900800 | bytes 6371328 | tf_op jit(solution)/shard_map/khp,pl->khl/dot_general | solution.py:47
  123.8 1.3 pad_maximum_fusion
  125.2 1.5 copy.268
  126.8 23.5 %reduce-scatter.4.cloned.1.call-done = f32[32,4,513]{2,0,1:T(8,128)} async-done(((f32[32,16,513]{2,0,1:T(8,128)}), f32[32,4,513]{2,0,1:T(8,128)}) %reduce-scatter.4.cloned.1.call-update) | async-done | bytes 262672 | tf_op jit(solution)/shard_map/reduce_scatter | solution.py:159
  151.6 1.8 gather_fusion.5
  153.4 13.3 %all-to-all-start.1 = ((f32[64,4,513]{2,1,0:T(4,128)}), f32[64,4,513]{2,1,0:T(4,128)}, u32[]{:S(2)}, u32[]{:S(2)}) async-start(f32[64,4,513]{2,1,0:T(4,128)} %gather_fusion.5), calls=%async_computation.2 | async-start | bytes 1310720 | tf_op jit(solution)/shard_map/all_to_all | solution.py:168
  166.7 1.5 fusion.69
  169.1 1.6 gather_fusion.9
  171.4 15.3 %all-to-all-done.1 = f32[64,4,513]{2,1,0:T(4,128)} async-done(((f32[64,4,513]{2,1,0:T(4,128)}), f32[64,4,513]{2,1,0:T(4,128)}, u32[]{:S(2)}, u32[]{:S(2)}) %all-to-all-start.1) | async-done | bytes 525344 | tf_op jit(solution)/shard_map/all_to_all | solution.py:168
  186.7 1.8 gather_fusion.6
  191.5 1.4 copy.272
  195.2 2.8 fusion.47
  198.3 16.2 %reduce-scatter.6.cloned.1.call-done = f32[32,512]{1,0:T(8,128)} async-done(((f32[32,2048]{1,0:T(8,128)}), f32[32,512]{1,0:T(8,128)}) %reduce-scatter.6.cloned.1.call-update) | async-done | bytes 65552 | tf_op jit(solution)/shard_map/reduce_scatter | solution.py:178
  215.7 11.9 %all-reduce.4 = (f32[32]{0:T(128)S(1)}, f32[32,64]{1,0:T(8,128)S(1)}) all-reduce(f32[32]{0:T(128)S(1)} %get-tuple-element.25, f32[32,64]{1,0:T(8,128)S(1)} %fusion.43), channel_id=1, replica_groups=mesh['tok'=64,'head'=4] {'head'}, use_global_device_ids=true, to_apply=%region_13.14 | all-reduce | flops 2080 | bytes 16640 | tf_op jit(solution)/shard_map/psum | solution.py:187
  227.6 2.6 gather_fusion.7
  230.2 1.9 reshape.508
  232.1 33.6 %all_to_all.20 = bf16[64,6,512]{2,1,0:T(8,128)(2,1)} all-to-all(bf16[64,6,512]{2,1,0:T(8,128)(2,1)} %reshape.508), channel_id=1, replica_groups=mesh['tok'=64,'head'=4] {'tok'}, dimensions={0} | all-to-all | bytes 786432 | tf_op jit(solution)/shard_map/all_to_all | solution.py:217
  265.8 1.9 reshape.509
  267.8 24.3 %all-gather.3.cloned.1.call-done = bf16[384,2048]{1,0:T(8,128)(2,1)} async-done(((bf16[384,512]{1,0:T(8,128)(2,1)}), bf16[384,2048]{1,0:T(8,128)(2,1)}) %all-gather.3.cloned.1.call-update) | async-done | bytes 1572880 | tf_op jit(solution)/shard_map/all_gather | solution.py:224
  292.0 3.6 fusion.8
  295.6 5.5 %convolution_convert_fusion = bf16[384,2048]{1,0:T(8,128)(2,1)} fusion(bf16[1,352,2048]{2,1,0:T(8,128)(2,1)} %param.33, bf16[384,2048]{1,0:T(8,128)(2,1)} %all-gather.3.cloned.1.call-done, bf16[1,2048,352]{1,2,0:T(8,128)(2,1)} %param.32, f32[384,352]{0,1:T(8,128)} %fusion.8), kind=kOutput, calls=%fused_computation.14 | convolution fusion | flops 1108893696 | bytes 6569984 | tf_op jit(solution)/shard_map/dot_general | solution.py:231
  301.9 26.9 %reduce-scatter.8.cloned.1.call-done = bf16[384,512]{1,0:T(8,128)(2,1)} async-done(((bf16[384,2048]{1,0:T(8,128)(2,1)}), bf16[384,512]{1,0:T(8,128)(2,1)}) %reduce-scatter.8.cloned.1.call-update) | async-done | bytes 393232 | tf_op jit(solution)/shard_map/reduce_scatter | solution.py:230
  328.9 1.9 reshape.510
  330.8 11.7 %all-to-all-start.3 = ((bf16[64,6,512]{2,1,0:T(8,128)(2,1)}), bf16[64,6,512]{2,1,0:T(8,128)(2,1)}, u32[]{:S(2)}, u32[]{:S(2)}) async-start(bf16[64,6,512]{2,1,0:T(8,128)(2,1)} %reshape.510), calls=%async_computation.6 | async-start | bytes 1048576 | tf_op jit(solution)/shard_map/all_to_all | solution.py:236
  343.4 16.2 %all-to-all-done.3 = bf16[64,6,512]{2,1,0:T(8,128)(2,1)} async-done(((bf16[64,6,512]{2,1,0:T(8,128)(2,1)}), bf16[64,6,512]{2,1,0:T(8,128)(2,1)}, u32[]{:S(2)}, u32[]{:S(2)}) %all-to-all-start.3) | async-done | bytes 393248 | tf_op jit(solution)/shard_map/all_to_all | solution.py:236
  360.8 1.7 gather_fusion.8
  362.5 1.8 reshape.593
  364.3 1.9 multiply_reduce_fusion
  (136 shorter events, 28.2 us)
Async XLA Ops:
  7.2 26.0 %copy-start = (bf16[2048,768]{1,0:T(8,128)(2,1)S(1)}, bf16[2048,768]{1,0:T(8,128)(2,1)}, u32[]{:S(2)}) copy-start(bf16[2048,768]{1,0:T(8,128)(2,1)} %param.20) | copy-start | bytes 9437188
  26.4 6.8 %copy-start.13 = (f32[2048]{0:T(1024)S(1)}, f32[2048]{0:T(1024)}, u32[]{:S(2)}) copy-start(f32[2048]{0:T(1024)} %param.19) | copy-start | bytes 24580
  33.2 0.9 copy-start.2
  33.2 0.9 copy-start.1
  44.5 82.1 %copy-start.5 = (f32[32,576]{1,0:T(8,128)}, f32[32,576]{1,0:T(8,128)S(1)}, u32[]{:S(2)}) copy-start(f32[32,576]{1,0:T(8,128)S(1)} %broadcast_multiply_fusion) | copy-start | bytes 221188
  46.2 7.5 %copy-start.3 = (bf16[32,4,576]{2,1,0:T(4,128)(2,1)}, bf16[32,4,576]{2,1,0:T(4,128)(2,1)S(1)}, u32[]{:S(2)}) copy-start(bf16[32,4,576]{2,1,0:T(4,128)(2,1)S(1)} %copy.246) | copy-start | bytes 442372
  53.7 34.2 %all-to-all-start = ((bf16[64,5,576]{2,1,0:T(8,128)(2,1)}), bf16[64,5,576]{2,1,0:T(8,128)(2,1)}, u32[]{:S(2)}, u32[]{:S(2)}) async-start(bf16[64,5,576]{2,1,0:T(8,128)(2,1)} %pad_maximum_fusion.1), calls=%async_computation | async-start | bytes 1310720 | tf_op jit(solution)/shard_map/all_to_all | solution.py:146
  67.9 82.4 %reduce-scatter.4.cloned.1.call-start = ((), (), s32[]{:S(2)}) async-start(), calls=%async_computation.7 | async-start | bytes 1638400 | tf_op jit(solution)/shard_map/reduce_scatter | solution.py:159
  107.6 1.8 copy-start.15
  108.0 1.7 copy-start.6
  151.6 17.1 %copy-start.11 = (s32[32,6]{0,1:T(8,128)S(1)}, s32[32,6]{0,1:T(8,128)}, u32[]{:S(2)}) copy-start(s32[32,6]{0,1:T(8,128)} %param.30) | copy-start | bytes 2308
  153.4 15.0 %copy-start.4 = (bf16[32,4,576]{2,1,0:T(4,128)(2,1)S(1)}, bf16[32,4,576]{2,1,0:T(4,128)(2,1)}, u32[]{:S(2)}) copy-start(bf16[32,4,576]{2,1,0:T(4,128)(2,1)} %copy-done.3) | copy-start | bytes 442372
  153.4 33.4 %all-to-all-start.1 = ((f32[64,4,513]{2,1,0:T(4,128)}), f32[64,4,513]{2,1,0:T(4,128)}, u32[]{:S(2)}, u32[]{:S(2)}) async-start(f32[64,4,513]{2,1,0:T(4,128)} %gather_fusion.5), calls=%async_computation.2 | async-start | bytes 1310720 | tf_op jit(solution)/shard_map/all_to_all | solution.py:168
  166.7 47.9 %reduce-scatter.6.cloned.1.call-start = ((), (), s32[]{:S(2)}) async-start(), calls=%async_computation.8 | async-start | bytes 327680 | tf_op jit(solution)/shard_map/reduce_scatter | solution.py:178
  193.9 4.2 %copy-start.10 = (s32[32,6]{1,0:T(8,128)S(1)}, s32[32,6]{1,0:T(8,128)}, u32[]{:S(2)}) copy-start(s32[32,6]{1,0:T(8,128)} %reshape.587) | copy-start | bytes 2308
  193.9 20.7 %copy-start.7 = (bf16[32,512]{1,0:T(8,128)(2,1)S(1)}, bf16[32,512]{1,0:T(8,128)(2,1)}, u32[]{:S(2)}) copy-start(bf16[32,512]{1,0:T(8,128)(2,1)} %param.18) | copy-start | bytes 98308
  195.2 20.4 %copy-start.9 = (bf16[512,64]{0,1:T(8,128)(2,1)S(1)}, bf16[512,64]{0,1:T(8,128)(2,1)}, u32[]{:S(2)}) copy-start(bf16[512,64]{0,1:T(8,128)(2,1)} %param.29) | copy-start | bytes 196612
  195.2 20.4 %copy-start.14 = (f32[512]{0:T(512)S(1)}, f32[512]{0:T(512)}, u32[]{:S(2)}) copy-start(f32[512]{0:T(512)} %param.28) | copy-start | bytes 6148
  198.0 94.1 %all-gather.3.cloned.1.call-start = ((), (), s32[]{:S(2)}) async-start(), calls=%async_computation.9 | async-start | bytes 1966080 | tf_op jit(solution)/shard_map/all_gather | solution.py:224
  215.5 12.0 %copy-start.8 = (bf16[32,512]{1,0:T(8,128)(2,1)}, bf16[32,512]{1,0:T(8,128)(2,1)S(1)}, u32[]{:S(2)}) copy-start(bf16[32,512]{1,0:T(8,128)(2,1)S(1)} %get-tuple-element.26) | copy-start | bytes 98308
  267.7 61.1 %reduce-scatter.8.cloned.1.call-start = ((), (), s32[]{:S(2)}) async-start(), calls=%async_computation.10 | async-start | bytes 1966080 | tf_op jit(solution)/shard_map/reduce_scatter | solution.py:230
  301.1 41.4 %copy-start.12 = (s32[32,6]{0,1:T(8,128)S(1)}, s32[32,6]{0,1:T(8,128)}, u32[]{:S(2)}) copy-start(s32[32,6]{0,1:T(8,128)} %param.30) | copy-start | bytes 2308
  330.8 28.9 %all-to-all-start.3 = ((bf16[64,6,512]{2,1,0:T(8,128)(2,1)}), bf16[64,6,512]{2,1,0:T(8,128)(2,1)}, u32[]{:S(2)}, u32[]{:S(2)}) async-start(bf16[64,6,512]{2,1,0:T(8,128)(2,1)} %reshape.510), calls=%async_computation.6 | async-start | bytes 1048576 | tf_op jit(solution)/shard_map/all_to_all | solution.py:236
Sparse Core Ops, SparseCore 0:
  126.8 23.4 reduce-scatter.3
  198.1 16.3 reduce-scatter.5
  267.8 24.1 all-gather.2
  301.3 27.5 reduce-scatter.7

commit v3 on v2

--- a/solution.py
+++ b/solution.py
@@ -49,6 +49,13 @@
     )
     denominator = jnp.sum(weights.astype(jnp.float32), axis=2)
     return (numerator, denominator)
+
+
+def head_sum_scatter(values, axis):
+    groups = lax.axis_size("head")
+    moved = lax.all_to_all(values, "head", split_axis=axis, concat_axis=0, tiled=True)
+    moved = moved.reshape((groups, values.shape[0]) + moved.shape[1:])
+    return jnp.sum(moved.astype(jnp.float32), axis=0)
 
 
 def body(
@@ -156,12 +163,7 @@
     numerator, denominator = owner_attend(
         all_heads, owner_lengths, latent_cache, head_index, factor
     )
-    joined = lax.psum_scatter(
-        jnp.concatenate([numerator, denominator[:, :, None]], axis=2),
-        "head",
-        scatter_dimension=1,
-        tiled=True,
-    )
+    joined = head_sum_scatter(jnp.concatenate([numerator, denominator[:, :, None]], axis=2), 1)
     joined = jnp.concatenate([joined, jnp.zeros((1,) + joined.shape[1:], jnp.float32)], axis=0)
     back_valid = (local_slot >= 0) & (local_slot < local_rows)
     back_row = jnp.where(back_valid, local_slot, local_rows)
@@ -175,12 +177,7 @@
         "bhl,hld->bhd", mixed_latent, w_value_up, preferred_element_type=jnp.float32
     ).astype(jnp.bfloat16)
     head_out = head_out.reshape(local_rows, local_heads * NOPE)
-    attn_piece = lax.psum_scatter(
-        jnp.dot(head_out, w_out, preferred_element_type=jnp.float32),
-        "head",
-        scatter_dimension=1,
-        tiled=True,
-    )
+    attn_piece = head_sum_scatter(jnp.dot(head_out, w_out, preferred_element_type=jnp.float32), 1)
     attended = (hidden.astype(jnp.float32) + attn_piece).astype(jnp.bfloat16)
     attended_wide = attended.astype(jnp.float32)
     gained = (attended_wide * ffn_gain).astype(jnp.bfloat16)
@@ -221,18 +218,24 @@
         concat_axis=0,
         tiled=True,
     )
-    expert_in = lax.all_gather(
-        arrived.reshape(peer_count * capacity, quarter_width), "head", axis=1, tiled=True
-    )
+    head_count = lax.axis_size("head")
+    expert_in = lax.all_to_all(
+        jnp.broadcast_to(
+            arrived.reshape(1, peer_count * capacity, quarter_width),
+            (head_count, peer_count * capacity, quarter_width),
+        ),
+        "head",
+        split_axis=0,
+        concat_axis=2,
+        tiled=True,
+    ).reshape(peer_count * capacity, head_count * quarter_width)
     gate_value = jnp.dot(expert_in, expert_gate[0], preferred_element_type=jnp.float32)
     up_value = jnp.dot(expert_in, expert_up[0], preferred_element_type=jnp.float32)
     activity = (jax.nn.silu(gate_value) * up_value).astype(jnp.bfloat16)
-    expert_share = lax.psum_scatter(
+    expert_share = head_sum_scatter(
         jnp.dot(activity, expert_down[0], preferred_element_type=jnp.float32).astype(jnp.bfloat16),
-        "head",
-        scatter_dimension=1,
-        tiled=True,
-    )
+        1,
+    ).astype(jnp.bfloat16)
     returned = lax.all_to_all(
         expert_share.reshape(peer_count, capacity, quarter_width),
         "tok",

time: 374 us -> 341 us (0.912)
  waiting for transfers between devices: 142 us -> 84.7 us
  blocking collectives: 70 us -> 88 us
  between operations: 14.3 us -> 1.28 us
  local copies, waits for them, and re-layouts: 57.8 us -> 66.9 us
  other arithmetic: 22.4 us -> 28.1 us
  starting transfers between devices: 39.3 us -> 43.4 us
    reduce_scatter x3 -> x0, waiting for transfers between devices: 66.6 us -> none  [the longest x1 26.9 us: body(): lax.psum_scatter(jnp.dot(activity, expert_down[0], preferred_element_type...]
    all_to_all x0 -> x3, waiting for transfers between devices: none -> 39.2 us  [head_sum_scatter(): lax.all_to_all(values, 'head', split_axis=axis, concat_axis=0, tiled=True)]
    all_gather x1 -> x0, waiting for transfers between devices: 24.3 us -> none  [body(): lax.all_gather(arrived.reshape(peer_count * capacity, quarter_width), 'he...]
    all_to_all x0 -> x1, blocking collectives: none -> 23.1 us  [body(): lax.all_to_all(jnp.broadcast_to(arrived.reshape(1, peer_count * capacity,...]
    all_to_all x0 -> x3, starting transfers between devices: none -> 12.3 us  [head_sum_scatter(): lax.all_to_all(values, 'head', split_axis=axis, concat_axis=0, tiled=True)]
    all_to_all x1, blocking collectives: 33.6 us -> 27.9 us  [body(): lax.all_to_all(padded_rows[source_token].reshape(expert_count, capacity,...]
    all_to_all x1, waiting for transfers between devices: 15.3 us -> 9.97 us  [body(): lax.all_to_all(joined[back_row], 'tok', 0, 0, tiled=True)[dest_owner]]
    all_to_all x1, starting transfers between devices: 13.3 us -> 9.07 us  [body(): lax.all_to_all(joined[back_row], 'tok', 0, 0, tiled=True)[dest_owner]]
  transfers between devices with their start and end apart: 7 -> 6, of which waited for: 7 -> 6; matrix products, arithmetic and copies ran while one was open for 2% -> 4% of each run, Pallas kernels for 0% -> 0%
where the time goes in v3:
time: 341 us; the launch traced here: 339 us
  blocking collectives  88 us (26%)
  waiting for transfers between devices  84.7 us (25%)
  local copies, waits for them, and re-layouts  66.9 us (20%)
  starting transfers between devices  43.4 us (13%)
  other arithmetic  28.1 us (8%)
  matrix products  26.6 us (8%)
    all_to_all x3, waiting for transfers between devices, head_sum_scatter(): lax.all_to_all(values, 'head', split_axis=axis, concat_axis=0, tiled=True)  39.2 us
    all_to_all x1, blocking collectives, body(): lax.all_to_all(padded_rows[source_token].reshape(expert_count, capacity,...  27.9 us
    all_to_all x1, blocking collectives, body(): lax.all_to_all(jnp.broadcast_to(arrived.reshape(1, peer_count * capacity,...  23.1 us
    all_to_all x1, waiting for transfers between devices, body(): got_packed = lax.all_to_all(packed, 'tok', 0, 0, tiled=True)  20 us
    all_to_all x1, waiting for transfers between devices, body(): lax.all_to_all(expert_share.reshape(peer_count, capacity, quarter_width),...  15.5 us
    all_to_all x1, starting transfers between devices, body(): got_packed = lax.all_to_all(packed, 'tok', 0, 0, tiled=True)  14.2 us
    psum x1, blocking collectives, body(): lax.psum((jnp.sum(attended_wide * attended_wide, axis=1), jnp.dot(gained,...  12.4 us
    all_gather x1, blocking collectives, body(): lax.all_gather(send_rows, 'head', axis=1, tiled=True)  12.4 us
  transfers between devices with their start and end apart: 6, of which 6 were waited for; matrix products, arithmetic and copies ran while one was open for 4% of the time, Pallas kernels for 0%

profile of v3, /device:TPU:1, one launch (start us, length us, event | category | flops | bytes accessed | tf_op | source)
XLA Modules:
  0.0 338.8 jit_solution(17548323209759700449)
XLA Ops:
  3.8 12.4 %all-gather = bf16[4,2240,32]{1,2,0:T(8,128)(2,1)S(1)} all-gather(bf16[1,2240,32]{1,2,0:T(8,128)(2,1)S(1)} %bitcast.109), channel_id=1, replica_groups=mesh['tok'=64,'head'=4] {'head'}, dimensions={0}, use_global_device_ids=true | all-gather | bytes 716800 | tf_op jit(solution)/shard_map/all_gather | solution.py:107
  17.5 2.4 reshape.616
  19.9 2.6 reshape.517
  23.7 2.0 slice.127
  30.7 2.1 copy_convert_fusion
  32.7 2.5 reshape.528
  35.2 3.2 fusion.25
  40.2 1.6 gather_fusion
  43.7 1.8 copy.368
  45.4 2.2 pad_maximum_fusion.1
  47.7 14.2 %all-to-all-start = ((bf16[64,5,576]{2,1,0:T(8,128)(2,1)}), bf16[64,5,576]{2,1,0:T(8,128)(2,1)}, u32[]{:S(2)}, u32[]{:S(2)}) async-start(bf16[64,5,576]{2,1,0:T(8,128)(2,1)} %pad_maximum_fusion.1), calls=%async_computation | async-start | bytes 1310720 | tf_op jit(solution)/shard_map/all_to_all | solution.py:153
  61.9 20.0 %all-to-all-done = bf16[64,5,576]{2,1,0:T(8,128)(2,1)} async-done(((bf16[64,5,576]{2,1,0:T(8,128)(2,1)}), bf16[64,5,576]{2,1,0:T(8,128)(2,1)}, u32[]{:S(2)}, u32[]{:S(2)}) %all-to-all-start) | async-done | bytes 368672 | tf_op jit(solution)/shard_map/all_to_all | solution.py:153
  83.8 1.9 copy.370
  85.7 2.1 gather_fusion.4
  87.8 12.1 %all_gather.7 = bf16[32,16,576]{2,0,1:T(8,128)(2,1)S(1)} all-gather(bf16[32,4,576]{2,0,1:T(8,128)(2,1)S(1)} %gather_fusion.4), channel_id=1, replica_groups=mesh['tok'=64,'head'=4] {'head'}, dimensions={1}, use_global_device_ids=true | all-gather | bytes 737280 | tf_op jit(solution)/shard_map/all_gather | solution.py:162
  104.1 4.5 %convert_reduce_fusion = (f32[512]{0:T(512)S(1)}, bf16[512,2496]{0,1:T(8,128)(2,1)}) fusion(pred[512,2496]{0,1:T(32,128)(4,1)S(1)} %copy.374, bf16[512,576]{1,0:T(8,128)(2,1)S(1)} %bitcast.108, bf16[2496,576]{0,1:T(8,128)(2,1)S(1)} %copy-done.23), kind=kOutput, calls=%fused_computation.11 | convolution fusion | flops 1478589952 | bytes 7301120 | tf_op jit(solution)/shard_map/qc,pc->qp/dot_general | solution.py:39
  108.6 4.4 %copy.372 = bf16[512,2496]{1,0:T(8,128)(2,1)} copy(bf16[512,2496]{0,1:T(8,128)(2,1)} %get-tuple-element.53) | data formatting | bytes 5111808 | tf_op jit(solution)/shard_map/exp | solution.py:46
  113.0 5.1 %fusion = f32[32,16,512]{2,1,0:T(8,128)} fusion(bf16[32,16,2496]{2,1,0:T(8,128)(2,1)} %bitcast.99, bf16[2496,576]{0,1:T(8,128)(2,1)} %param.25, pred[32,2496]{1,0:T(8,128)(4,1)S(1)} %compare_and_fusion), kind=kOutput, calls=%fused_computation.15 | convolution fusion | flops 1309900800 | bytes 6371328 | tf_op jit(solution)/shard_map/khp,pl->khl/dot_general | solution.py:47
  119.6 1.5 copy.376
  121.1 4.4 %all-to-all-start.1 = ((f32[32,16,513]{2,0,1:T(8,128)}), f32[32,16,513]{2,0,1:T(8,128)}, u32[]{:S(2)}, u32[]{:S(2)}) async-start(f32[32,16,513]{2,0,1:T(8,128)} %copy.376), calls=%async_computation.1 | async-start | bytes 2621440 | tf_op jit(solution)/shard_map/all_to_all | solution.py:56
  126.4 14.8 %all-to-all-done.1 = f32[32,16,513]{2,0,1:T(8,128)} async-done(((f32[32,16,513]{2,0,1:T(8,128)}), f32[32,16,513]{2,0,1:T(8,128)}, u32[]{:S(2)}, u32[]{:S(2)}) %all-to-all-start.1) | async-done | bytes 1050656 | tf_op jit(solution)/shard_map/all_to_all | solution.py:56
  141.2 1.4 reduce_sum.141
  142.9 1.8 gather_fusion.5
  144.7 9.1 %all-to-all-start.2 = ((f32[64,4,513]{2,1,0:T(4,128)}), f32[64,4,513]{2,1,0:T(4,128)}, u32[]{:S(2)}, u32[]{:S(2)}) async-start(f32[64,4,513]{2,1,0:T(4,128)} %gather_fusion.5), calls=%async_computation.2 | async-start | bytes 1310720 | tf_op jit(solution)/shard_map/all_to_all | solution.py:170
  155.7 3.9 %copy.396 = bf16[2048,512]{1,0:T(8,128)(2,1)} copy(bf16[2048,512]{0,1:T(8,128)(2,1)} %bitcast.101) | data formatting | bytes 4194304 | tf_op jit(solution)/shard_map/dot_general | solution.py:180
  160.1 1.6 gather_fusion.9
  163.8 10.0 %all-to-all-done.2 = f32[64,4,513]{2,1,0:T(4,128)} async-done(((f32[64,4,513]{2,1,0:T(4,128)}), f32[64,4,513]{2,1,0:T(4,128)}, u32[]{:S(2)}, u32[]{:S(2)}) %all-to-all-start.2) | async-done | bytes 525344 | tf_op jit(solution)/shard_map/all_to_all | solution.py:170
  173.8 2.0 gather_fusion.6
  176.4 1.5 copy.379
  184.1 3.0 fusion.67
  187.2 3.4 %all-to-all-start.3 = ((f32[32,4,512]{2,0,1:T(8,128)}), f32[32,4,512]{2,0,1:T(8,128)S(1)}, u32[]{:S(2)}, u32[]{:S(2)}) async-start(f32[32,4,512]{2,0,1:T(8,128)} %fusion.67), calls=%async_computation.3 | async-start | bytes 524288 | tf_op jit(solution)/shard_map/all_to_all | solution.py:56
  190.7 6.1 %all-to-all-done.3 = f32[32,4,512]{2,0,1:T(8,128)S(1)} async-done(((f32[32,4,512]{2,0,1:T(8,128)}), f32[32,4,512]{2,0,1:T(8,128)S(1)}, u32[]{:S(2)}, u32[]{:S(2)}) %all-to-all-start.3) | async-done | bytes 262176 | tf_op jit(solution)/shard_map/all_to_all | solution.py:56
  197.9 12.4 %all-reduce.4 = (f32[32]{0:T(128)S(1)}, f32[32,64]{1,0:T(8,128)}) all-reduce(f32[32]{0:T(128)S(1)} %get-tuple-element.25, f32[32,64]{1,0:T(8,128)S(1)} %fusion.43), channel_id=1, replica_groups=mesh['tok'=64,'head'=4] {'head'}, use_global_device_ids=true, to_apply=%region_13.14 | all-reduce | flops 2080 | bytes 16640 | tf_op jit(solution)/shard_map/psum | solution.py:184
  210.5 2.6 gather_fusion.7
  213.1 1.9 reshape.524
  215.0 27.9 %all_to_all.70 = bf16[64,6,512]{2,1,0:T(8,128)(2,1)} all-to-all(bf16[64,6,512]{2,1,0:T(8,128)(2,1)} %reshape.524), channel_id=1, replica_groups=mesh['tok'=64,'head'=4] {'tok'}, dimensions={0} | all-to-all | bytes 786432 | tf_op jit(solution)/shard_map/all_to_all | solution.py:214
  246.2 23.1 %all_to_all.71 = bf16[4,384,512]{1,2,0:T(8,128)(2,1)S(1)} all-to-all(bf16[4,384,512]{1,2,0:T(8,128)(2,1)S(1)} %broadcast_in_dim.151), channel_id=1, replica_groups=mesh['tok'=64,'head'=4] {'head'}, dimensions={0} | all-to-all | bytes 3145728 | tf_op jit(solution)/shard_map/all_to_all | solution.py:222
  270.4 1.7 fusion.8
  272.1 5.5 %convolution_convert_fusion = bf16[384,2048]{1,0:T(8,128)(2,1)} fusion(bf16[1,352,2048]{2,1,0:T(8,128)(2,1)} %param.33, bf16[384,2048]{0,1:T(8,128)(2,1)} %bitcast.103, bf16[1,2048,352]{1,2,0:T(8,128)(2,1)} %param.32, f32[384,352]{0,1:T(8,128)} %fusion.8), kind=kOutput, calls=%fused_computation.14 | convolution fusion | flops 1108893696 | bytes 6569984 | tf_op jit(solution)/shard_map/dot_general | solution.py:236
  277.6 2.7 copy.412
  280.3 4.5 %all-to-all-start.6 = ((bf16[384,4,512]{2,0,1:T(8,128)(2,1)}), bf16[384,4,512]{2,0,1:T(8,128)(2,1)}, u32[]{:S(2)}, u32[]{:S(2)}) async-start(bf16[384,4,512]{2,0,1:T(8,128)(2,1)} %bitcast.97), calls=%async_computation.6 | async-start | bytes 3145728 | tf_op jit(solution)/shard_map/all_to_all | solution.py:56
  286.1 18.3 %all-to-all-done.6 = bf16[384,4,512]{2,0,1:T(8,128)(2,1)} async-done(((bf16[384,4,512]{2,0,1:T(8,128)(2,1)}), bf16[384,4,512]{2,0,1:T(8,128)(2,1)}, u32[]{:S(2)}, u32[]{:S(2)}) %all-to-all-start.6) | async-done | bytes 1572896 | tf_op jit(solution)/shard_map/all_to_all | solution.py:56
  304.5 1.8 reduce_sum.147
  307.2 7.8 %all-to-all-start.7 = ((bf16[64,6,512]{2,1,0:T(8,128)(2,1)}), bf16[64,6,512]{2,1,0:T(8,128)(2,1)}, u32[]{:S(2)}, u32[]{:S(2)}) async-start(bf16[64,6,512]{2,1,0:T(8,128)(2,1)} %reshape.526), calls=%async_computation.7 | async-start | bytes 1048576 | tf_op jit(solution)/shard_map/all_to_all | solution.py:239
  316.8 15.5 %all-to-all-done.7 = bf16[64,6,512]{2,1,0:T(8,128)(2,1)} async-done(((bf16[64,6,512]{2,1,0:T(8,128)(2,1)}), bf16[64,6,512]{2,1,0:T(8,128)(2,1)}, u32[]{:S(2)}, u32[]{:S(2)}) %all-to-all-start.7) | async-done | bytes 393248 | tf_op jit(solution)/shard_map/all_to_all | solution.py:239
  333.5 1.7 gather_fusion.8
  335.1 1.8 reshape.609
  336.9 1.9 multiply_reduce_fusion
  (158 shorter events, 45.1 us)
Async XLA Ops:
  0.6 26.0 %copy-start = (bf16[2048,768]{1,0:T(8,128)(2,1)S(1)}, bf16[2048,768]{1,0:T(8,128)(2,1)}, u32[]{:S(2)}) copy-start(bf16[2048,768]{1,0:T(8,128)(2,1)} %param.20) | copy-start | bytes 9437188
  19.9 6.8 %copy-start.14 = (f32[2048]{0:T(1024)S(1)}, f32[2048]{0:T(1024)}, u32[]{:S(2)}) copy-start(f32[2048]{0:T(1024)} %param.19) | copy-start | bytes 24580
  26.7 0.9 copy-start.2
  26.7 0.9 copy-start.1
  40.2 7.5 %copy-start.4 = (bf16[32,4,576]{2,1,0:T(4,128)(2,1)}, bf16[32,4,576]{2,1,0:T(4,128)(2,1)S(1)}, u32[]{:S(2)}) copy-start(bf16[32,4,576]{2,1,0:T(4,128)(2,1)S(1)} %copy.354) | copy-start | bytes 442372
  47.7 34.2 %all-to-all-start = ((bf16[64,5,576]{2,1,0:T(8,128)(2,1)}), bf16[64,5,576]{2,1,0:T(8,128)(2,1)}, u32[]{:S(2)}, u32[]{:S(2)}) async-start(bf16[64,5,576]{2,1,0:T(8,128)(2,1)} %pad_maximum_fusion.1), calls=%async_computation | async-start | bytes 1310720 | tf_op jit(solution)/shard_map/all_to_all | solution.py:153
  102.0 1.8 copy-start.23
  102.4 1.7 copy-start.5
  121.1 5.3 %copy-start.21 = (s32[64]{0:T(128)S(1)}, s32[64]{0:T(128)}, u32[]{:S(2)}) copy-start(s32[64]{0:T(128)} %get-tuple-element.15) | copy-start | bytes 772
  121.1 20.1 %all-to-all-start.1 = ((f32[32,16,513]{2,0,1:T(8,128)}), f32[32,16,513]{2,0,1:T(8,128)}, u32[]{:S(2)}, u32[]{:S(2)}) async-start(f32[32,16,513]{2,0,1:T(8,128)} %copy.376), calls=%async_computation.1 | async-start | bytes 2621440 | tf_op jit(solution)/shard_map/all_to_all | solution.py:56
  126.4 27.4 %copy-start.8 = (bf16[32,512]{1,0:T(8,128)(2,1)}, bf16[32,512]{1,0:T(8,128)(2,1)S(1)}, u32[]{:S(2)}) copy-start(bf16[32,512]{1,0:T(8,128)(2,1)S(1)} %get-tuple-element.28) | copy-start | bytes 98308
  144.7 29.1 %all-to-all-start.2 = ((f32[64,4,513]{2,1,0:T(4,128)}), f32[64,4,513]{2,1,0:T(4,128)}, u32[]{:S(2)}, u32[]{:S(2)}) async-start(f32[64,4,513]{2,1,0:T(4,128)} %gather_fusion.5), calls=%async_computation.2 | async-start | bytes 1310720 | tf_op jit(solution)/shard_map/all_to_all | solution.py:170
  155.7 4.0 %copy-start.12 = (s32[32,6]{0,1:T(8,128)S(1)}, s32[32,6]{0,1:T(8,128)}, u32[]{:S(2)}) copy-start(s32[32,6]{0,1:T(8,128)} %param.30) | copy-start | bytes 2308
  160.0 2.4 copy-start.22
  160.0 21.9 %copy-start.10 = (f32[32,512]{1,0:T(8,128)S(1)}, f32[32,512]{1,0:T(8,128)}, u32[]{:S(2)}) copy-start(f32[32,512]{1,0:T(8,128)} %get-tuple-element.27) | copy-start | bytes 196612
  184.0 6.6 %copy-start.16 = (s32[384]{0:T(512)S(1)}, s32[384]{0:T(512)}, u32[]{:S(2)}) copy-start(s32[384]{0:T(512)} %get-tuple-element.17) | copy-start | bytes 4612
  184.1 6.6 %copy-start.17 = (s32[384]{0:T(512)S(1)}, s32[384]{0:T(512)}, u32[]{:S(2)}) copy-start(s32[384]{0:T(512)} %get-tuple-element.18) | copy-start | bytes 4612
  184.1 12.7 %copy-start.6 = (bf16[32,512]{1,0:T(8,128)(2,1)S(1)}, bf16[32,512]{1,0:T(8,128)(2,1)}, u32[]{:S(2)}) copy-start(bf16[32,512]{1,0:T(8,128)(2,1)} %param.18) | copy-start | bytes 98308
  184.1 12.8 %copy-start.15 = (f32[512]{0:T(512)S(1)}, f32[512]{0:T(512)}, u32[]{:S(2)}) copy-start(f32[512]{0:T(512)} %param.28) | copy-start | bytes 6148
  187.2 9.6 %all-to-all-start.3 = ((f32[32,4,512]{2,0,1:T(8,128)}), f32[32,4,512]{2,0,1:T(8,128)S(1)}, u32[]{:S(2)}, u32[]{:S(2)}) async-start(f32[32,4,512]{2,0,1:T(8,128)} %fusion.67), calls=%async_computation.3 | async-start | bytes 524288 | tf_op jit(solution)/shard_map/all_to_all | solution.py:56
  196.9 13.4 %copy-start.7 = (bf16[32,512]{1,0:T(8,128)(2,1)}, bf16[32,512]{1,0:T(8,128)(2,1)S(1)}, u32[]{:S(2)}) copy-start(bf16[32,512]{1,0:T(8,128)(2,1)S(1)} %get-tuple-element.26) | copy-start | bytes 98308
  210.4 2.7 copy-start.19
  246.2 24.2 %copy-start.24 = (bf16[1,2048,352]{1,2,0:T(8,128)(2,1)S(1)}, bf16[1,2048,352]{1,2,0:T(8,128)(2,1)}, u32[]{:S(2)}) copy-start(bf16[1,2048,352]{1,2,0:T(8,128)(2,1)} %param.31) | copy-start | bytes 4325380
  269.2 1.2 copy-start.3
  280.3 4.5 %copy-start.11 = (s32[32,6]{1,0:T(8,128)S(1)}, s32[32,6]{1,0:T(8,128)}, u32[]{:S(2)}) copy-start(s32[32,6]{1,0:T(8,128)} %get-tuple-element.23) | copy-start | bytes 2308
  280.3 5.2 %copy-start.9 = (bf16[32,512]{1,0:T(8,128)(2,1)S(1)}, bf16[32,512]{1,0:T(8,128)(2,1)}, u32[]{:S(2)}) copy-start(bf16[32,512]{1,0:T(8,128)(2,1)} %copy-done.8) | copy-start | bytes 98308
  280.3 24.2 %all-to-all-start.6 = ((bf16[384,4,512]{2,0,1:T(8,128)(2,1)}), bf16[384,4,512]{2,0,1:T(8,128)(2,1)}, u32[]{:S(2)}, u32[]{:S(2)}) async-start(bf16[384,4,512]{2,0,1:T(8,128)(2,1)} %bitcast.97), calls=%async_computation.6 | async-start | bytes 3145728 | tf_op jit(solution)/shard_map/all_to_all | solution.py:56
  286.1 28.9 %copy-start.18 = (s32[192]{0:T(256)S(1)}, s32[192]{0:T(256)}, u32[]{:S(2)}) copy-start(s32[192]{0:T(256)} %reshape.594) | copy-start | bytes 2308
  286.1 29.0 %copy-start.20 = (f32[32]{0:T(128)S(1)}, f32[32]{0:T(128)}, u32[]{:S(2)}) copy-start(f32[32]{0:T(128)} %copy-done.19) | copy-start | bytes 388
  286.1 29.8 %copy-start.13 = (s32[32,6]{0,1:T(8,128)S(1)}, s32[32,6]{0,1:T(8,128)}, u32[]{:S(2)}) copy-start(s32[32,6]{0,1:T(8,128)} %param.30) | copy-start | bytes 2308
  307.2 25.1 %all-to-all-start.7 = ((bf16[64,6,512]{2,1,0:T(8,128)(2,1)}), bf16[64,6,512]{2,1,0:T(8,128)(2,1)}, u32[]{:S(2)}, u32[]{:S(2)}) async-start(bf16[64,6,512]{2,1,0:T(8,128)(2,1)} %reshape.526), calls=%async_computation.7 | async-start | bytes 1048576 | tf_op jit(solution)/shard_map/all_to_all | solution.py:239

commit v4 on v3

--- a/solution.py
+++ b/solution.py
@@ -84,38 +84,46 @@
     tok_index = lax.axis_index("tok")
     row_ids = jnp.arange(local_rows, dtype=jnp.int32)
     latent_width = w_latent.shape[1]
+    head_count = lax.axis_size("head")
     gain_part = lax.dynamic_slice_in_dim(attn_gain, head_index * quarter_width, quarter_width, 0)
     raw_part = jnp.dot(
         (hidden.astype(jnp.float32) * gain_part).astype(jnp.bfloat16),
         w_latent,
         preferred_element_type=jnp.float32,
     )
+    part_width = -(-latent_width // 128) * 128
     part_hi = lax.reduce_precision(raw_part, exponent_bits=8, mantissa_bits=7)
     rest = raw_part - part_hi
     part_mid = lax.reduce_precision(rest, exponent_bits=8, mantissa_bits=7)
     part_lo = rest - part_mid
+    lane_pad = jnp.zeros((local_rows, part_width - latent_width), jnp.bfloat16)
     send_rows = jnp.concatenate(
         [
             hidden,
             part_hi.astype(jnp.bfloat16),
+            lane_pad,
             part_mid.astype(jnp.bfloat16),
+            lane_pad,
             part_lo.astype(jnp.bfloat16),
+            lane_pad,
         ],
         axis=1,
     )
-    piece_width = send_rows.shape[1]
-    got_rows = lax.all_gather(send_rows, "head", axis=1, tiled=True).reshape(
-        local_rows, -1, piece_width
-    )
-    gathered = got_rows[:, :, :quarter_width].reshape(local_rows, -1)
-    got_parts = got_rows[:, :, quarter_width:].reshape(local_rows, -1, 3, latent_width).astype(
-        jnp.float32
-    )
-    part_sums = (got_parts[:, :, 0] + got_parts[:, :, 1]) + got_parts[:, :, 2]
-    widened = gathered.astype(jnp.float32)
-    inv_attn = lax.rsqrt(jnp.mean(widened * widened, axis=1, keepdims=True) + NORM_EPS)
-    normed_attn = (widened * inv_attn * attn_gain).astype(jnp.bfloat16)
-    compressed = jnp.sum(part_sums, axis=1) * inv_attn
+    got_rows = lax.all_gather(send_rows, "head", axis=0, tiled=False)
+    hidden_groups = got_rows[:, :, :quarter_width].astype(jnp.float32)
+
+    def part_piece(k):
+        offset = quarter_width + k * part_width
+        return got_rows[:, :, offset : offset + latent_width].astype(jnp.float32)
+
+    part_sums = (part_piece(0) + part_piece(1)) + part_piece(2)
+    inv_attn = lax.rsqrt(
+        jnp.sum(hidden_groups * hidden_groups, axis=(0, 2))[:, None] / D + NORM_EPS
+    )
+    normed_groups = (
+        hidden_groups * inv_attn[None] * attn_gain.reshape(head_count, 1, quarter_width)
+    ).astype(jnp.bfloat16)
+    compressed = jnp.sum(part_sums, axis=0) * inv_attn
     latent_new = compressed[:, :LATENT]
     latent_new = latent_new * lax.rsqrt(
         jnp.mean(latent_new * latent_new, axis=1, keepdims=True) + NORM_EPS
@@ -123,7 +131,12 @@
     new_entry = jnp.concatenate(
         [latent_new, rotate_pairs(compressed[:, LATENT:], cache_lengths)], axis=1
     ).astype(jnp.bfloat16)
-    queries = jnp.dot(normed_attn, w_query, preferred_element_type=jnp.float32).astype(jnp.bfloat16)
+    queries = jnp.einsum(
+        "gbf,gfq->bq",
+        normed_groups,
+        w_query.reshape(head_count, quarter_width, w_query.shape[1]),
+        preferred_element_type=jnp.float32,
+    ).astype(jnp.bfloat16)
     queries = queries.reshape(local_rows, local_heads, NOPE + ROPE)
     absorbed = jnp.einsum(
         "bhn,hnl->bhl", queries[:, :, :NOPE], w_key_up, preferred_element_type=jnp.float32
@@ -133,10 +146,6 @@
     )
     probes = jnp.concatenate([absorbed, turned], axis=2)
     factor = (NOPE + ROPE) ** (-0.5)
-    self_score = factor * jnp.einsum(
-        "bhc,bc->bh", probes, new_entry, preferred_element_type=jnp.float32
-    )
-    self_weight = jnp.exp(self_score).astype(jnp.bfloat16).astype(jnp.float32)
     owner_ids = jnp.arange(peer_count, dtype=jnp.int32)
     dest_owner = request_slot // local_rows
     goes_to = dest_owner[None, :] == owner_ids[:, None]
@@ -149,9 +158,11 @@
     ) * sent_any[:, None]
     code_row = jnp.zeros((peer_count, probes.shape[2]), jnp.float32)
     code_row = code_row.at[:, :5].set(code.astype(jnp.float32)).astype(jnp.bfloat16)
-    packed = jnp.concatenate([probes[sent_row], code_row[:, None, :]], axis=1)
+    packed = jnp.concatenate(
+        [probes[sent_row], new_entry[sent_row][:, None, :], code_row[:, None, :]], axis=1
+    )
     got_packed = lax.all_to_all(packed, "tok", 0, 0, tiled=True)
-    got_code = got_packed[:, local_heads, :5].astype(jnp.float32).astype(jnp.int32)
+    got_code = got_packed[:, local_heads + 1, :5].astype(jnp.float32).astype(jnp.int32)
     got_slot = jnp.where(got_code[:, 0] > 0, got_code[:, 1] * 64 + got_code[:, 2], -1)
     got_len = got_code[:, 3] * 64 + got_code[:, 4]
     local_slot = got_slot - tok_index * local_rows
@@ -159,23 +170,31 @@
     src_of_slot = jnp.sum(jnp.where(slot_sel, owner_ids[None, :], 0), axis=1)
     owner_probes = got_packed[src_of_slot, :local_heads]
     owner_lengths = got_len[src_of_slot]
+    owner_new = got_packed[src_of_slot, local_heads]
     all_heads = lax.all_gather(owner_probes, "head", axis=1, tiled=True)
     numerator, denominator = owner_attend(
         all_heads, owner_lengths, latent_cache, head_index, factor
     )
     joined = head_sum_scatter(jnp.concatenate([numerator, denominator[:, :, None]], axis=2), 1)
-    joined = jnp.concatenate([joined, jnp.zeros((1,) + joined.shape[1:], jnp.float32)], axis=0)
+    self_score = factor * jnp.einsum(
+        "bhc,bc->bh", owner_probes, owner_new, preferred_element_type=jnp.float32
+    )
+    self_weight = jnp.exp(self_score).astype(jnp.bfloat16).astype(jnp.float32)
+    total_num = joined[:, :, :LATENT] + self_weight[:, :, None] * owner_new[:, None, :LATENT].astype(
+        jnp.float32
+    )
+    total_den = joined[:, :, LATENT] + self_weight
+    mixed_latent = (total_num / total_den[:, :, None]).astype(jnp.bfloat16)
+    owner_out = jnp.einsum(
+        "bhl,hld->bhd", mixed_latent, w_value_up, preferred_element_type=jnp.float32
+    ).astype(jnp.bfloat16)
+    owner_out = owner_out.reshape(local_rows, local_heads * NOPE)
+    owner_out = jnp.concatenate(
+        [owner_out, jnp.zeros((1, local_heads * NOPE), jnp.bfloat16)], axis=0
+    )
     back_valid = (local_slot >= 0) & (local_slot < local_rows)
     back_row = jnp.where(back_valid, local_slot, local_rows)
-    returned = lax.all_to_all(joined[back_row], "tok", 0, 0, tiled=True)[dest_owner]
-    total_num = returned[:, :, :LATENT] + self_weight[:, :, None] * new_entry[:, None, :LATENT].astype(
-        jnp.float32
-    )
-    total_den = returned[:, :, LATENT] + self_weight
-    mixed_latent = (total_num / total_den[:, :, None]).astype(jnp.bfloat16)
-    head_out = jnp.einsum(
-        "bhl,hld->bhd", mixed_latent, w_value_up, preferred_element_type=jnp.float32
-    ).astype(jnp.bfloat16)
+    head_out = lax.all_to_all(owner_out[back_row], "tok", 0, 0, tiled=True)[dest_owner]
     head_out = head_out.reshape(local_rows, local_heads * NOPE)
     attn_piece = head_sum_scatter(jnp.dot(head_out, w_out, preferred_element_type=jnp.float32), 1)
     attended = (hidden.astype(jnp.float32) + attn_piece).astype(jnp.bfloat16)
@@ -218,7 +237,6 @@
         concat_axis=0,
         tiled=True,
     )
-    head_count = lax.axis_size("head")
     expert_in = lax.all_to_all(
         jnp.broadcast_to(
             arrived.reshape(1, peer_count * capacity, quarter_width),

time: 341 us -> 311 us (0.912)
  local copies, waits for them, and re-layouts: 66.9 us -> 50.3 us
  other arithmetic: 28.1 us -> 23 us
  waiting for transfers between devices: 84.7 us -> 80.1 us
    dot_general x2 -> x1, local copies, waits for them, and re-layouts: 4.61 us -> 0.08 us  [body(): jnp.einsum('bhc,bc->bh', owner_probes, owner_new, preferred_element_type=...]
    reduce_sum x2, other arithmetic: 4.46 us -> 0.83 us  [the longest x1 0.69 us: body(): compressed = jnp.sum(part_sums, axis=0) * inv_attn]
  transfers between devices with their start and end apart: 6 -> 6, of which waited for: 6 -> 6; matrix products, arithmetic and copies ran while one was open for 4% -> 3% of each run, Pallas kernels for 0% -> 0%
where the time goes in v4:
time: 311 us; the launch traced here: 309 us
  blocking collectives  87.3 us (28%)
  waiting for transfers between devices  80.1 us (26%)
  local copies, waits for them, and re-layouts  50.3 us (16%)
  starting transfers between devices  43.4 us (14%)
  matrix products  23.7 us (8%)
  other arithmetic  23 us (7%)
    all_to_all x3, waiting for transfers between devices, head_sum_scatter(): lax.all_to_all(values, 'head', split_axis=axis, concat_axis=0, tiled=True)  37.7 us
    all_to_all x1, blocking collectives, body(): lax.all_to_all(padded_rows[source_token].reshape(expert_count, capacity,...  27.4 us
    all_to_all x1, blocking collectives, body(): lax.all_to_all(jnp.broadcast_to(arrived.reshape(1, peer_count * capacity,...  23 us
    all_to_all x1, waiting for transfers between devices, body(): got_packed = lax.all_to_all(packed, 'tok', 0, 0, tiled=True)  17.3 us
    all_to_all x1, waiting for transfers between devices, body(): lax.all_to_all(expert_share.reshape(peer_count, capacity, quarter_width),...  15.5 us
    all_to_all x1, starting transfers between devices, body(): got_packed = lax.all_to_all(packed, 'tok', 0, 0, tiled=True)  14.1 us
    all_gather x1, blocking collectives, body(): got_rows = lax.all_gather(send_rows, 'head', axis=0, tiled=False)  12.5 us
    all_to_all x3, starting transfers between devices, head_sum_scatter(): lax.all_to_all(values, 'head', split_axis=axis, concat_axis=0, tiled=True)  12.3 us
  transfers between devices with their start and end apart: 6, of which 6 were waited for; matrix products, arithmetic and copies ran while one was open for 3% of the time, Pallas kernels for 0%

profile of v4, /device:TPU:1, one launch (start us, length us, event | category | flops | bytes accessed | tf_op | source)
XLA Modules:
  0.0 308.9 jit_solution(16886196573759821360)
XLA Ops:
  3.0 1.2 compare_select_fusion.5
  4.5 1.4 gather_fusion.3
  6.0 1.4 gather_fusion.2
  8.9 1.4 fusion.39
  10.4 12.5 %all-gather = bf16[128,2432]{1,0:T(8,128)(2,1)S(1)} all-gather(bf16[32,2432]{1,0:T(8,128)(2,1)S(1)} %concatenate.33), channel_id=2, replica_groups=mesh['tok'=64,'head'=4] {'head'}, dimensions={0}, use_global_device_ids=true | all-gather | bytes 778240 | tf_op jit(solution)/shard_map/all_gather | solution.py:112
  27.9 1.4 multiply_cosine_fusion
  30.9 1.3 fusion.16
  33.1 1.6 gather_fusion
  34.7 2.5 pad_maximum_fusion.1
  37.2 14.1 %all-to-all-start = ((bf16[64,6,576]{2,1,0:T(8,128)(2,1)}), bf16[64,6,576]{2,1,0:T(8,128)(2,1)}, u32[]{:S(2)}, u32[]{:S(2)}) async-start(bf16[64,6,576]{2,1,0:T(8,128)(2,1)} %pad_maximum_fusion.1), calls=%async_computation | async-start | bytes 1310720 | tf_op jit(solution)/shard_map/all_to_all | solution.py:164
  51.7 1.6 gather_fusion.11
  54.0 17.3 %all-to-all-done = bf16[64,6,576]{2,1,0:T(8,128)(2,1)} async-done(((bf16[64,6,576]{2,1,0:T(8,128)(2,1)}), bf16[64,6,576]{2,1,0:T(8,128)(2,1)}, u32[]{:S(2)}, u32[]{:S(2)}) %all-to-all-start) | async-done | bytes 442400 | tf_op jit(solution)/shard_map/all_to_all | solution.py:164
  73.7 1.9 copy.274
  75.7 2.1 gather_fusion.5
  77.8 12.1 %all_gather.11 = bf16[32,16,576]{2,0,1:T(8,128)(2,1)S(1)} all-gather(bf16[32,4,576]{2,0,1:T(8,128)(2,1)S(1)} %gather_fusion.5), channel_id=1, replica_groups=mesh['tok'=64,'head'=4] {'head'}, dimensions={1}, use_global_device_ids=true | all-gather | bytes 737280 | tf_op jit(solution)/shard_map/all_gather | solution.py:174
  90.7 1.4 copy.278
  92.1 4.5 %convert_reduce_fusion = (f32[512]{0:T(512)S(1)}, bf16[512,2496]{0,1:T(8,128)(2,1)}) fusion(pred[512,2496]{0,1:T(32,128)(4,1)S(1)} %copy.278, bf16[512,576]{1,0:T(8,128)(2,1)S(1)} %bitcast.119, bf16[2496,576]{0,1:T(8,128)(2,1)S(1)} %copy-done.13), kind=kOutput, calls=%fused_computation.13 | convolution fusion | flops 1478589952 | bytes 7301120 | tf_op jit(solution)/shard_map/qc,pc->qp/dot_general | solution.py:39
  96.9 4.4 %copy.276 = bf16[512,2496]{1,0:T(8,128)(2,1)} copy(bf16[512,2496]{0,1:T(8,128)(2,1)} %get-tuple-element.52) | data formatting | bytes 5111808 | tf_op jit(solution)/shard_map/exp | solution.py:46
  101.3 4.1 %fusion = f32[32,16,512]{2,1,0:T(8,128)S(1)} fusion(bf16[32,16,2496]{2,1,0:T(8,128)(2,1)} %bitcast.111, bf16[2496,576]{0,1:T(8,128)(2,1)} %param.25, pred[32,2496]{1,0:T(8,128)(4,1)S(1)} %compare_and_fusion), kind=kOutput, calls=%fused_computation.17 | convolution fusion | flops 1309900800 | bytes 6371328 | tf_op jit(solution)/shard_map/khp,pl->khl/dot_general | solution.py:47
  105.5 1.5 copy.280
  107.0 4.4 %all-to-all-start.1 = ((f32[32,16,513]{2,0,1:T(8,128)}), f32[32,16,513]{2,0,1:T(8,128)}, u32[]{:S(2)}, u32[]{:S(2)}) async-start(f32[32,16,513]{2,0,1:T(8,128)} %copy.280), calls=%async_computation.1 | async-start | bytes 2621440 | tf_op jit(solution)/shard_map/all_to_all | solution.py:56
  112.0 1.8 gather_fusion.6
  114.8 12.2 %all-to-all-done.1 = f32[32,16,513]{2,0,1:T(8,128)} async-done(((f32[32,16,513]{2,0,1:T(8,128)}), f32[32,16,513]{2,0,1:T(8,128)}, u32[]{:S(2)}, u32[]{:S(2)}) %all-to-all-start.1) | async-done | bytes 1050656 | tf_op jit(solution)/shard_map/all_to_all | solution.py:56
  127.0 1.4 reduce_sum.141
  130.9 1.2 fusion.31
  132.1 1.2 fusion.18
  135.9 8.9 %all-to-all-start.2 = ((bf16[64,2,256]{2,1,0:T(2,128)(2,1)}), bf16[64,2,256]{2,1,0:T(2,128)(2,1)S(1)}, u32[]{:S(2)}, u32[]{:S(2)}) async-start(bf16[64,2,256]{2,1,0:T(2,128)(2,1)} %reshape.637), calls=%async_computation.2 | async-start | bytes 131072 | tf_op jit(solution)/shard_map/all_to_all | solution.py:197
  145.1 9.5 %all-to-all-done.2 = bf16[64,2,256]{2,1,0:T(2,128)(2,1)S(1)} async-done(((bf16[64,2,256]{2,1,0:T(2,128)(2,1)}), bf16[64,2,256]{2,1,0:T(2,128)(2,1)S(1)}, u32[]{:S(2)}, u32[]{:S(2)}) %all-to-all-start.2) | async-done | bytes 65568 | tf_op jit(solution)/shard_map/all_to_all | solution.py:197
  155.3 2.1 fusion.73
  158.1 3.4 %all-to-all-start.3 = ((f32[32,4,512]{2,0,1:T(8,128)}), f32[32,4,512]{2,0,1:T(8,128)S(1)}, u32[]{:S(2)}, u32[]{:S(2)}) async-start(f32[32,4,512]{2,0,1:T(8,128)} %bitcast.118), calls=%async_computation.3 | async-start | bytes 524288 | tf_op jit(solution)/shard_map/all_to_all | solution.py:56
  161.6 6.0 %all-to-all-done.3 = f32[32,4,512]{2,0,1:T(8,128)S(1)} async-done(((f32[32,4,512]{2,0,1:T(8,128)}), f32[32,4,512]{2,0,1:T(8,128)S(1)}, u32[]{:S(2)}, u32[]{:S(2)}) %all-to-all-start.3) | async-done | bytes 262176 | tf_op jit(solution)/shard_map/all_to_all | solution.py:56
  168.7 12.3 %all-reduce.5 = (f32[32]{0:T(128)S(1)}, f32[32,64]{1,0:T(8,128)}) all-reduce(f32[32]{0:T(128)S(1)} %get-tuple-element.25, f32[32,64]{1,0:T(8,128)S(1)} %fusion.49), channel_id=1, replica_groups=mesh['tok'=64,'head'=4] {'head'}, use_global_device_ids=true, to_apply=%region_13.14 | all-reduce | flops 2080 | bytes 16640 | tf_op jit(solution)/shard_map/psum | solution.py:203
  181.1 2.6 gather_fusion.9
  183.7 1.9 reshape.523
  185.6 27.4 %all_to_all.80 = bf16[64,6,512]{2,1,0:T(8,128)(2,1)} all-to-all(bf16[64,6,512]{2,1,0:T(8,128)(2,1)} %reshape.523), channel_id=1, replica_groups=mesh['tok'=64,'head'=4] {'tok'}, dimensions={0} | all-to-all | bytes 786432 | tf_op jit(solution)/shard_map/all_to_all | solution.py:233
  213.0 1.2 broadcast_in_dim.159
  216.3 23.0 %all_to_all.81 = bf16[4,384,512]{1,2,0:T(8,128)(2,1)S(1)} all-to-all(bf16[4,384,512]{1,2,0:T(8,128)(2,1)S(1)} %broadcast_in_dim.160), channel_id=1, replica_groups=mesh['tok'=64,'head'=4] {'head'}, dimensions={0} | all-to-all | bytes 3145728 | tf_op jit(solution)/shard_map/all_to_all | solution.py:240
  240.4 1.7 fusion.8
  242.1 5.5 %convolution_convert_fusion = bf16[384,2048]{1,0:T(8,128)(2,1)} fusion(bf16[1,352,2048]{2,1,0:T(8,128)(2,1)} %param.33, bf16[384,2048]{0,1:T(8,128)(2,1)} %bitcast.114, bf16[1,2048,352]{1,2,0:T(8,128)(2,1)} %param.32, f32[384,352]{0,1:T(8,128)} %fusion.8), kind=kOutput, calls=%fused_computation.16 | convolution fusion | flops 1108893696 | bytes 6569984 | tf_op jit(solution)/shard_map/dot_general | solution.py:254
  247.6 2.7 copy.332
  250.3 4.5 %all-to-all-start.6 = ((bf16[384,4,512]{2,0,1:T(8,128)(2,1)}), bf16[384,4,512]{2,0,1:T(8,128)(2,1)}, u32[]{:S(2)}, u32[]{:S(2)}) async-start(bf16[384,4,512]{2,0,1:T(8,128)(2,1)} %bitcast.106), calls=%async_computation.6 | async-start | bytes 3145728 | tf_op jit(solution)/shard_map/all_to_all | solution.py:56
  254.9 19.5 %all-to-all-done.6 = bf16[384,4,512]{2,0,1:T(8,128)(2,1)} async-done(((bf16[384,4,512]{2,0,1:T(8,128)(2,1)}), bf16[384,4,512]{2,0,1:T(8,128)(2,1)}, u32[]{:S(2)}, u32[]{:S(2)}) %all-to-all-start.6) | async-done | bytes 1572896 | tf_op jit(solution)/shard_map/all_to_all | solution.py:56
  274.4 1.8 reduce_sum.147
  277.2 8.1 %all-to-all-start.7 = ((bf16[64,6,512]{2,1,0:T(8,128)(2,1)}), bf16[64,6,512]{2,1,0:T(8,128)(2,1)}, u32[]{:S(2)}, u32[]{:S(2)}) async-start(bf16[64,6,512]{2,1,0:T(8,128)(2,1)} %reshape.525), calls=%async_computation.7 | async-start | bytes 1048576 | tf_op jit(solution)/shard_map/all_to_all | solution.py:257
  286.9 15.5 %all-to-all-done.7 = bf16[64,6,512]{2,1,0:T(8,128)(2,1)} async-done(((bf16[64,6,512]{2,1,0:T(8,128)(2,1)}), bf16[64,6,512]{2,1,0:T(8,128)(2,1)}, u32[]{:S(2)}, u32[]{:S(2)}) %all-to-all-start.7) | async-done | bytes 393248 | tf_op jit(solution)/shard_map/all_to_all | solution.py:257
  303.6 1.7 gather_fusion.10
  305.3 1.8 reshape.621
  307.0 1.9 multiply_reduce_fusion
  (139 shorter events, 32.8 us)
Async XLA Ops:
  0.6 23.1 %copy-start = (bf16[2048,768]{1,0:T(8,128)(2,1)S(1)}, bf16[2048,768]{1,0:T(8,128)(2,1)}, u32[]{:S(2)}) copy-start(bf16[2048,768]{1,0:T(8,128)(2,1)} %param.20) | copy-start | bytes 9437188
  0.6 9.6 %copy-start.6 = (bf16[32,512]{1,0:T(8,128)(2,1)S(1)}, bf16[32,512]{1,0:T(8,128)(2,1)}, u32[]{:S(2)}) copy-start(bf16[32,512]{1,0:T(8,128)(2,1)} %param.18) | copy-start | bytes 98308
  23.7 4.1 %copy-start.12 = (f32[32]{0:T(128)S(1)}, f32[32]{0:T(128)}, u32[]{:S(2)}) copy-start(f32[32]{0:T(128)} %multiply_power_fusion) | copy-start | bytes 388
  29.3 5.4 %copy-start.1 = (bf16[32,576]{1,0:T(8,128)(2,1)}, bf16[32,576]{1,0:T(8,128)(2,1)S(1)}, u32[]{:S(2)}) copy-start(bf16[32,576]{1,0:T(8,128)(2,1)S(1)} %pad_maximum_fusion.3) | copy-start | bytes 110596
  33.1 18.2 %copy-start.9 = (s32[32,6]{0,1:T(8,128)S(1)}, s32[32,6]{0,1:T(8,128)}, u32[]{:S(2)}) copy-start(s32[32,6]{0,1:T(8,128)} %param.30) | copy-start | bytes 2308
  37.2 34.2 %all-to-all-start = ((bf16[64,6,576]{2,1,0:T(8,128)(2,1)}), bf16[64,6,576]{2,1,0:T(8,128)(2,1)}, u32[]{:S(2)}, u32[]{:S(2)}) async-start(bf16[64,6,576]{2,1,0:T(8,128)(2,1)} %pad_maximum_fusion.1), calls=%async_computation | async-start | bytes 1310720 | tf_op jit(solution)/shard_map/all_to_all | solution.py:164
  77.8 12.8 %copy-start.3 = (bf16[32,4,576]{2,0,1:T(8,128)(2,1)}, bf16[32,4,576]{2,0,1:T(8,128)(2,1)S(1)}, u32[]{:S(2)}) copy-start(bf16[32,4,576]{2,0,1:T(8,128)(2,1)S(1)} %gather_fusion.5) | copy-start | bytes 442372
  90.3 1.8 copy-start.13
  107.0 4.4 %copy-start.8 = (s32[32,6]{1,0:T(8,128)S(1)}, s32[32,6]{1,0:T(8,128)}, u32[]{:S(2)}) copy-start(s32[32,6]{1,0:T(8,128)} %reshape.614) | copy-start | bytes 2308
  107.0 6.8 %copy-start.4 = (bf16[32,4,576]{2,0,1:T(8,128)(2,1)S(1)}, bf16[32,4,576]{2,0,1:T(8,128)(2,1)}, u32[]{:S(2)}) copy-start(bf16[32,4,576]{2,0,1:T(8,128)(2,1)} %copy-done.3) | copy-start | bytes 442372
  107.0 20.1 %all-to-all-start.1 = ((f32[32,16,513]{2,0,1:T(8,128)}), f32[32,16,513]{2,0,1:T(8,128)}, u32[]{:S(2)}, u32[]{:S(2)}) async-start(f32[32,16,513]{2,0,1:T(8,128)} %copy.280), calls=%async_computation.1 | async-start | bytes 2621440 | tf_op jit(solution)/shard_map/all_to_all | solution.py:56
  128.5 16.4 %copy-start.11 = (s32[32]{0:T(128)S(1)}, s32[32]{0:T(128)}, u32[]{:S(2)}) copy-start(s32[32]{0:T(128)} %get-tuple-element.27) | copy-start | bytes 388
  135.9 18.7 %all-to-all-start.2 = ((bf16[64,2,256]{2,1,0:T(2,128)(2,1)}), bf16[64,2,256]{2,1,0:T(2,128)(2,1)S(1)}, u32[]{:S(2)}, u32[]{:S(2)}) async-start(bf16[64,2,256]{2,1,0:T(2,128)(2,1)} %reshape.637), calls=%async_computation.2 | async-start | bytes 131072 | tf_op jit(solution)/shard_map/all_to_all | solution.py:197
  155.3 12.4 %copy-start.10 = (f32[512]{0:T(512)S(1)}, f32[512]{0:T(512)}, u32[]{:S(2)}) copy-start(f32[512]{0:T(512)} %param.28) | copy-start | bytes 6148
  158.1 9.5 %all-to-all-start.3 = ((f32[32,4,512]{2,0,1:T(8,128)}), f32[32,4,512]{2,0,1:T(8,128)S(1)}, u32[]{:S(2)}, u32[]{:S(2)}) async-start(f32[32,4,512]{2,0,1:T(8,128)} %bitcast.118), calls=%async_computation.3 | async-start | bytes 524288 | tf_op jit(solution)/shard_map/all_to_all | solution.py:56
  167.7 13.3 %copy-start.5 = (bf16[32,512]{1,0:T(8,128)(2,1)}, bf16[32,512]{1,0:T(8,128)(2,1)S(1)}, u32[]{:S(2)}) copy-start(bf16[32,512]{1,0:T(8,128)(2,1)S(1)} %get-tuple-element.26) | copy-start | bytes 98308
  216.2 24.2 %copy-start.14 = (bf16[1,2048,352]{1,2,0:T(8,128)(2,1)S(1)}, bf16[1,2048,352]{1,2,0:T(8,128)(2,1)}, u32[]{:S(2)}) copy-start(bf16[1,2048,352]{1,2,0:T(8,128)(2,1)} %param.31) | copy-start | bytes 4325380
  239.3 1.1 copy-start.2
  250.3 4.5 %copy-start.7 = (s32[32,6]{1,0:T(8,128)S(1)}, s32[32,6]{1,0:T(8,128)}, u32[]{:S(2)}) copy-start(s32[32,6]{1,0:T(8,128)} %get-tuple-element.23) | copy-start | bytes 2308
  250.3 24.1 %all-to-all-start.6 = ((bf16[384,4,512]{2,0,1:T(8,128)(2,1)}), bf16[384,4,512]{2,0,1:T(8,128)(2,1)}, u32[]{:S(2)}, u32[]{:S(2)}) async-start(bf16[384,4,512]{2,0,1:T(8,128)(2,1)} %bitcast.106), calls=%async_computation.6 | async-start | bytes 3145728 | tf_op jit(solution)/shard_map/all_to_all | solution.py:56
  277.2 25.3 %all-to-all-start.7 = ((bf16[64,6,512]{2,1,0:T(8,128)(2,1)}), bf16[64,6,512]{2,1,0:T(8,128)(2,1)}, u32[]{:S(2)}, u32[]{:S(2)}) async-start(bf16[64,6,512]{2,1,0:T(8,128)(2,1)} %reshape.525), calls=%async_computation.7 | async-start | bytes 1048576 | tf_op jit(solution)/shard_map/all_to_all | solution.py:257

commit v5 on v4

--- a/solution.py
+++ b/solution.py
@@ -109,7 +109,20 @@
         ],
         axis=1,
     )
-    got_rows = lax.all_gather(send_rows, "head", axis=0, tiled=False)
+    gain_hi = lax.reduce_precision(ffn_gain, exponent_bits=8, mantissa_bits=7)
+    gain_rest = ffn_gain - gain_hi
+    gain_mid = lax.reduce_precision(gain_rest, exponent_bits=8, mantissa_bits=7)
+    gain_lo = gain_rest - gain_mid
+    gain_rows = jnp.zeros((8, send_rows.shape[1]), jnp.bfloat16)
+    gain_rows = gain_rows.at[:3, :quarter_width].set(
+        jnp.stack([gain_hi, gain_mid, gain_lo]).astype(jnp.bfloat16)
+    )
+    got_all = lax.all_gather(
+        jnp.concatenate([send_rows, gain_rows], axis=0), "head", axis=0, tiled=False
+    )
+    got_rows = got_all[:, :local_rows]
+    got_gain = got_all[:, local_rows : local_rows + 3, :quarter_width].astype(jnp.float32)
+    gain_full = ((got_gain[:, 0] + got_gain[:, 1]) + got_gain[:, 2]).reshape(-1)
     hidden_groups = got_rows[:, :, :quarter_width].astype(jnp.float32)
 
     def part_piece(k):
@@ -200,16 +213,18 @@
     attended = (hidden.astype(jnp.float32) + attn_piece).astype(jnp.bfloat16)
     attended_wide = attended.astype(jnp.float32)
     gained = (attended_wide * ffn_gain).astype(jnp.bfloat16)
-    squares, logit_part = lax.psum(
-        (
-            jnp.sum(attended_wide * attended_wide, axis=1),
-            jnp.dot(gained, w_router, preferred_element_type=jnp.float32),
+    stats = lax.psum(
+        jnp.concatenate(
+            [
+                jnp.sum(attended_wide * attended_wide, axis=1, keepdims=True),
+                jnp.dot(gained, w_router, preferred_element_type=jnp.float32),
+            ],
+            axis=1,
         ),
         "head",
     )
-    inv_ffn = lax.rsqrt(squares / D + NORM_EPS)
-    logits = logit_part * inv_ffn[:, None]
-    normed_ffn = (attended_wide * ffn_gain * inv_ffn[:, None]).astype(jnp.bfloat16)
+    inv_ffn = lax.rsqrt(stats[:, 0] / D + NORM_EPS)
+    logits = stats[:, 1:] * inv_ffn[:, None]
     expert_count = w_router.shape[1]
     route_count = routes.shape[1]
     expert_ids = jnp.arange(expert_count, dtype=jnp.int32)
@@ -228,7 +243,7 @@
         jnp.where(filled, row_ids[None, :, None], 0), axis=(1, 2)
     ) + local_rows * (1 - jnp.max(filled.astype(jnp.int32), axis=(1, 2)))
     padded_rows = jnp.concatenate(
-        [normed_ffn, jnp.zeros((1, normed_ffn.shape[1]), jnp.bfloat16)], axis=0
+        [attended, jnp.zeros((1, attended.shape[1]), jnp.bfloat16)], axis=0
     )
     arrived = lax.all_to_all(
         padded_rows[source_token].reshape(expert_count, capacity, quarter_width),
@@ -247,6 +262,9 @@
         concat_axis=2,
         tiled=True,
     ).reshape(peer_count * capacity, head_count * quarter_width)
+    expert_wide = expert_in.astype(jnp.float32)
+    expert_inv = lax.rsqrt(jnp.mean(expert_wide * expert_wide, axis=1, keepdims=True) + NORM_EPS)
+    expert_in = (expert_wide * gain_full * expert_inv).astype(jnp.bfloat16)
     gate_value = jnp.dot(expert_in, expert_gate[0], preferred_element_type=jnp.float32)
     up_value = jnp.dot(expert_in, expert_up[0], preferred_element_type=jnp.float32)
     activity = (jax.nn.silu(gate_value) * up_value).astype(jnp.bfloat16)

time: 311 us -> 311 us (level)
  blocking collectives: 87.3 us -> 74.2 us
  other arithmetic: 23 us -> 29.2 us
  starting transfers between devices: 43.4 us -> 49.5 us
    all_to_all x1 -> x0, blocking collectives: 23 us -> none  [body(): lax.all_to_all(jnp.broadcast_to(arrived.reshape(1, peer_count * capacity,...]
    all_to_all x0 -> x1, waiting for transfers between devices: none -> 19.8 us  [body(): lax.all_to_all(jnp.broadcast_to(arrived.reshape(1, peer_count * capacity,...]
    all_to_all x3, waiting for transfers between devices: 37.7 us -> 18.2 us  [head_sum_scatter(): lax.all_to_all(values, 'head', split_axis=axis, concat_axis=0, tiled=True)]
    psum x1, blocking collectives: 12.3 us -> 25.2 us  [body(): lax.psum(jnp.concatenate([jnp.sum(attended_wide * attended_wide, axis=1,...]
    all_to_all x0 -> x1, starting transfers between devices: none -> 4.33 us  [body(): lax.all_to_all(jnp.broadcast_to(arrived.reshape(1, peer_count * capacity,...]
    all_to_all x1, blocking collectives: 27.4 us -> 23.9 us  [body(): lax.all_to_all(padded_rows[source_token].reshape(expert_count, capacity,...]
  transfers between devices with their start and end apart: 6 -> 7, of which waited for: 6 -> 6; matrix products, arithmetic and copies ran while one was open for 3% -> 3% of each run, Pallas kernels for 0% -> 0%
where the time goes in v5:
time: 311 us; the launch traced here: 309 us
  waiting for transfers between devices  80.9 us (26%)
  blocking collectives  74.2 us (24%)
  local copies, waits for them, and re-layouts  51.6 us (17%)
  starting transfers between devices  49.5 us (16%)
  other arithmetic  29.2 us (9%)
  matrix products  22.8 us (7%)
    psum x1, blocking collectives, body(): lax.psum(jnp.concatenate([jnp.sum(attended_wide * attended_wide, axis=1,...  25.2 us
    all_to_all x1, blocking collectives, body(): lax.all_to_all(padded_rows[source_token].reshape(expert_count, capacity,...  23.9 us
    all_to_all x1, waiting for transfers between devices, body(): lax.all_to_all(jnp.broadcast_to(arrived.reshape(1, peer_count * capacity,...  19.8 us
    all_to_all x3, waiting for transfers between devices, head_sum_scatter(): lax.all_to_all(values, 'head', split_axis=axis, concat_axis=0, tiled=True)  18.2 us
    all_to_all x1, waiting for transfers between devices, body(): got_packed = lax.all_to_all(packed, 'tok', 0, 0, tiled=True)  17.3 us
    all_to_all x1, waiting for transfers between devices, body(): lax.all_to_all(expert_share.reshape(peer_count, capacity, quarter_width),...  16 us
    all_to_all x1, starting transfers between devices, body(): got_packed = lax.all_to_all(packed, 'tok', 0, 0, tiled=True)  14.1 us
    all_gather x1, blocking collectives, body(): lax.all_gather(jnp.concatenate([send_rows, gain_rows], axis=0), 'head', a...  12.9 us
  transfers between devices with their start and end apart: 7, of which 6 were waited for; matrix products, arithmetic and copies ran while one was open for 3% of the time, Pallas kernels for 0%

profile of v5, /device:TPU:1, one launch (start us, length us, event | category | flops | bytes accessed | tf_op | source)
XLA Modules:
  0.0 309.5 jit_solution(13623373031676293840)
XLA Ops:
  4.6 1.4 gather_fusion.3
  6.0 1.4 gather_fusion.2
  9.6 1.4 fusion.42
  11.2 12.9 %all-gather = bf16[160,2432]{1,0:T(8,128)(2,1)S(1)} all-gather(bf16[40,2432]{1,0:T(8,128)(2,1)S(1)} %pad_maximum_fusion.2), channel_id=2, replica_groups=mesh['tok'=64,'head'=4] {'head'}, dimensions={0}, use_global_device_ids=true | all-gather | bytes 972800 | tf_op jit(solution)/shard_map/all_gather | solution.py:120
  29.2 1.4 multiply_cosine_fusion
  32.2 1.2 fusion.19
  34.5 1.6 gather_fusion
  36.0 2.5 pad_maximum_fusion.1
  38.5 14.1 %all-to-all-start = ((bf16[64,6,576]{2,1,0:T(8,128)(2,1)}), bf16[64,6,576]{2,1,0:T(8,128)(2,1)}, u32[]{:S(2)}, u32[]{:S(2)}) async-start(bf16[64,6,576]{2,1,0:T(8,128)(2,1)} %pad_maximum_fusion.1), calls=%async_computation | async-start | bytes 1310720 | tf_op jit(solution)/shard_map/all_to_all | solution.py:177
  53.0 1.6 gather_fusion.11
  55.3 17.3 %all-to-all-done = bf16[64,6,576]{2,1,0:T(8,128)(2,1)} async-done(((bf16[64,6,576]{2,1,0:T(8,128)(2,1)}), bf16[64,6,576]{2,1,0:T(8,128)(2,1)}, u32[]{:S(2)}, u32[]{:S(2)}) %all-to-all-start) | async-done | bytes 442400 | tf_op jit(solution)/shard_map/all_to_all | solution.py:177
  75.0 1.9 copy.280
  76.9 2.1 gather_fusion.5
  79.1 12.2 %all_gather.11 = bf16[32,16,576]{2,0,1:T(8,128)(2,1)S(1)} all-gather(bf16[32,4,576]{2,0,1:T(8,128)(2,1)S(1)} %gather_fusion.5), channel_id=1, replica_groups=mesh['tok'=64,'head'=4] {'head'}, dimensions={1}, use_global_device_ids=true | all-gather | bytes 737280 | tf_op jit(solution)/shard_map/all_gather | solution.py:187
  92.0 1.4 copy.284
  93.5 4.5 %convert_reduce_fusion = (f32[512]{0:T(512)S(1)}, bf16[512,2496]{0,1:T(8,128)(2,1)}) fusion(pred[512,2496]{0,1:T(32,128)(4,1)S(1)} %copy.284, bf16[512,576]{1,0:T(8,128)(2,1)S(1)} %bitcast.126, bf16[2496,576]{0,1:T(8,128)(2,1)S(1)} %copy-done.16), kind=kOutput, calls=%fused_computation.13 | convolution fusion | flops 1478589952 | bytes 7301120 | tf_op jit(solution)/shard_map/qc,pc->qp/dot_general | solution.py:39
  98.2 4.4 %copy.282 = bf16[512,2496]{1,0:T(8,128)(2,1)} copy(bf16[512,2496]{0,1:T(8,128)(2,1)} %get-tuple-element.65) | data formatting | bytes 5111808 | tf_op jit(solution)/shard_map/exp | solution.py:46
  102.6 4.1 %fusion.3 = f32[32,16,512]{2,1,0:T(8,128)S(1)} fusion(bf16[32,16,2496]{2,1,0:T(8,128)(2,1)} %bitcast.118, bf16[2496,576]{0,1:T(8,128)(2,1)} %param.27, pred[32,2496]{1,0:T(8,128)(4,1)S(1)} %compare_and_fusion), kind=kOutput, calls=%fused_computation.22 | convolution fusion | flops 1309900800 | bytes 6371328 | tf_op jit(solution)/shard_map/khp,pl->khl/dot_general | solution.py:47
  106.8 1.5 copy.286
  108.3 4.4 %all-to-all-start.1 = ((f32[32,16,513]{2,0,1:T(8,128)}), f32[32,16,513]{2,0,1:T(8,128)}, u32[]{:S(2)}, u32[]{:S(2)}) async-start(f32[32,16,513]{2,0,1:T(8,128)} %copy.286), calls=%async_computation.1 | async-start | bytes 2621440 | tf_op jit(solution)/shard_map/all_to_all | solution.py:56
  113.4 1.8 gather_fusion.6
  116.2 12.2 %all-to-all-done.1 = f32[32,16,513]{2,0,1:T(8,128)} async-done(((f32[32,16,513]{2,0,1:T(8,128)}), f32[32,16,513]{2,0,1:T(8,128)}, u32[]{:S(2)}, u32[]{:S(2)}) %all-to-all-start.1) | async-done | bytes 1050656 | tf_op jit(solution)/shard_map/all_to_all | solution.py:56
  128.4 1.4 reduce_sum.150
  133.5 1.2 fusion.21
  137.3 8.8 %all-to-all-start.2 = ((bf16[64,2,256]{2,1,0:T(2,128)(2,1)}), bf16[64,2,256]{2,1,0:T(2,128)(2,1)S(1)}, u32[]{:S(2)}, u32[]{:S(2)}) async-start(bf16[64,2,256]{2,1,0:T(2,128)(2,1)} %reshape.718), calls=%async_computation.2 | async-start | bytes 131072 | tf_op jit(solution)/shard_map/all_to_all | solution.py:210
  146.3 9.5 %all-to-all-done.2 = bf16[64,2,256]{2,1,0:T(2,128)(2,1)S(1)} async-done(((bf16[64,2,256]{2,1,0:T(2,128)(2,1)}), bf16[64,2,256]{2,1,0:T(2,128)(2,1)S(1)}, u32[]{:S(2)}, u32[]{:S(2)}) %all-to-all-start.2) | async-done | bytes 65568 | tf_op jit(solution)/shard_map/all_to_all | solution.py:210
  156.6 2.1 fusion.87
  159.3 3.4 %all-to-all-start.3 = ((f32[32,4,512]{2,0,1:T(8,128)}), f32[32,4,512]{2,0,1:T(8,128)S(1)}, u32[]{:S(2)}, u32[]{:S(2)}) async-start(f32[32,4,512]{2,0,1:T(8,128)} %bitcast.125), calls=%async_computation.3 | async-start | bytes 524288 | tf_op jit(solution)/shard_map/all_to_all | solution.py:56
  162.8 6.0 %all-to-all-done.3 = f32[32,4,512]{2,0,1:T(8,128)S(1)} async-done(((f32[32,4,512]{2,0,1:T(8,128)}), f32[32,4,512]{2,0,1:T(8,128)S(1)}, u32[]{:S(2)}, u32[]{:S(2)}) %all-to-all-start.3) | async-done | bytes 262176 | tf_op jit(solution)/shard_map/all_to_all | solution.py:56
  169.6 2.6 gather_fusion.9
  172.1 1.9 reshape.603
  174.1 23.9 %all_to_all.74 = bf16[64,6,512]{2,1,0:T(8,128)(2,1)} all-to-all(bf16[64,6,512]{2,1,0:T(8,128)(2,1)} %reshape.603), channel_id=1, replica_groups=mesh['tok'=64,'head'=4] {'tok'}, dimensions={0} | all-to-all | bytes 786432 | tf_op jit(solution)/shard_map/all_to_all | solution.py:248
  200.1 2.3 broadcast_in_dim.164
  202.3 4.3 %all-to-all-start.5 = ((bf16[4,384,512]{1,2,0:T(8,128)(2,1)}), bf16[4,384,512]{1,2,0:T(8,128)(2,1)}, u32[]{:S(2)}, u32[]{:S(2)}) async-start(bf16[4,384,512]{1,2,0:T(8,128)(2,1)} %broadcast_in_dim.164), calls=%async_computation.5 | async-start | bytes 3145728 | tf_op jit(solution)/shard_map/all_to_all | solution.py:255
  207.5 19.8 %all-to-all-done.5 = bf16[4,384,512]{1,2,0:T(8,128)(2,1)} async-done(((bf16[4,384,512]{1,2,0:T(8,128)(2,1)}), bf16[4,384,512]{1,2,0:T(8,128)(2,1)}, u32[]{:S(2)}, u32[]{:S(2)}) %all-to-all-start.5) | async-done | bytes 1572896 | tf_op jit(solution)/shard_map/all_to_all | solution.py:255
  227.3 1.8 fusion.2
  229.1 2.0 fusion.1
  232.2 1.7 fusion.11
  233.9 5.5 %convolution_convert_fusion = bf16[384,2048]{1,0:T(8,128)(2,1)} fusion(bf16[1,352,2048]{2,1,0:T(8,128)(2,1)} %param.35, bf16[384,2048]{0,1:T(8,128)(2,1)} %bitcast.122, bf16[1,2048,352]{1,2,0:T(8,128)(2,1)} %param.34, f32[384,352]{0,1:T(8,128)} %fusion.11), kind=kOutput, calls=%fused_computation.21 | convolution fusion | flops 1108893696 | bytes 6569984 | tf_op jit(solution)/shard_map/dot_general | solution.py:272
  239.4 2.7 copy.341
  242.1 4.5 %all-to-all-start.6 = ((bf16[384,4,512]{2,0,1:T(8,128)(2,1)}), bf16[384,4,512]{2,0,1:T(8,128)(2,1)}, u32[]{:S(2)}, u32[]{:S(2)}) async-start(bf16[384,4,512]{2,0,1:T(8,128)(2,1)} %bitcast.112), calls=%async_computation.6 | async-start | bytes 3145728 | tf_op jit(solution)/shard_map/all_to_all | solution.py:56
  247.6 25.2 %psum.7 = f32[32,65]{1,0:T(8,128)S(1)} all-reduce(f32[32,65]{1,0:T(8,128)S(1)} %pad_maximum_fusion.5), channel_id=1, replica_groups=mesh['tok'=64,'head'=4] {'head'}, use_global_device_ids=true, to_apply=%region_12.13 | all-reduce | flops 2080 | bytes 16640 | tf_op jit(solution)/shard_map/psum | solution.py:216
  272.8 1.8 reduce_sum.157
  275.6 10.0 %all-to-all-start.7 = ((bf16[64,6,512]{2,1,0:T(8,128)(2,1)}), bf16[64,6,512]{2,1,0:T(8,128)(2,1)}, u32[]{:S(2)}, u32[]{:S(2)}) async-start(bf16[64,6,512]{2,1,0:T(8,128)(2,1)} %reshape.604), calls=%async_computation.7 | async-start | bytes 1048576 | tf_op jit(solution)/shard_map/all_to_all | solution.py:275
  286.8 16.0 %all-to-all-done.7 = bf16[64,6,512]{2,1,0:T(8,128)(2,1)} async-done(((bf16[64,6,512]{2,1,0:T(8,128)(2,1)}), bf16[64,6,512]{2,1,0:T(8,128)(2,1)}, u32[]{:S(2)}, u32[]{:S(2)}) %all-to-all-start.7) | async-done | bytes 393248 | tf_op jit(solution)/shard_map/all_to_all | solution.py:275
  304.0 1.8 gather_fusion.10
  305.8 1.8 reshape.701
  307.6 1.9 multiply_reduce_fusion
  (159 shorter events, 37.0 us)
Async XLA Ops:
  0.6 24.3 %copy-start = (bf16[2048,768]{1,0:T(8,128)(2,1)S(1)}, bf16[2048,768]{1,0:T(8,128)(2,1)}, u32[]{:S(2)}) copy-start(bf16[2048,768]{1,0:T(8,128)(2,1)} %param.22) | copy-start | bytes 9437188
  0.6 10.4 %copy-start.8 = (bf16[32,512]{1,0:T(8,128)(2,1)S(1)}, bf16[32,512]{1,0:T(8,128)(2,1)}, u32[]{:S(2)}) copy-start(bf16[32,512]{1,0:T(8,128)(2,1)} %param.20) | copy-start | bytes 98308
  24.1 0.9 copy-start.2
  25.0 4.2 %copy-start.15 = (f32[32]{0:T(128)S(1)}, f32[32]{0:T(128)}, u32[]{:S(2)}) copy-start(f32[32]{0:T(128)} %multiply_power_fusion) | copy-start | bytes 388
  30.7 5.4 %copy-start.1 = (bf16[32,576]{1,0:T(8,128)(2,1)}, bf16[32,576]{1,0:T(8,128)(2,1)S(1)}, u32[]{:S(2)}) copy-start(bf16[32,576]{1,0:T(8,128)(2,1)S(1)} %pad_maximum_fusion.4) | copy-start | bytes 110596
  34.5 18.1 %copy-start.12 = (s32[32,6]{0,1:T(8,128)S(1)}, s32[32,6]{0,1:T(8,128)}, u32[]{:S(2)}) copy-start(s32[32,6]{0,1:T(8,128)} %param.32) | copy-start | bytes 2308
  38.5 34.1 %all-to-all-start = ((bf16[64,6,576]{2,1,0:T(8,128)(2,1)}), bf16[64,6,576]{2,1,0:T(8,128)(2,1)}, u32[]{:S(2)}, u32[]{:S(2)}) async-start(bf16[64,6,576]{2,1,0:T(8,128)(2,1)} %pad_maximum_fusion.1), calls=%async_computation | async-start | bytes 1310720 | tf_op jit(solution)/shard_map/all_to_all | solution.py:177
  79.1 12.9 %copy-start.4 = (bf16[32,4,576]{2,0,1:T(8,128)(2,1)}, bf16[32,4,576]{2,0,1:T(8,128)(2,1)S(1)}, u32[]{:S(2)}) copy-start(bf16[32,4,576]{2,0,1:T(8,128)(2,1)S(1)} %gather_fusion.5) | copy-start | bytes 442372
  91.6 1.8 copy-start.16
  108.3 4.4 %copy-start.11 = (s32[32,6]{1,0:T(8,128)S(1)}, s32[32,6]{1,0:T(8,128)}, u32[]{:S(2)}) copy-start(s32[32,6]{1,0:T(8,128)} %reshape.694) | copy-start | bytes 2308
  108.3 6.8 %copy-start.5 = (bf16[32,4,576]{2,0,1:T(8,128)(2,1)S(1)}, bf16[32,4,576]{2,0,1:T(8,128)(2,1)}, u32[]{:S(2)}) copy-start(bf16[32,4,576]{2,0,1:T(8,128)(2,1)} %copy-done.4) | copy-start | bytes 442372
  108.3 20.1 %all-to-all-start.1 = ((f32[32,16,513]{2,0,1:T(8,128)}), f32[32,16,513]{2,0,1:T(8,128)}, u32[]{:S(2)}, u32[]{:S(2)}) async-start(f32[32,16,513]{2,0,1:T(8,128)} %copy.286), calls=%async_computation.1 | async-start | bytes 2621440 | tf_op jit(solution)/shard_map/all_to_all | solution.py:56
  129.8 16.3 %copy-start.14 = (s32[32]{0:T(128)S(1)}, s32[32]{0:T(128)}, u32[]{:S(2)}) copy-start(s32[32]{0:T(128)} %get-tuple-element.37) | copy-start | bytes 388
  137.3 18.6 %all-to-all-start.2 = ((bf16[64,2,256]{2,1,0:T(2,128)(2,1)}), bf16[64,2,256]{2,1,0:T(2,128)(2,1)S(1)}, u32[]{:S(2)}, u32[]{:S(2)}) async-start(bf16[64,2,256]{2,1,0:T(2,128)(2,1)} %reshape.718), calls=%async_computation.2 | async-start | bytes 131072 | tf_op jit(solution)/shard_map/all_to_all | solution.py:210
  159.3 9.5 %all-to-all-start.3 = ((f32[32,4,512]{2,0,1:T(8,128)}), f32[32,4,512]{2,0,1:T(8,128)S(1)}, u32[]{:S(2)}, u32[]{:S(2)}) async-start(f32[32,4,512]{2,0,1:T(8,128)} %bitcast.125), calls=%async_computation.3 | async-start | bytes 524288 | tf_op jit(solution)/shard_map/all_to_all | solution.py:56
  169.0 0.6 copy-start.6
  202.3 24.9 %all-to-all-start.5 = ((bf16[4,384,512]{1,2,0:T(8,128)(2,1)}), bf16[4,384,512]{1,2,0:T(8,128)(2,1)}, u32[]{:S(2)}, u32[]{:S(2)}) async-start(bf16[4,384,512]{1,2,0:T(8,128)(2,1)} %broadcast_in_dim.164), calls=%async_computation.5 | async-start | bytes 3145728 | tf_op jit(solution)/shard_map/all_to_all | solution.py:255
  229.1 3.1 %copy-start.17 = (bf16[1,2048,352]{1,2,0:T(8,128)(2,1)S(1)}, bf16[1,2048,352]{1,2,0:T(8,128)(2,1)}, u32[]{:S(2)}) copy-start(bf16[1,2048,352]{1,2,0:T(8,128)(2,1)} %param.33) | copy-start | bytes 4325380
  231.1 1.1 copy-start.3
  242.1 4.5 %copy-start.10 = (s32[32,6]{1,0:T(8,128)S(1)}, s32[32,6]{1,0:T(8,128)}, u32[]{:S(2)}) copy-start(s32[32,6]{1,0:T(8,128)} %get-tuple-element.35) | copy-start | bytes 2308
  242.1 5.3 %copy-start.7 = (bf16[32,512]{1,0:T(8,128)(2,1)S(1)}, bf16[32,512]{1,0:T(8,128)(2,1)}, u32[]{:S(2)}) copy-start(bf16[32,512]{1,0:T(8,128)(2,1)} %copy-done.6) | copy-start | bytes 98308
  242.1 5.3 %copy-start.9 = (bf16[512,64]{0,1:T(8,128)(2,1)S(1)}, bf16[512,64]{0,1:T(8,128)(2,1)}, u32[]{:S(2)}) copy-start(bf16[512,64]{0,1:T(8,128)(2,1)} %param.31) | copy-start | bytes 196612
  242.1 5.3 %copy-start.13 = (f32[512]{0:T(512)S(1)}, f32[512]{0:T(512)}, u32[]{:S(2)}) copy-start(f32[512]{0:T(512)} %param.30) | copy-start | bytes 6148
  242.1 30.7 %all-to-all-start.6 = ((bf16[384,4,512]{2,0,1:T(8,128)(2,1)}), bf16[384,4,512]{2,0,1:T(8,128)(2,1)}, u32[]{:S(2)}, u32[]{:S(2)}) async-start(bf16[384,4,512]{2,0,1:T(8,128)(2,1)} %bitcast.112), calls=%async_computation.6 | async-start | bytes 3145728 | tf_op jit(solution)/shard_map/all_to_all | solution.py:56
  275.6 27.2 %all-to-all-start.7 = ((bf16[64,6,512]{2,1,0:T(8,128)(2,1)}), bf16[64,6,512]{2,1,0:T(8,128)(2,1)}, u32[]{:S(2)}, u32[]{:S(2)}) async-start(bf16[64,6,512]{2,1,0:T(8,128)(2,1)} %reshape.604), calls=%async_computation.7 | async-start | bytes 1048576 | tf_op jit(solution)/shard_map/all_to_all | solution.py:275

commit v6 on v5

--- a/solution.py
+++ b/solution.py
@@ -114,8 +114,12 @@
     gain_mid = lax.reduce_precision(gain_rest, exponent_bits=8, mantissa_bits=7)
     gain_lo = gain_rest - gain_mid
     gain_rows = jnp.zeros((8, send_rows.shape[1]), jnp.bfloat16)
-    gain_rows = gain_rows.at[:3, :quarter_width].set(
-        jnp.stack([gain_hi, gain_mid, gain_lo]).astype(jnp.bfloat16)
+    router_column = lax.dynamic_index_in_dim(w_router, tok_index, axis=1, keepdims=False)
+    gain_rows = gain_rows.at[:4, :quarter_width].set(
+        jnp.concatenate(
+            [jnp.stack([gain_hi, gain_mid, gain_lo]).astype(jnp.bfloat16), router_column[None]],
+            axis=0,
+        )
     )
     got_all = lax.all_gather(
         jnp.concatenate([send_rows, gain_rows], axis=0), "head", axis=0, tiled=False
@@ -123,6 +127,7 @@
     got_rows = got_all[:, :local_rows]
     got_gain = got_all[:, local_rows : local_rows + 3, :quarter_width].astype(jnp.float32)
     gain_full = ((got_gain[:, 0] + got_gain[:, 1]) + got_gain[:, 2]).reshape(-1)
+    expert_column = got_all[:, local_rows + 3, :quarter_width].reshape(-1)
     hidden_groups = got_rows[:, :, :quarter_width].astype(jnp.float32)
 
     def part_piece(k):
@@ -212,26 +217,10 @@
     attn_piece = head_sum_scatter(jnp.dot(head_out, w_out, preferred_element_type=jnp.float32), 1)
     attended = (hidden.astype(jnp.float32) + attn_piece).astype(jnp.bfloat16)
     attended_wide = attended.astype(jnp.float32)
-    gained = (attended_wide * ffn_gain).astype(jnp.bfloat16)
-    stats = lax.psum(
-        jnp.concatenate(
-            [
-                jnp.sum(attended_wide * attended_wide, axis=1, keepdims=True),
-                jnp.dot(gained, w_router, preferred_element_type=jnp.float32),
-            ],
-            axis=1,
-        ),
-        "head",
-    )
-    inv_ffn = lax.rsqrt(stats[:, 0] / D + NORM_EPS)
-    logits = stats[:, 1:] * inv_ffn[:, None]
     expert_count = w_router.shape[1]
     route_count = routes.shape[1]
     expert_ids = jnp.arange(expert_count, dtype=jnp.int32)
     named = routes[:, :, None] == expert_ids[None, None, :]
-    picked = jnp.sum(jnp.where(named, logits[:, None, :], 0.0), axis=2)
-    lifted = jnp.exp(picked)
-    route_weight = lifted / jnp.sum(lifted, axis=1, keepdims=True)
     struck = jnp.max(named.astype(jnp.int32), axis=1)
     earlier_hits = jnp.cumsum(struck, axis=0) - struck
     capacity = min(local_rows, max(2, 2 * local_rows * route_count // expert_count))
@@ -264,6 +253,11 @@
     ).reshape(peer_count * capacity, head_count * quarter_width)
     expert_wide = expert_in.astype(jnp.float32)
     expert_inv = lax.rsqrt(jnp.mean(expert_wide * expert_wide, axis=1, keepdims=True) + NORM_EPS)
+    expert_gained = (expert_wide * gain_full).astype(jnp.bfloat16)
+    expert_logit = (
+        jnp.dot(expert_gained, expert_column, preferred_element_type=jnp.float32)
+        * expert_inv[:, 0]
+    )
     expert_in = (expert_wide * gain_full * expert_inv).astype(jnp.bfloat16)
     gate_value = jnp.dot(expert_in, expert_gate[0], preferred_element_type=jnp.float32)
     up_value = jnp.dot(expert_in, expert_up[0], preferred_element_type=jnp.float32)
@@ -272,14 +266,30 @@
         jnp.dot(activity, expert_down[0], preferred_element_type=jnp.float32).astype(jnp.bfloat16),
         1,
     ).astype(jnp.bfloat16)
+    logit_hi = lax.reduce_precision(expert_logit, exponent_bits=8, mantissa_bits=7)
+    logit_rest = expert_logit - logit_hi
+    logit_mid = lax.reduce_precision(logit_rest, exponent_bits=8, mantissa_bits=7)
+    logit_lo = logit_rest - logit_mid
+    logit_code = jnp.stack([logit_hi, logit_mid, logit_lo], axis=1).reshape(
+        peer_count, capacity * 3
+    )
+    logit_row = jnp.zeros((peer_count, 1, quarter_width), jnp.float32)
+    logit_row = logit_row.at[:, 0, : capacity * 3].set(logit_code).astype(jnp.bfloat16)
     returned = lax.all_to_all(
-        expert_share.reshape(peer_count, capacity, quarter_width),
+        jnp.concatenate(
+            [expert_share.reshape(peer_count, capacity, quarter_width), logit_row], axis=1
+        ),
         "tok",
         split_axis=0,
         concat_axis=0,
         tiled=True,
     )
-    chosen_rows = returned.reshape(slot_total, quarter_width)[route_place]
+    chosen_rows = returned[:, :capacity].reshape(slot_total, quarter_width)[route_place]
+    got_logit = returned[:, capacity, : capacity * 3].reshape(slot_total, 3).astype(jnp.float32)
+    slot_logit = (got_logit[:, 0] + got_logit[:, 1]) + got_logit[:, 2]
+    picked = slot_logit[route_place]
+    lifted = jnp.exp(picked)
+    route_weight = lifted / jnp.sum(lifted, axis=1, keepdims=True)
     expert_mix = jnp.sum(route_weight[:, :, None] * chosen_rows.astype(jnp.float32), axis=1).astype(
         jnp.bfloat16
     )

time: 311 us -> 310 us (level)
  blocking collectives: 74.2 us -> 49 us
  waiting for transfers between devices: 80.9 us -> 98.1 us
  other arithmetic: 29.2 us -> 32.7 us
  local copies, waits for them, and re-layouts: 51.6 us -> 54.9 us
    psum x1 -> x0, blocking collectives: 25.2 us -> none  [body(): lax.psum(jnp.concatenate([jnp.sum(attended_wide * attended_wide, axis=1,...]
    all_to_all x3, waiting for transfers between devices: 18.2 us -> 34.4 us  [head_sum_scatter(): lax.all_to_all(values, 'head', split_axis=axis, concat_axis=0, tiled=True)]
  transfers between devices with their start and end apart: 7 -> 7, of which waited for: 6 -> 7; matrix products, arithmetic and copies ran while one was open for 3% -> 3% of each run, Pallas kernels for 0% -> 0%
where the time goes in v6:
time: 310 us; the launch traced here: 308 us
  waiting for transfers between devices  98.1 us (32%)
  local copies, waits for them, and re-layouts  54.9 us (18%)
  blocking collectives  49 us (16%)
  starting transfers between devices  47.4 us (15%)
  other arithmetic  32.7 us (11%)
  matrix products  24.4 us (8%)
    all_to_all x3, waiting for transfers between devices, head_sum_scatter(): lax.all_to_all(values, 'head', split_axis=axis, concat_axis=0, tiled=True)  34.4 us
    all_to_all x1, blocking collectives, body(): lax.all_to_all(padded_rows[source_token].reshape(expert_count, capacity,...  23.9 us
    all_to_all x1, waiting for transfers between devices, body(): lax.all_to_all(jnp.broadcast_to(arrived.reshape(1, peer_count * capacity,...  19.8 us
    all_to_all x1, waiting for transfers between devices, body(): got_packed = lax.all_to_all(packed, 'tok', 0, 0, tiled=True)  17.3 us
    all_to_all x1, waiting for transfers between devices, body(): lax.all_to_all(jnp.concatenate([expert_share.reshape(peer_count, capacity...  17.1 us
    all_to_all x1, starting transfers between devices, body(): got_packed = lax.all_to_all(packed, 'tok', 0, 0, tiled=True)  14.1 us
    all_gather x1, blocking collectives, body(): lax.all_gather(jnp.concatenate([send_rows, gain_rows], axis=0), 'head', a...  12.9 us
    all_gather x1, blocking collectives, body(): all_heads = lax.all_gather(owner_probes, 'head', axis=1, tiled=True)  12.2 us
  transfers between devices with their start and end apart: 7, of which 7 were waited for; matrix products, arithmetic and copies ran while one was open for 3% of the time, Pallas kernels for 0%

profile of v6, /device:TPU:1, one launch (start us, length us, event | category | flops | bytes accessed | tf_op | source)
XLA Modules:
  0.0 307.8 jit_solution(6608472102722035242)
XLA Ops:
  4.6 1.4 gather_fusion.3
  6.0 1.4 gather_fusion.2
  11.9 12.9 %all-gather = bf16[160,2432]{1,0:T(8,128)(2,1)S(1)} all-gather(bf16[40,2432]{1,0:T(8,128)(2,1)S(1)} %pad_maximum_fusion.2), channel_id=2, replica_groups=mesh['tok'=64,'head'=4] {'head'}, dimensions={0}, use_global_device_ids=true | all-gather | bytes 972800 | tf_op jit(solution)/shard_map/all_gather | solution.py:124
  29.9 1.4 multiply_cosine_fusion
  35.2 1.6 gather_fusion
  36.8 2.5 pad_maximum_fusion.1
  39.2 14.1 %all-to-all-start = ((bf16[64,6,576]{2,1,0:T(8,128)(2,1)}), bf16[64,6,576]{2,1,0:T(8,128)(2,1)}, u32[]{:S(2)}, u32[]{:S(2)}) async-start(bf16[64,6,576]{2,1,0:T(8,128)(2,1)} %pad_maximum_fusion.1), calls=%async_computation | async-start | bytes 1310720 | tf_op jit(solution)/shard_map/all_to_all | solution.py:182
  53.7 1.6 gather_fusion.12
  56.0 17.3 %all-to-all-done = bf16[64,6,576]{2,1,0:T(8,128)(2,1)} async-done(((bf16[64,6,576]{2,1,0:T(8,128)(2,1)}), bf16[64,6,576]{2,1,0:T(8,128)(2,1)}, u32[]{:S(2)}, u32[]{:S(2)}) %all-to-all-start) | async-done | bytes 442400 | tf_op jit(solution)/shard_map/all_to_all | solution.py:182
  75.7 1.9 copy.288
  77.6 2.1 gather_fusion.5
  79.8 12.2 %all_gather.11 = bf16[32,16,576]{2,0,1:T(8,128)(2,1)S(1)} all-gather(bf16[32,4,576]{2,0,1:T(8,128)(2,1)S(1)} %gather_fusion.5), channel_id=1, replica_groups=mesh['tok'=64,'head'=4] {'head'}, dimensions={1}, use_global_device_ids=true | all-gather | bytes 737280 | tf_op jit(solution)/shard_map/all_gather | solution.py:192
  92.7 1.4 copy.292
  94.2 4.5 %convert_reduce_fusion = (f32[512]{0:T(512)S(1)}, bf16[512,2496]{0,1:T(8,128)(2,1)}) fusion(pred[512,2496]{0,1:T(32,128)(4,1)S(1)} %copy.292, bf16[512,576]{1,0:T(8,128)(2,1)S(1)} %bitcast.136, bf16[2496,576]{0,1:T(8,128)(2,1)S(1)} %copy-done.13), kind=kOutput, calls=%fused_computation.14 | convolution fusion | flops 1478589952 | bytes 7301120 | tf_op jit(solution)/shard_map/qc,pc->qp/dot_general | solution.py:39
  98.9 4.4 %copy.290 = bf16[512,2496]{1,0:T(8,128)(2,1)} copy(bf16[512,2496]{0,1:T(8,128)(2,1)} %get-tuple-element.80) | data formatting | bytes 5111808 | tf_op jit(solution)/shard_map/exp | solution.py:46
  103.3 4.1 %fusion.4 = f32[32,16,512]{2,1,0:T(8,128)S(1)} fusion(bf16[32,16,2496]{2,1,0:T(8,128)(2,1)} %bitcast.128, bf16[2496,576]{0,1:T(8,128)(2,1)} %param.29, pred[32,2496]{1,0:T(8,128)(4,1)S(1)} %compare_and_fusion), kind=kOutput, calls=%fused_computation.24 | convolution fusion | flops 1309900800 | bytes 6371328 | tf_op jit(solution)/shard_map/khp,pl->khl/dot_general | solution.py:47
  107.5 1.5 copy.294
  109.0 4.4 %all-to-all-start.1 = ((f32[32,16,513]{2,0,1:T(8,128)}), f32[32,16,513]{2,0,1:T(8,128)}, u32[]{:S(2)}, u32[]{:S(2)}) async-start(f32[32,16,513]{2,0,1:T(8,128)} %copy.294), calls=%async_computation.1 | async-start | bytes 2621440 | tf_op jit(solution)/shard_map/all_to_all | solution.py:56
  114.1 1.8 gather_fusion.6
  116.9 12.2 %all-to-all-done.1 = f32[32,16,513]{2,0,1:T(8,128)} async-done(((f32[32,16,513]{2,0,1:T(8,128)}), f32[32,16,513]{2,0,1:T(8,128)}, u32[]{:S(2)}, u32[]{:S(2)}) %all-to-all-start.1) | async-done | bytes 1050656 | tf_op jit(solution)/shard_map/all_to_all | solution.py:56
  129.1 1.4 reduce_sum.132
  138.0 8.8 %all-to-all-start.2 = ((bf16[64,2,256]{2,1,0:T(2,128)(2,1)}), bf16[64,2,256]{2,1,0:T(2,128)(2,1)S(1)}, u32[]{:S(2)}, u32[]{:S(2)}) async-start(bf16[64,2,256]{2,1,0:T(2,128)(2,1)} %reshape.793), calls=%async_computation.2 | async-start | bytes 131072 | tf_op jit(solution)/shard_map/all_to_all | solution.py:215
  147.0 9.5 %all-to-all-done.2 = bf16[64,2,256]{2,1,0:T(2,128)(2,1)S(1)} async-done(((bf16[64,2,256]{2,1,0:T(2,128)(2,1)}), bf16[64,2,256]{2,1,0:T(2,128)(2,1)S(1)}, u32[]{:S(2)}, u32[]{:S(2)}) %all-to-all-start.2) | async-done | bytes 65568 | tf_op jit(solution)/shard_map/all_to_all | solution.py:215
  157.3 2.1 fusion.87
  160.1 3.4 %all-to-all-start.3 = ((f32[32,4,512]{2,0,1:T(8,128)}), f32[32,4,512]{2,0,1:T(8,128)S(1)}, u32[]{:S(2)}, u32[]{:S(2)}) async-start(f32[32,4,512]{2,0,1:T(8,128)} %bitcast.135), calls=%async_computation.3 | async-start | bytes 524288 | tf_op jit(solution)/shard_map/all_to_all | solution.py:56
  163.5 6.0 %all-to-all-done.3 = f32[32,4,512]{2,0,1:T(8,128)S(1)} async-done(((f32[32,4,512]{2,0,1:T(8,128)}), f32[32,4,512]{2,0,1:T(8,128)S(1)}, u32[]{:S(2)}, u32[]{:S(2)}) %all-to-all-start.3) | async-done | bytes 262176 | tf_op jit(solution)/shard_map/all_to_all | solution.py:56
  169.6 2.6 gather_fusion.9
  172.2 1.9 reshape.653
  174.1 23.9 %all_to_all.74 = bf16[64,6,512]{2,1,0:T(8,128)(2,1)} all-to-all(bf16[64,6,512]{2,1,0:T(8,128)(2,1)} %reshape.653), channel_id=1, replica_groups=mesh['tok'=64,'head'=4] {'tok'}, dimensions={0} | all-to-all | bytes 786432 | tf_op jit(solution)/shard_map/all_to_all | solution.py:237
  200.1 2.3 broadcast_in_dim.149
  202.4 4.3 %all-to-all-start.5 = ((bf16[4,384,512]{1,2,0:T(8,128)(2,1)}), bf16[4,384,512]{1,2,0:T(8,128)(2,1)}, u32[]{:S(2)}, u32[]{:S(2)}) async-start(bf16[4,384,512]{1,2,0:T(8,128)(2,1)} %broadcast_in_dim.149), calls=%async_computation.5 | async-start | bytes 3145728 | tf_op jit(solution)/shard_map/all_to_all | solution.py:244
  207.5 19.8 %all-to-all-done.5 = bf16[4,384,512]{1,2,0:T(8,128)(2,1)} async-done(((bf16[4,384,512]{1,2,0:T(8,128)(2,1)}), bf16[4,384,512]{1,2,0:T(8,128)(2,1)}, u32[]{:S(2)}, u32[]{:S(2)}) %all-to-all-start.5) | async-done | bytes 1572896 | tf_op jit(solution)/shard_map/all_to_all | solution.py:244
  227.3 1.8 fusion.3
  229.1 3.2 %fusion.2 = (bf16[4,1,384,512]{2,3,0,1:T(8,128)(2,1)S(1)}, bf16[4,1,384,512]{2,3,0,1:T(8,128)(2,1)}) fusion(bf16[4,384,512]{1,2,0:T(8,128)(2,1)} %all-to-all-done.5, f32[384]{0:T(512)S(1)} %add_rsqrt_fusion, f32[4,512]{1,0:T(4,128)S(1)} %bitcast.141), kind=kLoop, calls=%fused_computation.21 | loop fusion | flops 3932160 | bytes 4728320 | tf_op jit(solution)/shard_map/convert_element_type | solution.py:261
  233.5 1.7 fusion.12
  235.2 5.4 %convolution_convert_fusion = bf16[384,2048]{1,0:T(8,128)(2,1)} fusion(bf16[1,352,2048]{2,1,0:T(8,128)(2,1)} %param.37, bf16[384,2048]{0,1:T(8,128)(2,1)} %bitcast.132, bf16[1,2048,352]{1,2,0:T(8,128)(2,1)} %param.36, f32[384,352]{0,1:T(8,128)} %fusion.12), kind=kOutput, calls=%fused_computation.23 | convolution fusion | flops 1108893696 | bytes 6569984 | tf_op jit(solution)/shard_map/dot_general | solution.py:266
  240.6 2.7 copy.351
  243.3 4.3 %all-to-all-start.6 = ((bf16[384,4,512]{2,0,1:T(8,128)(2,1)}), bf16[384,4,512]{2,0,1:T(8,128)(2,1)}, u32[]{:S(2)}, u32[]{:S(2)}) async-start(bf16[384,4,512]{2,0,1:T(8,128)(2,1)} %bitcast.120), calls=%async_computation.6 | async-start | bytes 3145728 | tf_op jit(solution)/shard_map/all_to_all | solution.py:56
  248.5 1.7 convolution_reduce_fusion
  251.2 16.2 %all-to-all-done.6 = bf16[384,4,512]{2,0,1:T(8,128)(2,1)} async-done(((bf16[384,4,512]{2,0,1:T(8,128)(2,1)}), bf16[384,4,512]{2,0,1:T(8,128)(2,1)}, u32[]{:S(2)}, u32[]{:S(2)}) %all-to-all-start.6) | async-done | bytes 1572896 | tf_op jit(solution)/shard_map/all_to_all | solution.py:56
  267.4 1.8 reduce_sum.136
  270.1 2.0 fusion.31
  272.2 8.0 %all-to-all-start.7 = ((bf16[64,7,512]{2,1,0:T(8,128)(2,1)}), bf16[64,7,512]{2,1,0:T(8,128)(2,1)}, u32[]{:S(2)}, u32[]{:S(2)}) async-start(bf16[64,7,512]{2,1,0:T(8,128)(2,1)} %fusion.31), calls=%async_computation.7 | async-start | bytes 1048576 | tf_op jit(solution)/shard_map/all_to_all | solution.py:278
  280.3 17.1 %all-to-all-done.7 = bf16[64,7,512]{2,1,0:T(8,128)(2,1)} async-done(((bf16[64,7,512]{2,1,0:T(8,128)(2,1)}), bf16[64,7,512]{2,1,0:T(8,128)(2,1)}, u32[]{:S(2)}, u32[]{:S(2)}) %all-to-all-start.7) | async-done | bytes 458784 | tf_op jit(solution)/shard_map/all_to_all | solution.py:278
  298.8 1.6 gather_fusion.10
  302.5 1.7 gather_fusion.11
  304.2 1.8 reshape.764
  305.9 1.9 multiply_reduce_fusion
  (162 shorter events, 42.7 us)
Async XLA Ops:
  0.6 25.1 %copy-start = (bf16[2048,768]{1,0:T(8,128)(2,1)S(1)}, bf16[2048,768]{1,0:T(8,128)(2,1)}, u32[]{:S(2)}) copy-start(bf16[2048,768]{1,0:T(8,128)(2,1)} %param.24) | copy-start | bytes 9437188
  0.6 11.1 %copy-start.6 = (bf16[32,512]{1,0:T(8,128)(2,1)S(1)}, bf16[32,512]{1,0:T(8,128)(2,1)}, u32[]{:S(2)}) copy-start(bf16[32,512]{1,0:T(8,128)(2,1)} %param.22) | copy-start | bytes 98308
  24.8 0.9 copy-start.2
  25.7 4.2 %copy-start.12 = (f32[32]{0:T(128)S(1)}, f32[32]{0:T(128)}, u32[]{:S(2)}) copy-start(f32[32]{0:T(128)} %multiply_power_fusion) | copy-start | bytes 388
  31.4 5.4 %copy-start.1 = (bf16[32,576]{1,0:T(8,128)(2,1)}, bf16[32,576]{1,0:T(8,128)(2,1)S(1)}, u32[]{:S(2)}) copy-start(bf16[32,576]{1,0:T(8,128)(2,1)S(1)} %pad_maximum_fusion.4) | copy-start | bytes 110596
  35.2 18.1 %copy-start.10 = (s32[32,6]{0,1:T(8,128)S(1)}, s32[32,6]{0,1:T(8,128)}, u32[]{:S(2)}) copy-start(s32[32,6]{0,1:T(8,128)} %param.34) | copy-start | bytes 2308
  39.2 34.1 %all-to-all-start = ((bf16[64,6,576]{2,1,0:T(8,128)(2,1)}), bf16[64,6,576]{2,1,0:T(8,128)(2,1)}, u32[]{:S(2)}, u32[]{:S(2)}) async-start(bf16[64,6,576]{2,1,0:T(8,128)(2,1)} %pad_maximum_fusion.1), calls=%async_computation | async-start | bytes 1310720 | tf_op jit(solution)/shard_map/all_to_all | solution.py:182
  79.8 12.9 %copy-start.4 = (bf16[32,4,576]{2,0,1:T(8,128)(2,1)}, bf16[32,4,576]{2,0,1:T(8,128)(2,1)S(1)}, u32[]{:S(2)}) copy-start(bf16[32,4,576]{2,0,1:T(8,128)(2,1)S(1)} %gather_fusion.5) | copy-start | bytes 442372
  92.4 1.8 copy-start.13
  109.0 4.4 %copy-start.9 = (s32[32,6]{1,0:T(8,128)S(1)}, s32[32,6]{1,0:T(8,128)}, u32[]{:S(2)}) copy-start(s32[32,6]{1,0:T(8,128)} %reshape.754) | copy-start | bytes 2308
  109.0 6.8 %copy-start.5 = (bf16[32,4,576]{2,0,1:T(8,128)(2,1)S(1)}, bf16[32,4,576]{2,0,1:T(8,128)(2,1)}, u32[]{:S(2)}) copy-start(bf16[32,4,576]{2,0,1:T(8,128)(2,1)} %copy-done.4) | copy-start | bytes 442372
  109.0 20.1 %all-to-all-start.1 = ((f32[32,16,513]{2,0,1:T(8,128)}), f32[32,16,513]{2,0,1:T(8,128)}, u32[]{:S(2)}, u32[]{:S(2)}) async-start(f32[32,16,513]{2,0,1:T(8,128)} %copy.294), calls=%async_computation.1 | async-start | bytes 2621440 | tf_op jit(solution)/shard_map/all_to_all | solution.py:56
  130.5 16.3 %copy-start.11 = (s32[32]{0:T(128)S(1)}, s32[32]{0:T(128)}, u32[]{:S(2)}) copy-start(s32[32]{0:T(128)} %get-tuple-element.47) | copy-start | bytes 388
  138.0 18.6 %all-to-all-start.2 = ((bf16[64,2,256]{2,1,0:T(2,128)(2,1)}), bf16[64,2,256]{2,1,0:T(2,128)(2,1)S(1)}, u32[]{:S(2)}, u32[]{:S(2)}) async-start(bf16[64,2,256]{2,1,0:T(2,128)(2,1)} %reshape.793), calls=%async_computation.2 | async-start | bytes 131072 | tf_op jit(solution)/shard_map/all_to_all | solution.py:215
  160.1 9.5 %all-to-all-start.3 = ((f32[32,4,512]{2,0,1:T(8,128)}), f32[32,4,512]{2,0,1:T(8,128)S(1)}, u32[]{:S(2)}, u32[]{:S(2)}) async-start(f32[32,4,512]{2,0,1:T(8,128)} %bitcast.135), calls=%async_computation.3 | async-start | bytes 524288 | tf_op jit(solution)/shard_map/all_to_all | solution.py:56
  169.6 2.6 copy-start.7
  202.4 24.9 %all-to-all-start.5 = ((bf16[4,384,512]{1,2,0:T(8,128)(2,1)}), bf16[4,384,512]{1,2,0:T(8,128)(2,1)}, u32[]{:S(2)}, u32[]{:S(2)}) async-start(bf16[4,384,512]{1,2,0:T(8,128)(2,1)} %broadcast_in_dim.149), calls=%async_computation.5 | async-start | bytes 3145728 | tf_op jit(solution)/shard_map/all_to_all | solution.py:244
  229.1 4.3 %copy-start.14 = (bf16[1,2048,352]{1,2,0:T(8,128)(2,1)S(1)}, bf16[1,2048,352]{1,2,0:T(8,128)(2,1)}, u32[]{:S(2)}) copy-start(bf16[1,2048,352]{1,2,0:T(8,128)(2,1)} %param.35) | copy-start | bytes 4325380
  232.3 1.1 copy-start.3
  243.3 24.1 %all-to-all-start.6 = ((bf16[384,4,512]{2,0,1:T(8,128)(2,1)}), bf16[384,4,512]{2,0,1:T(8,128)(2,1)}, u32[]{:S(2)}, u32[]{:S(2)}) async-start(bf16[384,4,512]{2,0,1:T(8,128)(2,1)} %bitcast.120), calls=%async_computation.6 | async-start | bytes 3145728 | tf_op jit(solution)/shard_map/all_to_all | solution.py:56
  269.2 11.0 %copy-start.8 = (s32[32,6]{1,0:T(8,128)S(1)}, s32[32,6]{1,0:T(8,128)}, u32[]{:S(2)}) copy-start(s32[32,6]{1,0:T(8,128)} %get-tuple-element.45) | copy-start | bytes 2308
  272.2 25.2 %all-to-all-start.7 = ((bf16[64,7,512]{2,1,0:T(8,128)(2,1)}), bf16[64,7,512]{2,1,0:T(8,128)(2,1)}, u32[]{:S(2)}, u32[]{:S(2)}) async-start(bf16[64,7,512]{2,1,0:T(8,128)(2,1)} %fusion.31), calls=%async_computation.7 | async-start | bytes 1048576 | tf_op jit(solution)/shard_map/all_to_all | solution.py:278

commit v7 on v6

--- a/solution.py
+++ b/solution.py
@@ -26,10 +26,8 @@
     )
 
 
-def owner_attend(all_heads, owner_lengths, latent_cache, head_index, factor):
-    slot_rows = all_heads.shape[0]
-    total_heads = all_heads.shape[1]
-    probe_width = all_heads.shape[2]
+def owner_attend(grouped_heads, owner_lengths, latent_cache, head_index, factor):
+    groups, slot_rows, group_heads, probe_width = grouped_heads.shape
     key_rows = latent_cache.shape[0]
     starts = jnp.cumsum(owner_lengths) - owner_lengths
     places = head_index * key_rows + jnp.arange(key_rows, dtype=jnp.int32)
@@ -38,23 +36,24 @@
     )
     scores = factor * jnp.einsum(
         "qc,pc->qp",
-        all_heads.reshape(slot_rows * total_heads, probe_width),
+        grouped_heads.reshape(-1, probe_width),
         latent_cache,
         preferred_element_type=jnp.float32,
     )
-    scores = scores.reshape(slot_rows, total_heads, key_rows)
-    weights = jnp.where(inside[:, None, :], jnp.exp(scores), 0.0).astype(jnp.bfloat16)
+    scores = scores.reshape(groups, slot_rows, group_heads, key_rows)
+    weights = jnp.where(inside[None, :, None, :], jnp.exp(scores), 0.0).astype(jnp.bfloat16)
     numerator = jnp.einsum(
-        "khp,pl->khl", weights, latent_cache[:, :LATENT], preferred_element_type=jnp.float32
-    )
-    denominator = jnp.sum(weights.astype(jnp.float32), axis=2)
+        "qp,pl->ql",
+        weights.reshape(-1, key_rows),
+        latent_cache[:, :LATENT],
+        preferred_element_type=jnp.float32,
+    ).reshape(groups, slot_rows, group_heads, LATENT)
+    denominator = jnp.sum(weights.astype(jnp.float32), axis=3)
     return (numerator, denominator)
 
 
-def head_sum_scatter(values, axis):
-    groups = lax.axis_size("head")
-    moved = lax.all_to_all(values, "head", split_axis=axis, concat_axis=0, tiled=True)
-    moved = moved.reshape((groups, values.shape[0]) + moved.shape[1:])
+def head_sum_scatter(grouped):
+    moved = lax.all_to_all(grouped, "head", split_axis=0, concat_axis=0, tiled=True)
     return jnp.sum(moved.astype(jnp.float32), axis=0)
 
 
@@ -189,11 +188,11 @@
     owner_probes = got_packed[src_of_slot, :local_heads]
     owner_lengths = got_len[src_of_slot]
     owner_new = got_packed[src_of_slot, local_heads]
-    all_heads = lax.all_gather(owner_probes, "head", axis=1, tiled=True)
+    all_heads = lax.all_gather(owner_probes, "head", axis=0, tiled=False)
     numerator, denominator = owner_attend(
         all_heads, owner_lengths, latent_cache, head_index, factor
     )
-    joined = head_sum_scatter(jnp.concatenate([numerator, denominator[:, :, None]], axis=2), 1)
+    joined = head_sum_scatter(jnp.concatenate([numerator, denominator[..., None]], axis=3))
     self_score = factor * jnp.einsum(
         "bhc,bc->bh", owner_probes, owner_new, preferred_element_type=jnp.float32
     )
@@ -214,7 +213,14 @@
     back_row = jnp.where(back_valid, local_slot, local_rows)
     head_out = lax.all_to_all(owner_out[back_row], "tok", 0, 0, tiled=True)[dest_owner]
     head_out = head_out.reshape(local_rows, local_heads * NOPE)
-    attn_piece = head_sum_scatter(jnp.dot(head_out, w_out, preferred_element_type=jnp.float32), 1)
+    attn_piece = head_sum_scatter(
+        jnp.einsum(
+            "bk,kgf->gbf",
+            head_out,
+            w_out.reshape(w_out.shape[0], head_count, quarter_width),
+            preferred_element_type=jnp.float32,
+        )
+    )
     attended = (hidden.astype(jnp.float32) + attn_piece).astype(jnp.bfloat16)
     attended_wide = attended.astype(jnp.float32)
     expert_count = w_router.shape[1]
@@ -263,8 +269,12 @@
     up_value = jnp.dot(expert_in, expert_up[0], preferred_element_type=jnp.float32)
     activity = (jax.nn.silu(gate_value) * up_value).astype(jnp.bfloat16)
     expert_share = head_sum_scatter(
-        jnp.dot(activity, expert_down[0], preferred_element_type=jnp.float32).astype(jnp.bfloat16),
-        1,
+        jnp.einsum(
+            "rk,kgf->grf",
+            activity,
+            expert_down[0].reshape(expert_down.shape[1], head_count, quarter_width),
+            preferred_element_type=jnp.float32,
+        ).astype(jnp.bfloat16)
     ).astype(jnp.bfloat16)
     logit_hi = lax.reduce_precision(expert_logit, exponent_bits=8, mantissa_bits=7)
     logit_rest = expert_logit - logit_hi

time: 310 us -> 324 us (1.045)
  local copies, waits for them, and re-layouts: 54.9 us -> 71.2 us
  waiting for transfers between devices: 98.1 us -> 93.2 us
  matrix products: 24.4 us -> 28.5 us
    broadcast_in_dim x3 -> x5, local copies, waits for them, and re-layouts: 1.95 us -> 10.9 us  [the longest x3 9.78 us: owner_attend(): jnp.where(inside[None, :, None, :], jnp.exp(scores), 0.0)]
    dot_general x0 -> x1, local copies, waits for them, and re-layouts: none -> 5.58 us  [owner_attend(): jnp.einsum('qp,pl->ql', weights.reshape(-1, key_rows), latent_cache[:, :L...]
    all_to_all x1, waiting for transfers between devices: 19.8 us -> 15.4 us  [body(): lax.all_to_all(jnp.broadcast_to(arrived.reshape(1, peer_count * capacity,...]
    another operation x2 -> x3, local copies, waits for them, and re-layouts: 0.83 us -> 5.23 us  [the longest x1 4.4 us: body(): expert_down[0].reshape(expert_down.shape[1], head_count, quarter_width)]
    exp x1 -> x0, local copies, waits for them, and re-layouts: 4.37 us -> none  [owner_attend(): jnp.exp(scores)]
    convert_element_type x1, local copies, waits for them, and re-layouts: 0.09 us -> 4.38 us  [owner_attend(): jnp.where(inside[None, :, None, :], jnp.exp(scores), 0.0)]
    all_to_all x2 -> x0, local copies, waits for them, and re-layouts: 3.42 us -> none  [head_sum_scatter(): lax.all_to_all(values, 'head', split_axis=axis, concat_axis=0, tiled=True)]
  transfers between devices with their start and end apart: 7 -> 7, of which waited for: 7 -> 7; matrix products, arithmetic and copies ran while one was open for 3% -> 5% of each run, Pallas kernels for 0% -> 0%
where the time goes in v7:
time: 324 us; the launch traced here: 322 us
  waiting for transfers between devices  93.2 us (29%)
  local copies, waits for them, and re-layouts  71.2 us (22%)
  blocking collectives  48.8 us (15%)
  starting transfers between devices  47.4 us (15%)
  other arithmetic  31.2 us (10%)
  matrix products  28.5 us (9%)
    all_to_all x3, waiting for transfers between devices, head_sum_scatter(): lax.all_to_all(grouped, 'head', split_axis=0, concat_axis=0, tiled=True)  33.9 us
    all_to_all x1, blocking collectives, body(): lax.all_to_all(padded_rows[source_token].reshape(expert_count, capacity,...  23.7 us
    all_to_all x1, waiting for transfers between devices, body(): got_packed = lax.all_to_all(packed, 'tok', 0, 0, tiled=True)  17.9 us
    all_to_all x1, waiting for transfers between devices, body(): lax.all_to_all(jnp.concatenate([expert_share.reshape(peer_count, capacity...  17.1 us
    all_to_all x1, waiting for transfers between devices, body(): lax.all_to_all(jnp.broadcast_to(arrived.reshape(1, peer_count * capacity,...  15.4 us
    all_to_all x1, starting transfers between devices, body(): got_packed = lax.all_to_all(packed, 'tok', 0, 0, tiled=True)  14.1 us
    all_gather x1, blocking collectives, body(): lax.all_gather(jnp.concatenate([send_rows, gain_rows], axis=0), 'head', a...  12.9 us
    all_gather x1, blocking collectives, body(): all_heads = lax.all_gather(owner_probes, 'head', axis=0, tiled=False)  12.2 us
  transfers between devices with their start and end apart: 7, of which 7 were waited for; matrix products, arithmetic and copies ran while one was open for 5% of the time, Pallas kernels for 0%

profile of v7, /device:TPU:1, one launch (start us, length us, event | category | flops | bytes accessed | tf_op | source)
XLA Modules:
  0.0 321.6 jit_solution(7755771841582683662)
XLA Ops:
  5.4 12.9 %all-gather = bf16[160,2432]{1,0:T(8,128)(2,1)S(1)} all-gather(bf16[40,2432]{1,0:T(8,128)(2,1)S(1)} %pad_maximum_fusion.2), channel_id=2, replica_groups=mesh['tok'=64,'head'=4] {'head'}, dimensions={0}, use_global_device_ids=true | all-gather | bytes 972800 | tf_op jit(solution)/shard_map/all_gather | solution.py:123
  22.9 1.6 fusion.30
  35.3 1.6 gather_fusion
  36.8 2.5 pad_maximum_fusion.1
  39.3 14.1 %all-to-all-start = ((bf16[64,6,576]{2,1,0:T(8,128)(2,1)}), bf16[64,6,576]{2,1,0:T(8,128)(2,1)}, u32[]{:S(2)}, u32[]{:S(2)}) async-start(bf16[64,6,576]{2,1,0:T(8,128)(2,1)} %pad_maximum_fusion.1), calls=%async_computation | async-start | bytes 1310720 | tf_op jit(solution)/shard_map/all_to_all | solution.py:181
  53.8 1.6 gather_fusion.12
  55.5 17.9 %all-to-all-done = bf16[64,6,576]{2,1,0:T(8,128)(2,1)} async-done(((bf16[64,6,576]{2,1,0:T(8,128)(2,1)}), bf16[64,6,576]{2,1,0:T(8,128)(2,1)}, u32[]{:S(2)}, u32[]{:S(2)}) %all-to-all-start) | async-done | bytes 442400 | tf_op jit(solution)/shard_map/all_to_all | solution.py:181
  76.0 1.8 broadcast_in_dim.83
  77.7 4.3 %broadcast_in_dim.84 = pred[512,2496]{1,0:T(32,128)(4,1)} reshape(pred[4,32,4,2496]{3,2,1,0:T(4,128)(4,1)} %broadcast_in_dim.83) | data formatting | bytes 2555904 | tf_op jit(solution)/shard_map/jit(_where)/broadcast_in_dim | solution.py:44
  82.0 3.7 %copy.282 = pred[512,2496]{0,1:T(32,128)(4,1)} copy(pred[512,2496]{1,0:T(32,128)(4,1)} %broadcast_in_dim.84) | data formatting | bytes 2555904 | tf_op jit(solution)/shard_map/jit(_where)/broadcast_in_dim | solution.py:44
  85.7 1.9 copy.280
  87.7 2.1 gather_fusion.5
  89.8 12.2 %all-gather.1 = bf16[128,4,576]{2,0,1:T(8,128)(2,1)S(1)} all-gather(bf16[32,4,576]{2,0,1:T(8,128)(2,1)S(1)} %gather_fusion.5), channel_id=3, replica_groups=mesh['tok'=64,'head'=4] {'head'}, dimensions={0}, use_global_device_ids=true | all-gather | bytes 737280 | tf_op jit(solution)/shard_map/all_gather | solution.py:191
  103.4 2.2 reshape.650
  105.6 6.8 %convert_reduce_fusion = (f32[512]{0:T(512)S(1)}, bf16[512,2496]{0,1:T(8,128)(2,1)}) fusion(pred[512,2496]{0,1:T(32,128)(4,1)} %copy.282, bf16[512,576]{1,0:T(8,128)(2,1)} %reshape.650, bf16[2496,576]{0,1:T(8,128)(2,1)} %param.29), kind=kOutput, calls=%fused_computation.13 | convolution fusion | flops 1478589952 | bytes 7301120 | tf_op jit(solution)/shard_map/qc,pc->qp/dot_general | solution.py:37
  113.6 4.4 %copy.283 = bf16[512,2496]{1,0:T(8,128)(2,1)} copy(bf16[512,2496]{0,1:T(8,128)(2,1)} %get-tuple-element.80) | data formatting | bytes 5111808 | tf_op jit(solution)/shard_map/convert_element_type | solution.py:44
  118.0 5.6 %dot_general.42 = bf16[4,32,4,2496]{3,2,1,0:T(4,128)(2,1)} reshape(bf16[512,2496]{1,0:T(8,128)(2,1)} %copy.283) | data formatting | bytes 5111808 | tf_op jit(solution)/shard_map/qp,pl->ql/dot_general | solution.py:45
  123.6 4.1 %fusion.4 = f32[4,32,4,512]{3,1,2,0:T(8,128)S(1)} fusion(bf16[4,32,4,2496]{3,2,1,0:T(4,128)(2,1)} %dot_general.42, bf16[2496,576]{0,1:T(8,128)(2,1)} %param.29), kind=kOutput, calls=%fused_computation.21 | convolution fusion | flops 1308622848 | bytes 6291456 | tf_op jit(solution)/shard_map/qp,pl->ql/dot_general | solution.py:45
  128.9 4.4 %all-to-all-start.1 = ((f32[4,32,4,513]{3,1,2,0:T(8,128)}), f32[4,32,4,513]{3,1,2,0:T(8,128)}, u32[]{:S(2)}, u32[]{:S(2)}) async-start(f32[4,32,4,513]{3,1,2,0:T(8,128)} %pad_maximum_fusion), calls=%async_computation.1 | async-start | bytes 2621440 | tf_op jit(solution)/shard_map/all_to_all | solution.py:56
  133.9 1.8 gather_fusion.6
  137.2 11.7 %all-to-all-done.1 = f32[4,32,4,513]{3,1,2,0:T(8,128)} async-done(((f32[4,32,4,513]{3,1,2,0:T(8,128)}), f32[4,32,4,513]{3,1,2,0:T(8,128)}, u32[]{:S(2)}, u32[]{:S(2)}) %all-to-all-start.1) | async-done | bytes 1050656 | tf_op jit(solution)/shard_map/all_to_all | solution.py:56
  155.1 8.8 %all-to-all-start.2 = ((bf16[64,2,256]{2,1,0:T(2,128)(2,1)}), bf16[64,2,256]{2,1,0:T(2,128)(2,1)S(1)}, u32[]{:S(2)}, u32[]{:S(2)}) async-start(bf16[64,2,256]{2,1,0:T(2,128)(2,1)} %reshape.799), calls=%async_computation.2 | async-start | bytes 131072 | tf_op jit(solution)/shard_map/all_to_all | solution.py:214
  164.8 8.9 %all-to-all-done.2 = bf16[64,2,256]{2,1,0:T(2,128)(2,1)S(1)} async-done(((bf16[64,2,256]{2,1,0:T(2,128)(2,1)}), bf16[64,2,256]{2,1,0:T(2,128)(2,1)S(1)}, u32[]{:S(2)}, u32[]{:S(2)}) %all-to-all-start.2) | async-done | bytes 65568 | tf_op jit(solution)/shard_map/all_to_all | solution.py:214
  174.4 2.8 fusion.26
  177.2 3.4 %all-to-all-start.3 = ((f32[4,32,512]{2,1,0:T(8,128)}), f32[4,32,512]{2,1,0:T(8,128)S(1)}, u32[]{:S(2)}, u32[]{:S(2)}) async-start(f32[4,32,512]{2,1,0:T(8,128)} %fusion.26), calls=%async_computation.3 | async-start | bytes 524288 | tf_op jit(solution)/shard_map/all_to_all | solution.py:56
  180.7 6.0 %all-to-all-done.3 = f32[4,32,512]{2,1,0:T(8,128)S(1)} async-done(((f32[4,32,512]{2,1,0:T(8,128)}), f32[4,32,512]{2,1,0:T(8,128)S(1)}, u32[]{:S(2)}, u32[]{:S(2)}) %all-to-all-start.3) | async-done | bytes 262176 | tf_op jit(solution)/shard_map/all_to_all | solution.py:56
  186.7 2.6 gather_fusion.9
  189.3 1.9 reshape.654
  191.2 23.7 %all_to_all.51 = bf16[64,6,512]{2,1,0:T(8,128)(2,1)} all-to-all(bf16[64,6,512]{2,1,0:T(8,128)(2,1)} %reshape.654), channel_id=1, replica_groups=mesh['tok'=64,'head'=4] {'tok'}, dimensions={0} | all-to-all | bytes 786432 | tf_op jit(solution)/shard_map/all_to_all | solution.py:243
  217.0 2.3 broadcast_in_dim.146
  219.3 4.3 %all-to-all-start.5 = ((bf16[4,384,512]{1,2,0:T(8,128)(2,1)}), bf16[4,384,512]{1,2,0:T(8,128)(2,1)}, u32[]{:S(2)}, u32[]{:S(2)}) async-start(bf16[4,384,512]{1,2,0:T(8,128)(2,1)} %broadcast_in_dim.146), calls=%async_computation.5 | async-start | bytes 3145728 | tf_op jit(solution)/shard_map/all_to_all | solution.py:250
  224.4 4.4 %reshape_squeeze.7 = bf16[352,4,512]{2,1,0:T(4,128)(2,1)} reshape(bf16[1,352,2048]{2,1,0:T(8,128)(2,1)} %param.37) | data formatting | bytes 2883584 | tf_op jit(solution)/shard_map/reshape;squeeze | solution.py:275
  228.8 15.4 %all-to-all-done.5 = bf16[4,384,512]{1,2,0:T(8,128)(2,1)} async-done(((bf16[4,384,512]{1,2,0:T(8,128)(2,1)}), bf16[4,384,512]{1,2,0:T(8,128)(2,1)}, u32[]{:S(2)}, u32[]{:S(2)}) %all-to-all-start.5) | async-done | bytes 1572896 | tf_op jit(solution)/shard_map/all_to_all | solution.py:250
  244.2 1.8 fusion.3
  246.1 3.2 fusion.2
  250.4 1.7 fusion.14
  252.1 5.5 %fusion.11 = bf16[4,384,512]{2,1,0:T(8,128)(2,1)} fusion(bf16[352,4,512]{2,1,0:T(4,128)(2,1)} %reshape_squeeze.7, bf16[384,2048]{0,1:T(8,128)(2,1)} %bitcast.131, bf16[1,2048,352]{1,2,0:T(8,128)(2,1)} %param.36, f32[384,352]{0,1:T(8,128)} %fusion.14), kind=kOutput, calls=%fused_computation.29 | convolution fusion | flops 1108893696 | bytes 6569984 | tf_op jit(solution)/shard_map/rk,kgf->grf/dot_general | solution.py:272
  257.7 4.3 %all-to-all-start.6 = ((bf16[4,384,512]{2,1,0:T(8,128)(2,1)}), bf16[4,384,512]{2,1,0:T(8,128)(2,1)}, u32[]{:S(2)}, u32[]{:S(2)}) async-start(bf16[4,384,512]{2,1,0:T(8,128)(2,1)} %fusion.11), calls=%async_computation.6 | async-start | bytes 3145728 | tf_op jit(solution)/shard_map/all_to_all | solution.py:56
  262.8 1.7 convolution_reduce_fusion
  265.5 16.2 %all-to-all-done.6 = bf16[4,384,512]{2,1,0:T(8,128)(2,1)} async-done(((bf16[4,384,512]{2,1,0:T(8,128)(2,1)}), bf16[4,384,512]{2,1,0:T(8,128)(2,1)}, u32[]{:S(2)}, u32[]{:S(2)}) %all-to-all-start.6) | async-done | bytes 1572896 | tf_op jit(solution)/shard_map/all_to_all | solution.py:56
  281.7 1.8 reduce_sum.136
  284.5 2.0 fusion.40
  286.5 8.0 %all-to-all-start.7 = ((bf16[64,7,512]{2,1,0:T(8,128)(2,1)}), bf16[64,7,512]{2,1,0:T(8,128)(2,1)}, u32[]{:S(2)}, u32[]{:S(2)}) async-start(bf16[64,7,512]{2,1,0:T(8,128)(2,1)} %fusion.40), calls=%async_computation.7 | async-start | bytes 1048576 | tf_op jit(solution)/shard_map/all_to_all | solution.py:288
  294.7 17.1 %all-to-all-done.7 = bf16[64,7,512]{2,1,0:T(8,128)(2,1)} async-done(((bf16[64,7,512]{2,1,0:T(8,128)(2,1)}), bf16[64,7,512]{2,1,0:T(8,128)(2,1)}, u32[]{:S(2)}, u32[]{:S(2)}) %all-to-all-start.7) | async-done | bytes 458784 | tf_op jit(solution)/shard_map/all_to_all | solution.py:288
  312.9 1.7 gather_fusion.11
  314.6 1.8 reshape.767
  317.8 1.6 gather_fusion.10
  319.7 1.9 multiply_reduce_fusion
  (161 shorter events, 46.2 us)
Async XLA Ops:
  0.6 22.3 %copy-start = (bf16[2048,768]{1,0:T(8,128)(2,1)S(1)}, bf16[2048,768]{1,0:T(8,128)(2,1)}, u32[]{:S(2)}) copy-start(bf16[2048,768]{1,0:T(8,128)(2,1)} %param.24) | copy-start | bytes 9437188
  3.1 16.3 %copy-start.2 = (s32[32]{0:T(128)S(1)}, s32[32]{0:T(128)}, u32[]{:S(2)}) copy-start(s32[32]{0:T(128)} %param.30) | copy-start | bytes 388
  3.1 16.8 %copy-start.1 = (s32[32]{0:T(128)S(1)}, s32[32]{0:T(128)}, u32[]{:S(2)}) copy-start(s32[32]{0:T(128)} %param.31) | copy-start | bytes 388
  5.4 17.5 %copy-start.13 = (f32[2048]{0:T(1024)S(1)}, f32[2048]{0:T(1024)}, u32[]{:S(2)}) copy-start(f32[2048]{0:T(1024)} %param.23) | copy-start | bytes 24580
  18.3 0.9 copy-start.4
  24.6 0.6 copy-start.9
  25.3 7.7 %slice-start = ((bf16[32,4,192]{2,1,0:T(4,128)(2,1)}), bf16[32,4,64]{2,1,0:T(4,128)(2,1)S(1)}, s32[]{:S(2)}) async-start(bf16[32,4,192]{2,1,0:T(4,128)(2,1)} %copy-done.9), calls=%async_computation.8 | async-start | bytes 65536 | tf_op jit(solution)/shard_map/slice | solution.py:161
  25.3 7.7 %slice-start.1 = ((bf16[32,4,192]{2,1,0:T(4,128)(2,1)}), bf16[32,4,128]{2,1,0:T(4,128)(2,1)S(1)}, s32[]{:S(2)}) async-start(bf16[32,4,192]{2,1,0:T(4,128)(2,1)} %copy-done.9), calls=%async_computation.9 | async-start | bytes 65536 | tf_op jit(solution)/shard_map/slice | solution.py:159
  31.5 5.4 %copy-start.3 = (bf16[32,576]{1,0:T(8,128)(2,1)}, bf16[32,576]{1,0:T(8,128)(2,1)S(1)}, u32[]{:S(2)}) copy-start(bf16[32,576]{1,0:T(8,128)(2,1)S(1)} %pad_maximum_fusion.4) | copy-start | bytes 110596
  35.3 18.1 %copy-start.12 = (s32[32,6]{0,1:T(8,128)S(1)}, s32[32,6]{0,1:T(8,128)}, u32[]{:S(2)}) copy-start(s32[32,6]{0,1:T(8,128)} %param.34) | copy-start | bytes 2308
  39.3 34.1 %all-to-all-start = ((bf16[64,6,576]{2,1,0:T(8,128)(2,1)}), bf16[64,6,576]{2,1,0:T(8,128)(2,1)}, u32[]{:S(2)}, u32[]{:S(2)}) async-start(bf16[64,6,576]{2,1,0:T(8,128)(2,1)} %pad_maximum_fusion.1), calls=%async_computation | async-start | bytes 1310720 | tf_op jit(solution)/shard_map/all_to_all | solution.py:181
  89.8 15.8 %copy-start.6 = (bf16[32,4,576]{2,0,1:T(8,128)(2,1)}, bf16[32,4,576]{2,0,1:T(8,128)(2,1)S(1)}, u32[]{:S(2)}) copy-start(bf16[32,4,576]{2,0,1:T(8,128)(2,1)S(1)} %gather_fusion.5) | copy-start | bytes 442372
  128.9 6.8 %copy-start.7 = (bf16[32,4,576]{2,0,1:T(8,128)(2,1)S(1)}, bf16[32,4,576]{2,0,1:T(8,128)(2,1)}, u32[]{:S(2)}) copy-start(bf16[32,4,576]{2,0,1:T(8,128)(2,1)} %copy-done.6) | copy-start | bytes 442372
  128.9 20.1 %all-to-all-start.1 = ((f32[4,32,4,513]{3,1,2,0:T(8,128)}), f32[4,32,4,513]{3,1,2,0:T(8,128)}, u32[]{:S(2)}, u32[]{:S(2)}) async-start(f32[4,32,4,513]{3,1,2,0:T(8,128)} %pad_maximum_fusion), calls=%async_computation.1 | async-start | bytes 2621440 | tf_op jit(solution)/shard_map/all_to_all | solution.py:56
  155.1 18.6 %all-to-all-start.2 = ((bf16[64,2,256]{2,1,0:T(2,128)(2,1)}), bf16[64,2,256]{2,1,0:T(2,128)(2,1)S(1)}, u32[]{:S(2)}, u32[]{:S(2)}) async-start(bf16[64,2,256]{2,1,0:T(2,128)(2,1)} %reshape.799), calls=%async_computation.2 | async-start | bytes 131072 | tf_op jit(solution)/shard_map/all_to_all | solution.py:214
  174.4 12.3 %copy-start.8 = (bf16[32,512]{1,0:T(8,128)(2,1)S(1)}, bf16[32,512]{1,0:T(8,128)(2,1)}, u32[]{:S(2)}) copy-start(bf16[32,512]{1,0:T(8,128)(2,1)} %param.22) | copy-start | bytes 98308
  177.2 9.5 %all-to-all-start.3 = ((f32[4,32,512]{2,1,0:T(8,128)}), f32[4,32,512]{2,1,0:T(8,128)S(1)}, u32[]{:S(2)}, u32[]{:S(2)}) async-start(f32[4,32,512]{2,1,0:T(8,128)} %fusion.26), calls=%async_computation.3 | async-start | bytes 524288 | tf_op jit(solution)/shard_map/all_to_all | solution.py:56
  186.7 2.6 copy-start.10
  219.3 24.9 %all-to-all-start.5 = ((bf16[4,384,512]{1,2,0:T(8,128)(2,1)}), bf16[4,384,512]{1,2,0:T(8,128)(2,1)}, u32[]{:S(2)}, u32[]{:S(2)}) async-start(bf16[4,384,512]{1,2,0:T(8,128)(2,1)} %broadcast_in_dim.146), calls=%async_computation.5 | async-start | bytes 3145728 | tf_op jit(solution)/shard_map/all_to_all | solution.py:250
  246.1 4.3 %copy-start.14 = (bf16[1,2048,352]{1,2,0:T(8,128)(2,1)S(1)}, bf16[1,2048,352]{1,2,0:T(8,128)(2,1)}, u32[]{:S(2)}) copy-start(bf16[1,2048,352]{1,2,0:T(8,128)(2,1)} %param.35) | copy-start | bytes 4325380
  249.2 1.1 copy-start.5
  257.7 24.1 %all-to-all-start.6 = ((bf16[4,384,512]{2,1,0:T(8,128)(2,1)}), bf16[4,384,512]{2,1,0:T(8,128)(2,1)}, u32[]{:S(2)}, u32[]{:S(2)}) async-start(bf16[4,384,512]{2,1,0:T(8,128)(2,1)} %fusion.11), calls=%async_computation.6 | async-start | bytes 3145728 | tf_op jit(solution)/shard_map/all_to_all | solution.py:56
  283.6 11.0 %copy-start.11 = (s32[32,6]{1,0:T(8,128)S(1)}, s32[32,6]{1,0:T(8,128)}, u32[]{:S(2)}) copy-start(s32[32,6]{1,0:T(8,128)} %get-tuple-element.45) | copy-start | bytes 2308
  286.5 25.2 %all-to-all-start.7 = ((bf16[64,7,512]{2,1,0:T(8,128)(2,1)}), bf16[64,7,512]{2,1,0:T(8,128)(2,1)}, u32[]{:S(2)}, u32[]{:S(2)}) async-start(bf16[64,7,512]{2,1,0:T(8,128)(2,1)} %fusion.40), calls=%async_computation.7 | async-start | bytes 1048576 | tf_op jit(solution)/shard_map/all_to_all | solution.py:288

commit v8 on v6

--- a/solution.py
+++ b/solution.py
@@ -234,38 +234,51 @@
     padded_rows = jnp.concatenate(
         [attended, jnp.zeros((1, attended.shape[1]), jnp.bfloat16)], axis=0
     )
-    arrived = lax.all_to_all(
-        padded_rows[source_token].reshape(expert_count, capacity, quarter_width),
-        "tok",
-        split_axis=0,
-        concat_axis=0,
-        tiled=True,
-    )
-    expert_in = lax.all_to_all(
-        jnp.broadcast_to(
-            arrived.reshape(1, peer_count * capacity, quarter_width),
-            (head_count, peer_count * capacity, quarter_width),
-        ),
-        "head",
-        split_axis=0,
-        concat_axis=2,
-        tiled=True,
-    ).reshape(peer_count * capacity, head_count * quarter_width)
-    expert_wide = expert_in.astype(jnp.float32)
-    expert_inv = lax.rsqrt(jnp.mean(expert_wide * expert_wide, axis=1, keepdims=True) + NORM_EPS)
-    expert_gained = (expert_wide * gain_full).astype(jnp.bfloat16)
-    expert_logit = (
-        jnp.dot(expert_gained, expert_column, preferred_element_type=jnp.float32)
-        * expert_inv[:, 0]
-    )
-    expert_in = (expert_wide * gain_full * expert_inv).astype(jnp.bfloat16)
-    gate_value = jnp.dot(expert_in, expert_gate[0], preferred_element_type=jnp.float32)
-    up_value = jnp.dot(expert_in, expert_up[0], preferred_element_type=jnp.float32)
-    activity = (jax.nn.silu(gate_value) * up_value).astype(jnp.bfloat16)
-    expert_share = head_sum_scatter(
-        jnp.dot(activity, expert_down[0], preferred_element_type=jnp.float32).astype(jnp.bfloat16),
-        1,
-    ).astype(jnp.bfloat16)
+    half = capacity // 2
+    source_grid = source_token.reshape(expert_count, capacity)
+
+    def expert_half(lo, hi):
+        width = hi - lo
+        arrived = lax.all_to_all(
+            padded_rows[source_grid[:, lo:hi]], "tok", split_axis=0, concat_axis=0, tiled=True
+        )
+        expert_in = lax.all_to_all(
+            jnp.broadcast_to(
+                arrived.reshape(1, peer_count * width, quarter_width),
+                (head_count, peer_count * width, quarter_width),
+            ),
+            "head",
+            split_axis=0,
+            concat_axis=2,
+            tiled=True,
+        ).reshape(peer_count * width, head_count * quarter_width)
+        expert_wide = expert_in.astype(jnp.float32)
+        expert_inv = lax.rsqrt(
+            jnp.mean(expert_wide * expert_wide, axis=1, keepdims=True) + NORM_EPS
+        )
+        expert_gained = (expert_wide * gain_full).astype(jnp.bfloat16)
+        expert_logit = (
+            jnp.dot(expert_gained, expert_column, preferred_element_type=jnp.float32)
+            * expert_inv[:, 0]
+        )
+        expert_in = (expert_wide * gain_full * expert_inv).astype(jnp.bfloat16)
+        gate_value = jnp.dot(expert_in, expert_gate[0], preferred_element_type=jnp.float32)
+        up_value = jnp.dot(expert_in, expert_up[0], preferred_element_type=jnp.float32)
+        activity = (jax.nn.silu(gate_value) * up_value).astype(jnp.bfloat16)
+        share = head_sum_scatter(
+            jnp.dot(activity, expert_down[0], preferred_element_type=jnp.float32).astype(
+                jnp.bfloat16
+            ),
+            1,
+        ).astype(jnp.bfloat16)
+        return share.reshape(peer_count, width, quarter_width), expert_logit.reshape(
+            peer_count, width
+        )
+
+    share_a, logit_a = expert_half(0, half)
+    share_b, logit_b = expert_half(half, capacity)
+    expert_share = jnp.concatenate([share_a, share_b], axis=1)
+    expert_logit = jnp.concatenate([logit_a, logit_b], axis=1).reshape(-1)
     logit_hi = lax.reduce_precision(expert_logit, exponent_bits=8, mantissa_bits=7)
     logit_rest = expert_logit - logit_hi
     logit_mid = lax.reduce_precision(logit_rest, exponent_bits=8, mantissa_bits=7)

time: 310 us -> 334 us (1.077)
  blocking collectives: 49 us -> 25.1 us
  starting transfers between devices: 47.4 us -> 70 us
  local copies, waits for them, and re-layouts: 54.9 us -> 66.8 us
  waiting for transfers between devices: 98.1 us -> 106 us
  other arithmetic: 32.7 us -> 36.4 us
    all_to_all x1 -> x0, blocking collectives: 23.9 us -> none  [body(): lax.all_to_all(padded_rows[source_token].reshape(expert_count, capacity,...]
    all_to_all x1 -> x4, waiting for transfers between devices: 19.8 us -> 39.4 us  [the longest x2 20.1 us: expert_half(): lax.all_to_all(padded_rows[source_grid[:, lo:hi]], 'tok', split_axis=0, c...]
    all_to_all x1 -> x4, starting transfers between devices: 4.33 us -> 21.1 us  [the longest x2 12.7 us: expert_half(): lax.all_to_all(padded_rows[source_grid[:, lo:hi]], 'tok', split_axis=0, c...]
    all_to_all x3 -> x4, waiting for transfers between devices: 34.4 us -> 23 us  [head_sum_scatter(): lax.all_to_all(values, 'head', split_axis=axis, concat_axis=0, tiled=True)]
    convert_element_type x0 -> x4, local copies, waits for them, and re-layouts: none -> 4.78 us  [the longest x2 3.56 us: expert_half(): expert_gained = (expert_wide * gain_full).astype(jnp.bfloat16)]
    all_to_all x3 -> x4, starting transfers between devices: 12.2 us -> 16.5 us  [head_sum_scatter(): lax.all_to_all(values, 'head', split_axis=axis, concat_axis=0, tiled=True)]
    dot_general x3 -> x6, matrix products: 8.91 us -> 10.4 us  [the longest x2 8.47 us: expert_half(): jnp.dot(activity, expert_down[0], preferred_element_type=jnp.float32)]
  transfers between devices with their start and end apart: 7 -> 11, of which waited for: 7 -> 10; matrix products, arithmetic and copies ran while one was open for 3% -> 10% of each run, Pallas kernels for 0% -> 0%
where the time goes in v8:
time: 334 us; the launch traced here: 332 us
  waiting for transfers between devices  106 us (32%)
  starting transfers between devices  70 us (21%)
  local copies, waits for them, and re-layouts  66.8 us (20%)
  other arithmetic  36.4 us (11%)
  matrix products  25.9 us (8%)
  blocking collectives  25.1 us (8%)
    all_to_all x4, waiting for transfers between devices, head_sum_scatter(): lax.all_to_all(values, 'head', split_axis=axis, concat_axis=0, tiled=True)  23 us
    all_to_all x2, waiting for transfers between devices, expert_half(): lax.all_to_all(padded_rows[source_grid[:, lo:hi]], 'tok', split_axis=0, c...  20.1 us
    all_to_all x2, waiting for transfers between devices, expert_half(): lax.all_to_all(jnp.broadcast_to(arrived.reshape(1, peer_count * width, qu...  19.3 us
    all_to_all x1, waiting for transfers between devices, body(): got_packed = lax.all_to_all(packed, 'tok', 0, 0, tiled=True)  17.3 us
    all_to_all x1, waiting for transfers between devices, body(): lax.all_to_all(jnp.concatenate([expert_share.reshape(peer_count, capacity...  17.1 us
    all_to_all x4, starting transfers between devices, head_sum_scatter(): lax.all_to_all(values, 'head', split_axis=axis, concat_axis=0, tiled=True)  16.5 us
    all_to_all x1, starting transfers between devices, body(): got_packed = lax.all_to_all(packed, 'tok', 0, 0, tiled=True)  14.1 us
    all_gather x1, blocking collectives, body(): lax.all_gather(jnp.concatenate([send_rows, gain_rows], axis=0), 'head', a...  12.9 us
  transfers between devices with their start and end apart: 11, of which 10 were waited for; matrix products, arithmetic and copies ran while one was open for 10% of the time, Pallas kernels for 0%

profile of v8, /device:TPU:1, one launch (start us, length us, event | category | flops | bytes accessed | tf_op | source)
XLA Modules:
  0.0 332.1 jit_solution(7707859899687840811)
XLA Ops:
  11.9 12.9 %all-gather = bf16[160,2432]{1,0:T(8,128)(2,1)S(1)} all-gather(bf16[40,2432]{1,0:T(8,128)(2,1)S(1)} %pad_maximum_fusion.2), channel_id=2, replica_groups=mesh['tok'=64,'head'=4] {'head'}, dimensions={0}, use_global_device_ids=true | all-gather | bytes 972800 | tf_op jit(solution)/shard_map/all_gather | solution.py:124
  36.8 2.5 pad_maximum_fusion.1
  39.2 14.1 %all-to-all-start = ((bf16[64,6,576]{2,1,0:T(8,128)(2,1)}), bf16[64,6,576]{2,1,0:T(8,128)(2,1)}, u32[]{:S(2)}, u32[]{:S(2)}) async-start(bf16[64,6,576]{2,1,0:T(8,128)(2,1)} %pad_maximum_fusion.1), calls=%async_computation | async-start | bytes 1310720 | tf_op jit(solution)/shard_map/all_to_all | solution.py:182
  56.0 17.3 %all-to-all-done = bf16[64,6,576]{2,1,0:T(8,128)(2,1)} async-done(((bf16[64,6,576]{2,1,0:T(8,128)(2,1)}), bf16[64,6,576]{2,1,0:T(8,128)(2,1)}, u32[]{:S(2)}, u32[]{:S(2)}) %all-to-all-start) | async-done | bytes 442400 | tf_op jit(solution)/shard_map/all_to_all | solution.py:182
  75.7 1.9 copy.304
  77.6 2.1 gather_fusion.5
  79.8 12.2 %all_gather.11 = bf16[32,16,576]{2,0,1:T(8,128)(2,1)S(1)} all-gather(bf16[32,4,576]{2,0,1:T(8,128)(2,1)S(1)} %gather_fusion.5), channel_id=1, replica_groups=mesh['tok'=64,'head'=4] {'head'}, dimensions={1}, use_global_device_ids=true | all-gather | bytes 737280 | tf_op jit(solution)/shard_map/all_gather | solution.py:192
  94.2 4.5 %convert_reduce_fusion = (f32[512]{0:T(512)S(1)}, bf16[512,2496]{0,1:T(8,128)(2,1)}) fusion(pred[512,2496]{0,1:T(32,128)(4,1)S(1)} %copy.308, bf16[512,576]{1,0:T(8,128)(2,1)S(1)} %bitcast.186, bf16[2496,576]{0,1:T(8,128)(2,1)S(1)} %copy-done.19), kind=kOutput, calls=%fused_computation.15 | convolution fusion | flops 1478589952 | bytes 7301120 | tf_op jit(solution)/shard_map/qc,pc->qp/dot_general | solution.py:39
  98.9 4.4 %copy.306 = bf16[512,2496]{1,0:T(8,128)(2,1)} copy(bf16[512,2496]{0,1:T(8,128)(2,1)} %get-tuple-element.86) | data formatting | bytes 5111808 | tf_op jit(solution)/shard_map/exp | solution.py:46
  103.3 4.1 %fusion = f32[32,16,512]{2,1,0:T(8,128)S(1)} fusion(bf16[32,16,2496]{2,1,0:T(8,128)(2,1)} %bitcast.179, bf16[2496,576]{0,1:T(8,128)(2,1)} %param.29, pred[32,2496]{1,0:T(8,128)(4,1)S(1)} %compare_and_fusion), kind=kOutput, calls=%fused_computation.18 | convolution fusion | flops 1309900800 | bytes 6371328 | tf_op jit(solution)/shard_map/khp,pl->khl/dot_general | solution.py:47
  109.0 4.4 %all-to-all-start.1 = ((f32[32,16,513]{2,0,1:T(8,128)}), f32[32,16,513]{2,0,1:T(8,128)}, u32[]{:S(2)}, u32[]{:S(2)}) async-start(f32[32,16,513]{2,0,1:T(8,128)} %copy.310), calls=%async_computation.1 | async-start | bytes 2621440 | tf_op jit(solution)/shard_map/all_to_all | solution.py:56
  114.3 1.8 gather_fusion.6
  117.1 12.0 %all-to-all-done.1 = f32[32,16,513]{2,0,1:T(8,128)} async-done(((f32[32,16,513]{2,0,1:T(8,128)}), f32[32,16,513]{2,0,1:T(8,128)}, u32[]{:S(2)}, u32[]{:S(2)}) %all-to-all-start.1) | async-done | bytes 1050656 | tf_op jit(solution)/shard_map/all_to_all | solution.py:56
  138.0 8.8 %all-to-all-start.2 = ((bf16[64,2,256]{2,1,0:T(2,128)(2,1)}), bf16[64,2,256]{2,1,0:T(2,128)(2,1)S(1)}, u32[]{:S(2)}, u32[]{:S(2)}) async-start(bf16[64,2,256]{2,1,0:T(2,128)(2,1)} %reshape.886), calls=%async_computation.2 | async-start | bytes 131072 | tf_op jit(solution)/shard_map/all_to_all | solution.py:215
  147.0 9.6 %all-to-all-done.2 = bf16[64,2,256]{2,1,0:T(2,128)(2,1)S(1)} async-done(((bf16[64,2,256]{2,1,0:T(2,128)(2,1)}), bf16[64,2,256]{2,1,0:T(2,128)(2,1)S(1)}, u32[]{:S(2)}, u32[]{:S(2)}) %all-to-all-start.2) | async-done | bytes 65568 | tf_op jit(solution)/shard_map/all_to_all | solution.py:215
  157.3 2.1 fusion.116
  160.1 3.4 %all-to-all-start.3 = ((f32[32,4,512]{2,0,1:T(8,128)}), f32[32,4,512]{2,0,1:T(8,128)S(1)}, u32[]{:S(2)}, u32[]{:S(2)}) async-start(f32[32,4,512]{2,0,1:T(8,128)} %bitcast.183), calls=%async_computation.3 | async-start | bytes 524288 | tf_op jit(solution)/shard_map/all_to_all | solution.py:56
  164.3 5.2 %all-to-all-done.3 = f32[32,4,512]{2,0,1:T(8,128)S(1)} async-done(((f32[32,4,512]{2,0,1:T(8,128)}), f32[32,4,512]{2,0,1:T(8,128)S(1)}, u32[]{:S(2)}, u32[]{:S(2)}) %all-to-all-start.3) | async-done | bytes 262176 | tf_op jit(solution)/shard_map/all_to_all | solution.py:56
  171.4 6.6 %all-to-all-start.4 = ((bf16[64,3,512]{2,1,0:T(4,128)(2,1)}), bf16[64,3,512]{2,1,0:T(4,128)(2,1)}, u32[]{:S(2)}, u32[]{:S(2)}) async-start(bf16[64,3,512]{2,1,0:T(4,128)(2,1)} %reshape.808), calls=%async_computation.4 | async-start | bytes 524288 | tf_op jit(solution)/shard_map/all_to_all | solution.py:242
  180.0 9.9 %all-to-all-done.4 = bf16[64,3,512]{2,1,0:T(4,128)(2,1)} async-done(((bf16[64,3,512]{2,1,0:T(4,128)(2,1)}), bf16[64,3,512]{2,1,0:T(4,128)(2,1)}, u32[]{:S(2)}, u32[]{:S(2)}) %all-to-all-start.4) | async-done | bytes 196640 | tf_op jit(solution)/shard_map/all_to_all | solution.py:242
  189.9 6.1 %all-to-all-start.7 = ((bf16[64,3,512]{2,1,0:T(4,128)(2,1)}), bf16[64,3,512]{2,1,0:T(4,128)(2,1)S(1)}, u32[]{:S(2)}, u32[]{:S(2)}) async-start(bf16[64,3,512]{2,1,0:T(4,128)(2,1)} %reshape.816), calls=%async_computation.7 | async-start | bytes 524288 | tf_op jit(solution)/shard_map/all_to_all | solution.py:242
  196.1 1.8 broadcast_in_dim.162
  197.9 10.2 %all-to-all-done.7 = bf16[64,3,512]{2,1,0:T(4,128)(2,1)S(1)} async-done(((bf16[64,3,512]{2,1,0:T(4,128)(2,1)}), bf16[64,3,512]{2,1,0:T(4,128)(2,1)S(1)}, u32[]{:S(2)}, u32[]{:S(2)}) %all-to-all-start.7) | async-done | bytes 196640 | tf_op jit(solution)/shard_map/all_to_all | solution.py:242
  208.0 1.9 broadcast_in_dim.163
  209.9 4.2 %all-to-all-start.5 = ((bf16[4,192,512]{2,1,0:T(8,128)(2,1)}), bf16[4,192,512]{2,1,0:T(8,128)(2,1)}, u32[]{:S(2)}, u32[]{:S(2)}) async-start(bf16[4,192,512]{2,1,0:T(8,128)(2,1)} %broadcast_in_dim.163), calls=%async_computation.5 | async-start | bytes 1572864 | tf_op jit(solution)/shard_map/all_to_all | solution.py:245
  216.5 9.6 %all-to-all-done.5 = bf16[4,192,512]{2,1,0:T(8,128)(2,1)} async-done(((bf16[4,192,512]{2,1,0:T(8,128)(2,1)}), bf16[4,192,512]{2,1,0:T(8,128)(2,1)}, u32[]{:S(2)}, u32[]{:S(2)}) %all-to-all-start.5) | async-done | bytes 786464 | tf_op jit(solution)/shard_map/all_to_all | solution.py:245
  226.1 1.9 broadcast_in_dim.166
  228.0 4.2 %all-to-all-start.8 = ((bf16[4,192,512]{2,1,0:T(8,128)(2,1)}), bf16[4,192,512]{2,1,0:T(8,128)(2,1)}, u32[]{:S(2)}, u32[]{:S(2)}) async-start(bf16[4,192,512]{2,1,0:T(8,128)(2,1)} %broadcast_in_dim.166), calls=%async_computation.8 | async-start | bytes 1572864 | tf_op jit(solution)/shard_map/all_to_all | solution.py:245
  233.6 9.7 %all-to-all-done.8 = bf16[4,192,512]{2,1,0:T(8,128)(2,1)} async-done(((bf16[4,192,512]{2,1,0:T(8,128)(2,1)}), bf16[4,192,512]{2,1,0:T(8,128)(2,1)}, u32[]{:S(2)}, u32[]{:S(2)}) %all-to-all-start.8) | async-done | bytes 786464 | tf_op jit(solution)/shard_map/all_to_all | solution.py:245
  244.7 3.0 fusion.43
  250.1 4.2 %convolution_convert_fusion.1 = bf16[192,2048]{1,0:T(8,128)(2,1)} fusion(bf16[1,352,2048]{2,1,0:T(8,128)(2,1)} %param.37, bf16[192,2048]{1,0:T(8,128)(2,1)} %bitcast.163, bf16[1,2048,352]{1,2,0:T(8,128)(2,1)} %param.36, f32[192,352]{1,0:T(8,128)S(1)} %fusion.21), kind=kOutput, calls=%fused_computation.24 | convolution fusion | flops 554446848 | bytes 4726784 | tf_op jit(solution)/shard_map/dot_general | solution.py:269
  254.3 2.1 copy.378
  256.5 4.2 %all-to-all-start.6 = ((bf16[192,4,512]{2,0,1:T(8,128)(2,1)}), bf16[192,4,512]{2,0,1:T(8,128)(2,1)}, u32[]{:S(2)}, u32[]{:S(2)}) async-start(bf16[192,4,512]{2,0,1:T(8,128)(2,1)} %bitcast.167), calls=%async_computation.6 | async-start | bytes 1572864 | tf_op jit(solution)/shard_map/all_to_all | solution.py:56
  260.7 1.7 copy.329
  263.1 1.8 copy.331
  268.3 4.2 %convolution_convert_fusion = bf16[192,2048]{1,0:T(8,128)(2,1)} fusion(bf16[1,352,2048]{2,1,0:T(8,128)(2,1)} %param.37, bf16[192,2048]{1,0:T(8,128)(2,1)} %bitcast.165, bf16[1,2048,352]{1,2,0:T(8,128)(2,1)} %param.36, f32[192,352]{1,0:T(8,128)S(1)} %fusion.19), kind=kOutput, calls=%fused_computation.23 | convolution fusion | flops 554446848 | bytes 4726784 | tf_op jit(solution)/shard_map/dot_general | solution.py:269
  272.6 2.2 copy.377
  275.0 4.5 %all-to-all-start.9 = ((bf16[192,4,512]{2,0,1:T(8,128)(2,1)}), bf16[192,4,512]{2,0,1:T(8,128)(2,1)}, u32[]{:S(2)}, u32[]{:S(2)}) async-start(bf16[192,4,512]{2,0,1:T(8,128)(2,1)} %bitcast.166), calls=%async_computation.9 | async-start | bytes 1572864 | tf_op jit(solution)/shard_map/all_to_all | solution.py:56
  280.2 2.0 reduce_sum.157
  283.3 5.8 %all-to-all-done.9 = bf16[192,4,512]{2,0,1:T(8,128)(2,1)} async-done(((bf16[192,4,512]{2,0,1:T(8,128)(2,1)}), bf16[192,4,512]{2,0,1:T(8,128)(2,1)}, u32[]{:S(2)}, u32[]{:S(2)}) %all-to-all-start.9) | async-done | bytes 786464 | tf_op jit(solution)/shard_map/all_to_all | solution.py:56
  289.1 2.0 reduce_sum.159
  291.1 1.7 reshape.730
  292.8 2.1 fusion.47
  294.9 9.5 %all-to-all-start.10 = ((bf16[64,7,512]{2,1,0:T(8,128)(2,1)}), bf16[64,7,512]{2,1,0:T(8,128)(2,1)}, u32[]{:S(2)}, u32[]{:S(2)}) async-start(bf16[64,7,512]{2,1,0:T(8,128)(2,1)} %fusion.47), calls=%async_computation.10 | async-start | bytes 1048576 | tf_op jit(solution)/shard_map/all_to_all | solution.py:291
  304.5 17.1 %all-to-all-done.10 = bf16[64,7,512]{2,1,0:T(8,128)(2,1)} async-done(((bf16[64,7,512]{2,1,0:T(8,128)(2,1)}), bf16[64,7,512]{2,1,0:T(8,128)(2,1)}, u32[]{:S(2)}, u32[]{:S(2)}) %all-to-all-start.10) | async-done | bytes 458784 | tf_op jit(solution)/shard_map/all_to_all | solution.py:291
  326.7 1.7 gather_fusion.12
  328.4 1.8 reshape.856
  330.2 1.9 multiply_reduce_fusion
  (205 shorter events, 67.8 us)
Async XLA Ops:
  0.6 25.1 %copy-start = (bf16[2048,768]{1,0:T(8,128)(2,1)S(1)}, bf16[2048,768]{1,0:T(8,128)(2,1)}, u32[]{:S(2)}) copy-start(bf16[2048,768]{1,0:T(8,128)(2,1)} %param.24) | copy-start | bytes 9437188
  0.6 11.1 %copy-start.11 = (bf16[32,512]{1,0:T(8,128)(2,1)S(1)}, bf16[32,512]{1,0:T(8,128)(2,1)}, u32[]{:S(2)}) copy-start(bf16[32,512]{1,0:T(8,128)(2,1)} %param.22) | copy-start | bytes 98308
  24.8 0.9 copy-start.8
  25.7 4.2 %copy-start.18 = (f32[32]{0:T(128)S(1)}, f32[32]{0:T(128)}, u32[]{:S(2)}) copy-start(f32[32]{0:T(128)} %multiply_power_fusion) | copy-start | bytes 388
  31.4 5.4 %copy-start.1 = (bf16[32,576]{1,0:T(8,128)(2,1)}, bf16[32,576]{1,0:T(8,128)(2,1)S(1)}, u32[]{:S(2)}) copy-start(bf16[32,576]{1,0:T(8,128)(2,1)S(1)} %pad_maximum_fusion.4) | copy-start | bytes 110596
  35.2 18.1 %copy-start.16 = (s32[32,6]{0,1:T(8,128)S(1)}, s32[32,6]{0,1:T(8,128)}, u32[]{:S(2)}) copy-start(s32[32,6]{0,1:T(8,128)} %param.34) | copy-start | bytes 2308
  39.2 34.1 %all-to-all-start = ((bf16[64,6,576]{2,1,0:T(8,128)(2,1)}), bf16[64,6,576]{2,1,0:T(8,128)(2,1)}, u32[]{:S(2)}, u32[]{:S(2)}) async-start(bf16[64,6,576]{2,1,0:T(8,128)(2,1)} %pad_maximum_fusion.1), calls=%async_computation | async-start | bytes 1310720 | tf_op jit(solution)/shard_map/all_to_all | solution.py:182
  79.8 12.9 %copy-start.9 = (bf16[32,4,576]{2,0,1:T(8,128)(2,1)}, bf16[32,4,576]{2,0,1:T(8,128)(2,1)S(1)}, u32[]{:S(2)}) copy-start(bf16[32,4,576]{2,0,1:T(8,128)(2,1)S(1)} %gather_fusion.5) | copy-start | bytes 442372
  92.4 1.8 copy-start.19
  109.0 4.4 %copy-start.15 = (s32[32,6]{1,0:T(8,128)S(1)}, s32[32,6]{1,0:T(8,128)}, u32[]{:S(2)}) copy-start(s32[32,6]{1,0:T(8,128)} %reshape.842) | copy-start | bytes 2308
  109.0 7.0 %copy-start.10 = (bf16[32,4,576]{2,0,1:T(8,128)(2,1)S(1)}, bf16[32,4,576]{2,0,1:T(8,128)(2,1)}, u32[]{:S(2)}) copy-start(bf16[32,4,576]{2,0,1:T(8,128)(2,1)} %copy-done.9) | copy-start | bytes 442372
  109.0 20.1 %all-to-all-start.1 = ((f32[32,16,513]{2,0,1:T(8,128)}), f32[32,16,513]{2,0,1:T(8,128)}, u32[]{:S(2)}, u32[]{:S(2)}) async-start(f32[32,16,513]{2,0,1:T(8,128)} %copy.310), calls=%async_computation.1 | async-start | bytes 2621440 | tf_op jit(solution)/shard_map/all_to_all | solution.py:56
  130.5 16.4 %copy-start.17 = (s32[32]{0:T(128)S(1)}, s32[32]{0:T(128)}, u32[]{:S(2)}) copy-start(s32[32]{0:T(128)} %get-tuple-element.47) | copy-start | bytes 388
  138.0 18.6 %all-to-all-start.2 = ((bf16[64,2,256]{2,1,0:T(2,128)(2,1)}), bf16[64,2,256]{2,1,0:T(2,128)(2,1)S(1)}, u32[]{:S(2)}, u32[]{:S(2)}) async-start(bf16[64,2,256]{2,1,0:T(2,128)(2,1)} %reshape.886), calls=%async_computation.2 | async-start | bytes 131072 | tf_op jit(solution)/shard_map/all_to_all | solution.py:215
  160.1 9.5 %all-to-all-start.3 = ((f32[32,4,512]{2,0,1:T(8,128)}), f32[32,4,512]{2,0,1:T(8,128)S(1)}, u32[]{:S(2)}, u32[]{:S(2)}) async-start(f32[32,4,512]{2,0,1:T(8,128)} %bitcast.183), calls=%async_computation.3 | async-start | bytes 524288 | tf_op jit(solution)/shard_map/all_to_all | solution.py:56
  169.6 1.9 copy-start.12
  169.6 8.4 %copy-start.13 = (s32[64,3]{1,0:T(8,128)S(1)}, s32[64,3]{1,0:T(8,128)}, u32[]{:S(2)}) copy-start(s32[64,3]{1,0:T(8,128)} %get-tuple-element.61) | copy-start | bytes 2308
  171.4 18.5 %all-to-all-start.4 = ((bf16[64,3,512]{2,1,0:T(4,128)(2,1)}), bf16[64,3,512]{2,1,0:T(4,128)(2,1)}, u32[]{:S(2)}, u32[]{:S(2)}) async-start(bf16[64,3,512]{2,1,0:T(4,128)(2,1)} %reshape.808), calls=%async_computation.4 | async-start | bytes 524288 | tf_op jit(solution)/shard_map/all_to_all | solution.py:242
  189.9 18.1 %all-to-all-start.7 = ((bf16[64,3,512]{2,1,0:T(4,128)(2,1)}), bf16[64,3,512]{2,1,0:T(4,128)(2,1)S(1)}, u32[]{:S(2)}, u32[]{:S(2)}) async-start(bf16[64,3,512]{2,1,0:T(4,128)(2,1)} %reshape.816), calls=%async_computation.7 | async-start | bytes 524288 | tf_op jit(solution)/shard_map/all_to_all | solution.py:242
  209.9 16.2 %all-to-all-start.5 = ((bf16[4,192,512]{2,1,0:T(8,128)(2,1)}), bf16[4,192,512]{2,1,0:T(8,128)(2,1)}, u32[]{:S(2)}, u32[]{:S(2)}) async-start(bf16[4,192,512]{2,1,0:T(8,128)(2,1)} %broadcast_in_dim.163), calls=%async_computation.5 | async-start | bytes 1572864 | tf_op jit(solution)/shard_map/all_to_all | solution.py:245
  228.0 15.3 %all-to-all-start.8 = ((bf16[4,192,512]{2,1,0:T(8,128)(2,1)}), bf16[4,192,512]{2,1,0:T(8,128)(2,1)}, u32[]{:S(2)}, u32[]{:S(2)}) async-start(bf16[4,192,512]{2,1,0:T(8,128)(2,1)} %broadcast_in_dim.166), calls=%async_computation.8 | async-start | bytes 1572864 | tf_op jit(solution)/shard_map/all_to_all | solution.py:245
  247.7 1.7 copy-start.2
  248.5 0.9 copy-start.4
  256.5 18.6 %all-to-all-start.6 = ((bf16[192,4,512]{2,0,1:T(8,128)(2,1)}), bf16[192,4,512]{2,0,1:T(8,128)(2,1)}, u32[]{:S(2)}, u32[]{:S(2)}) async-start(bf16[192,4,512]{2,0,1:T(8,128)(2,1)} %bitcast.167), calls=%async_computation.6 | async-start | bytes 1572864 | tf_op jit(solution)/shard_map/all_to_all | solution.py:56
  263.1 2.9 copy-start.7
  266.0 1.7 copy-start.3
  266.8 0.9 copy-start.5
  272.6 2.2 copy-start.6
  275.0 14.0 %all-to-all-start.9 = ((bf16[192,4,512]{2,0,1:T(8,128)(2,1)}), bf16[192,4,512]{2,0,1:T(8,128)(2,1)}, u32[]{:S(2)}, u32[]{:S(2)}) async-start(bf16[192,4,512]{2,0,1:T(8,128)(2,1)} %bitcast.166), calls=%async_computation.9 | async-start | bytes 1572864 | tf_op jit(solution)/shard_map/all_to_all | solution.py:56
  283.3 21.2 %copy-start.14 = (s32[32,6]{1,0:T(8,128)S(1)}, s32[32,6]{1,0:T(8,128)}, u32[]{:S(2)}) copy-start(s32[32,6]{1,0:T(8,128)} %get-tuple-element.45) | copy-start | bytes 2308
  294.9 26.7 %all-to-all-start.10 = ((bf16[64,7,512]{2,1,0:T(8,128)(2,1)}), bf16[64,7,512]{2,1,0:T(8,128)(2,1)}, u32[]{:S(2)}, u32[]{:S(2)}) async-start(bf16[64,7,512]{2,1,0:T(8,128)(2,1)} %fusion.47), calls=%async_computation.10 | async-start | bytes 1048576 | tf_op jit(solution)/shard_map/all_to_all | solution.py:291

commit v9 on v4

--- a/solution.py
+++ b/solution.py
@@ -237,16 +237,9 @@
         concat_axis=0,
         tiled=True,
     )
-    expert_in = lax.all_to_all(
-        jnp.broadcast_to(
-            arrived.reshape(1, peer_count * capacity, quarter_width),
-            (head_count, peer_count * capacity, quarter_width),
-        ),
-        "head",
-        split_axis=0,
-        concat_axis=2,
-        tiled=True,
-    ).reshape(peer_count * capacity, head_count * quarter_width)
+    expert_in = lax.all_gather(
+        arrived.reshape(peer_count * capacity, quarter_width), "head", axis=1, tiled=True
+    )
     gate_value = jnp.dot(expert_in, expert_gate[0], preferred_element_type=jnp.float32)
     up_value = jnp.dot(expert_in, expert_up[0], preferred_element_type=jnp.float32)
     activity = (jax.nn.silu(gate_value) * up_value).astype(jnp.bfloat16)

time: 311 us -> 329 us (1.058)
  waiting for transfers between devices: 80.1 us -> 105 us
  blocking collectives: 87.3 us -> 64.3 us
  between operations: 1.21 us -> 14.6 us
  starting transfers between devices: 43.4 us -> 47.3 us
    all_gather x0 -> x1, waiting for transfers between devices: none -> 24.4 us  [body(): lax.all_gather(arrived.reshape(peer_count * capacity, quarter_width), 'he...]
    all_to_all x1 -> x0, blocking collectives: 23 us -> none  [body(): lax.all_to_all(jnp.broadcast_to(arrived.reshape(1, peer_count * capacity,...]
    all_to_all x1, starting transfers between devices: 8.06 us -> 11.9 us  [body(): lax.all_to_all(expert_share.reshape(peer_count, capacity, quarter_width),...]
  transfers between devices with their start and end apart: 6 -> 7, of which waited for: 6 -> 7; matrix products, arithmetic and copies ran while one was open for 3% -> 2% of each run, Pallas kernels for 0% -> 0%
where the time goes in v9:
time: 329 us; the launch traced here: 327 us
  waiting for transfers between devices  105 us (32%)
  blocking collectives  64.3 us (20%)
  local copies, waits for them, and re-layouts  47.8 us (15%)
  starting transfers between devices  47.3 us (14%)
  matrix products  25.6 us (8%)
  other arithmetic  23 us (7%)
  between operations  14.6 us (4%)
    all_to_all x3, waiting for transfers between devices, head_sum_scatter(): lax.all_to_all(values, 'head', split_axis=axis, concat_axis=0, tiled=True)  38.1 us
    all_to_all x1, blocking collectives, body(): lax.all_to_all(padded_rows[source_token].reshape(expert_count, capacity,...  27.4 us
    all_gather x1, waiting for transfers between devices, body(): lax.all_gather(arrived.reshape(peer_count * capacity, quarter_width), 'he...  24.4 us
    all_to_all x1, waiting for transfers between devices, body(): got_packed = lax.all_to_all(packed, 'tok', 0, 0, tiled=True)  17.3 us
    all_to_all x1, waiting for transfers between devices, body(): lax.all_to_all(expert_share.reshape(peer_count, capacity, quarter_width),...  15.5 us
    all_to_all x1, starting transfers between devices, body(): got_packed = lax.all_to_all(packed, 'tok', 0, 0, tiled=True)  14.1 us
    all_gather x1, blocking collectives, body(): got_rows = lax.all_gather(send_rows, 'head', axis=0, tiled=False)  12.5 us
    all_to_all x3, starting transfers between devices, head_sum_scatter(): lax.all_to_all(values, 'head', split_axis=axis, concat_axis=0, tiled=True)  12.3 us
  transfers between devices with their start and end apart: 7, of which 7 were waited for; matrix products, arithmetic and copies ran while one was open for 2% of the time, Pallas kernels for 0%

profile of v9, /device:TPU:1, one launch (start us, length us, event | category | flops | bytes accessed | tf_op | source)
XLA Modules:
  0.0 327.4 jit_solution(5464943514680004543)
XLA Ops:
  9.5 1.2 compare_select_fusion.5
  11.1 1.4 gather_fusion.3
  12.5 1.4 gather_fusion.2
  15.4 1.4 fusion.39
  16.9 12.5 %all-gather = bf16[128,2432]{1,0:T(8,128)(2,1)S(1)} all-gather(bf16[32,2432]{1,0:T(8,128)(2,1)S(1)} %concatenate.33), channel_id=2, replica_groups=mesh['tok'=64,'head'=4] {'head'}, dimensions={0}, use_global_device_ids=true | all-gather | bytes 778240 | tf_op jit(solution)/shard_map/all_gather | solution.py:112
  34.4 1.4 multiply_cosine_fusion
  37.4 1.3 fusion.16
  39.7 1.6 gather_fusion
  41.2 2.5 pad_maximum_fusion.1
  43.7 14.1 %all-to-all-start = ((bf16[64,6,576]{2,1,0:T(8,128)(2,1)}), bf16[64,6,576]{2,1,0:T(8,128)(2,1)}, u32[]{:S(2)}, u32[]{:S(2)}) async-start(bf16[64,6,576]{2,1,0:T(8,128)(2,1)} %pad_maximum_fusion.1), calls=%async_computation | async-start | bytes 1310720 | tf_op jit(solution)/shard_map/all_to_all | solution.py:164
  58.2 1.6 gather_fusion.11
  60.6 17.3 %all-to-all-done = bf16[64,6,576]{2,1,0:T(8,128)(2,1)} async-done(((bf16[64,6,576]{2,1,0:T(8,128)(2,1)}), bf16[64,6,576]{2,1,0:T(8,128)(2,1)}, u32[]{:S(2)}, u32[]{:S(2)}) %all-to-all-start) | async-done | bytes 442400 | tf_op jit(solution)/shard_map/all_to_all | solution.py:164
  80.3 1.9 copy.269
  82.2 2.1 gather_fusion.5
  84.4 12.1 %all_gather.14 = bf16[32,16,576]{2,0,1:T(8,128)(2,1)S(1)} all-gather(bf16[32,4,576]{2,0,1:T(8,128)(2,1)S(1)} %gather_fusion.5), channel_id=1, replica_groups=mesh['tok'=64,'head'=4] {'head'}, dimensions={1}, use_global_device_ids=true | all-gather | bytes 737280 | tf_op jit(solution)/shard_map/all_gather | solution.py:174
  97.2 1.4 copy.273
  98.7 4.5 %convert_reduce_fusion = (f32[512]{0:T(512)S(1)}, bf16[512,2496]{0,1:T(8,128)(2,1)}) fusion(pred[512,2496]{0,1:T(32,128)(4,1)S(1)} %copy.273, bf16[512,576]{1,0:T(8,128)(2,1)S(1)} %bitcast.112, bf16[2496,576]{0,1:T(8,128)(2,1)S(1)} %copy-done.12), kind=kOutput, calls=%fused_computation.13 | convolution fusion | flops 1478589952 | bytes 7301120 | tf_op jit(solution)/shard_map/qc,pc->qp/dot_general | solution.py:39
  103.4 4.4 %copy.271 = bf16[512,2496]{1,0:T(8,128)(2,1)} copy(bf16[512,2496]{0,1:T(8,128)(2,1)} %get-tuple-element.52) | data formatting | bytes 5111808 | tf_op jit(solution)/shard_map/exp | solution.py:46
  107.8 4.1 %fusion = f32[32,16,512]{2,1,0:T(8,128)S(1)} fusion(bf16[32,16,2496]{2,1,0:T(8,128)(2,1)} %bitcast.106, bf16[2496,576]{0,1:T(8,128)(2,1)} %param.25, pred[32,2496]{1,0:T(8,128)(4,1)S(1)} %compare_and_fusion), kind=kOutput, calls=%fused_computation.17 | convolution fusion | flops 1309900800 | bytes 6371328 | tf_op jit(solution)/shard_map/khp,pl->khl/dot_general | solution.py:47
  112.0 1.5 copy.275
  113.5 4.4 %all-to-all-start.1 = ((f32[32,16,513]{2,0,1:T(8,128)}), f32[32,16,513]{2,0,1:T(8,128)}, u32[]{:S(2)}, u32[]{:S(2)}) async-start(f32[32,16,513]{2,0,1:T(8,128)} %copy.275), calls=%async_computation.1 | async-start | bytes 2621440 | tf_op jit(solution)/shard_map/all_to_all | solution.py:56
  118.5 1.8 gather_fusion.6
  121.3 12.2 %all-to-all-done.1 = f32[32,16,513]{2,0,1:T(8,128)} async-done(((f32[32,16,513]{2,0,1:T(8,128)}), f32[32,16,513]{2,0,1:T(8,128)}, u32[]{:S(2)}, u32[]{:S(2)}) %all-to-all-start.1) | async-done | bytes 1050656 | tf_op jit(solution)/shard_map/all_to_all | solution.py:56
  133.6 1.4 reduce_sum.141
  137.5 1.2 fusion.31
  138.7 1.2 fusion.18
  142.5 8.9 %all-to-all-start.2 = ((bf16[64,2,256]{2,1,0:T(2,128)(2,1)}), bf16[64,2,256]{2,1,0:T(2,128)(2,1)S(1)}, u32[]{:S(2)}, u32[]{:S(2)}) async-start(bf16[64,2,256]{2,1,0:T(2,128)(2,1)} %reshape.634), calls=%async_computation.2 | async-start | bytes 131072 | tf_op jit(solution)/shard_map/all_to_all | solution.py:197
  151.6 9.5 %all-to-all-done.2 = bf16[64,2,256]{2,1,0:T(2,128)(2,1)S(1)} async-done(((bf16[64,2,256]{2,1,0:T(2,128)(2,1)}), bf16[64,2,256]{2,1,0:T(2,128)(2,1)S(1)}, u32[]{:S(2)}, u32[]{:S(2)}) %all-to-all-start.2) | async-done | bytes 65568 | tf_op jit(solution)/shard_map/all_to_all | solution.py:197
  161.9 2.1 fusion.73
  164.6 3.4 %all-to-all-start.3 = ((f32[32,4,512]{2,0,1:T(8,128)}), f32[32,4,512]{2,0,1:T(8,128)S(1)}, u32[]{:S(2)}, u32[]{:S(2)}) async-start(f32[32,4,512]{2,0,1:T(8,128)} %bitcast.111), calls=%async_computation.3 | async-start | bytes 524288 | tf_op jit(solution)/shard_map/all_to_all | solution.py:56
  168.1 6.0 %all-to-all-done.3 = f32[32,4,512]{2,0,1:T(8,128)S(1)} async-done(((f32[32,4,512]{2,0,1:T(8,128)}), f32[32,4,512]{2,0,1:T(8,128)S(1)}, u32[]{:S(2)}, u32[]{:S(2)}) %all-to-all-start.3) | async-done | bytes 262176 | tf_op jit(solution)/shard_map/all_to_all | solution.py:56
  175.2 12.3 %all-reduce.5 = (f32[32]{0:T(128)S(1)}, f32[32,64]{1,0:T(8,128)}) all-reduce(f32[32]{0:T(128)S(1)} %get-tuple-element.25, f32[32,64]{1,0:T(8,128)S(1)} %fusion.49), channel_id=1, replica_groups=mesh['tok'=64,'head'=4] {'head'}, use_global_device_ids=true, to_apply=%region_13.14 | all-reduce | flops 2080 | bytes 16640 | tf_op jit(solution)/shard_map/psum | solution.py:203
  187.6 2.6 gather_fusion.9
  190.2 1.9 reshape.520
  192.1 27.4 %all_to_all.65 = bf16[64,6,512]{2,1,0:T(8,128)(2,1)} all-to-all(bf16[64,6,512]{2,1,0:T(8,128)(2,1)} %reshape.520), channel_id=1, replica_groups=mesh['tok'=64,'head'=4] {'tok'}, dimensions={0} | all-to-all | bytes 786432 | tf_op jit(solution)/shard_map/all_to_all | solution.py:233
  219.5 1.9 reshape.521
  221.5 24.4 %all-gather.3.cloned.1.call-done = bf16[384,2048]{1,0:T(8,128)(2,1)} async-done(((bf16[384,512]{1,0:T(8,128)(2,1)}), bf16[384,2048]{1,0:T(8,128)(2,1)}) %all-gather.3.cloned.1.call-update) | async-done | bytes 1572880 | tf_op jit(solution)/shard_map/all_gather | solution.py:240
  245.9 3.6 %fusion.8 = f32[384,352]{0,1:T(8,128)} fusion(bf16[384,2048]{1,0:T(8,128)(2,1)} %all-gather.3.cloned.1.call-done, bf16[1,2048,352]{1,2,0:T(8,128)(2,1)} %param.31), kind=kOutput, calls=%fused_computation.26 | convolution fusion | flops 553648128 | bytes 3555328 | tf_op jit(solution)/shard_map/dot_general | solution.py:243
  249.5 5.5 %convolution_convert_fusion = bf16[384,2048]{1,0:T(8,128)(2,1)} fusion(bf16[1,352,2048]{2,1,0:T(8,128)(2,1)} %param.33, bf16[384,2048]{1,0:T(8,128)(2,1)} %all-gather.3.cloned.1.call-done, bf16[1,2048,352]{1,2,0:T(8,128)(2,1)} %param.32, f32[384,352]{0,1:T(8,128)} %fusion.8), kind=kOutput, calls=%fused_computation.16 | convolution fusion | flops 1108893696 | bytes 6569984 | tf_op jit(solution)/shard_map/dot_general | solution.py:247
  255.0 2.7 copy.326
  257.7 4.5 %all-to-all-start.5 = ((bf16[384,4,512]{2,0,1:T(8,128)(2,1)}), bf16[384,4,512]{2,0,1:T(8,128)(2,1)}, u32[]{:S(2)}, u32[]{:S(2)}) async-start(bf16[384,4,512]{2,0,1:T(8,128)(2,1)} %bitcast.101), calls=%async_computation.5 | async-start | bytes 3145728 | tf_op jit(solution)/shard_map/all_to_all | solution.py:56
  262.3 19.9 %all-to-all-done.5 = bf16[384,4,512]{2,0,1:T(8,128)(2,1)} async-done(((bf16[384,4,512]{2,0,1:T(8,128)(2,1)}), bf16[384,4,512]{2,0,1:T(8,128)(2,1)}, u32[]{:S(2)}, u32[]{:S(2)}) %all-to-all-start.5) | async-done | bytes 1572896 | tf_op jit(solution)/shard_map/all_to_all | solution.py:56
  282.2 1.8 reduce_sum.147
  284.9 11.9 %all-to-all-start.6 = ((bf16[64,6,512]{2,1,0:T(8,128)(2,1)}), bf16[64,6,512]{2,1,0:T(8,128)(2,1)}, u32[]{:S(2)}, u32[]{:S(2)}) async-start(bf16[64,6,512]{2,1,0:T(8,128)(2,1)} %reshape.522), calls=%async_computation.6 | async-start | bytes 1048576 | tf_op jit(solution)/shard_map/all_to_all | solution.py:250
  298.6 15.5 %all-to-all-done.6 = bf16[64,6,512]{2,1,0:T(8,128)(2,1)} async-done(((bf16[64,6,512]{2,1,0:T(8,128)(2,1)}), bf16[64,6,512]{2,1,0:T(8,128)(2,1)}, u32[]{:S(2)}, u32[]{:S(2)}) %all-to-all-start.6) | async-done | bytes 393248 | tf_op jit(solution)/shard_map/all_to_all | solution.py:250
  315.2 1.7 gather_fusion.10
  316.9 1.8 reshape.618
  318.7 1.9 multiply_reduce_fusion
  (135 shorter events, 29.7 us)
Async XLA Ops:
  7.2 23.1 %copy-start = (bf16[2048,768]{1,0:T(8,128)(2,1)S(1)}, bf16[2048,768]{1,0:T(8,128)(2,1)}, u32[]{:S(2)}) copy-start(bf16[2048,768]{1,0:T(8,128)(2,1)} %param.20) | copy-start | bytes 9437188
  7.2 9.6 %copy-start.5 = (bf16[32,512]{1,0:T(8,128)(2,1)S(1)}, bf16[32,512]{1,0:T(8,128)(2,1)}, u32[]{:S(2)}) copy-start(bf16[32,512]{1,0:T(8,128)(2,1)} %param.18) | copy-start | bytes 98308
  30.3 4.1 %copy-start.11 = (f32[32]{0:T(128)S(1)}, f32[32]{0:T(128)}, u32[]{:S(2)}) copy-start(f32[32]{0:T(128)} %multiply_power_fusion) | copy-start | bytes 388
  35.9 5.4 %copy-start.1 = (bf16[32,576]{1,0:T(8,128)(2,1)}, bf16[32,576]{1,0:T(8,128)(2,1)S(1)}, u32[]{:S(2)}) copy-start(bf16[32,576]{1,0:T(8,128)(2,1)S(1)} %pad_maximum_fusion.3) | copy-start | bytes 110596
  39.7 18.2 %copy-start.8 = (s32[32,6]{0,1:T(8,128)S(1)}, s32[32,6]{0,1:T(8,128)}, u32[]{:S(2)}) copy-start(s32[32,6]{0,1:T(8,128)} %param.30) | copy-start | bytes 2308
  43.7 34.2 %all-to-all-start = ((bf16[64,6,576]{2,1,0:T(8,128)(2,1)}), bf16[64,6,576]{2,1,0:T(8,128)(2,1)}, u32[]{:S(2)}, u32[]{:S(2)}) async-start(bf16[64,6,576]{2,1,0:T(8,128)(2,1)} %pad_maximum_fusion.1), calls=%async_computation | async-start | bytes 1310720 | tf_op jit(solution)/shard_map/all_to_all | solution.py:164
  84.4 12.8 %copy-start.2 = (bf16[32,4,576]{2,0,1:T(8,128)(2,1)}, bf16[32,4,576]{2,0,1:T(8,128)(2,1)S(1)}, u32[]{:S(2)}) copy-start(bf16[32,4,576]{2,0,1:T(8,128)(2,1)S(1)} %gather_fusion.5) | copy-start | bytes 442372
  96.8 1.8 copy-start.12
  113.5 4.4 %copy-start.7 = (s32[32,6]{1,0:T(8,128)S(1)}, s32[32,6]{1,0:T(8,128)}, u32[]{:S(2)}) copy-start(s32[32,6]{1,0:T(8,128)} %reshape.611) | copy-start | bytes 2308
  113.5 6.8 %copy-start.3 = (bf16[32,4,576]{2,0,1:T(8,128)(2,1)S(1)}, bf16[32,4,576]{2,0,1:T(8,128)(2,1)}, u32[]{:S(2)}) copy-start(bf16[32,4,576]{2,0,1:T(8,128)(2,1)} %copy-done.2) | copy-start | bytes 442372
  113.5 20.1 %all-to-all-start.1 = ((f32[32,16,513]{2,0,1:T(8,128)}), f32[32,16,513]{2,0,1:T(8,128)}, u32[]{:S(2)}, u32[]{:S(2)}) async-start(f32[32,16,513]{2,0,1:T(8,128)} %copy.275), calls=%async_computation.1 | async-start | bytes 2621440 | tf_op jit(solution)/shard_map/all_to_all | solution.py:56
  135.0 16.4 %copy-start.10 = (s32[32]{0:T(128)S(1)}, s32[32]{0:T(128)}, u32[]{:S(2)}) copy-start(s32[32]{0:T(128)} %get-tuple-element.27) | copy-start | bytes 388
  142.5 18.7 %all-to-all-start.2 = ((bf16[64,2,256]{2,1,0:T(2,128)(2,1)}), bf16[64,2,256]{2,1,0:T(2,128)(2,1)S(1)}, u32[]{:S(2)}, u32[]{:S(2)}) async-start(bf16[64,2,256]{2,1,0:T(2,128)(2,1)} %reshape.634), calls=%async_computation.2 | async-start | bytes 131072 | tf_op jit(solution)/shard_map/all_to_all | solution.py:197
  161.9 12.4 %copy-start.9 = (f32[512]{0:T(512)S(1)}, f32[512]{0:T(512)}, u32[]{:S(2)}) copy-start(f32[512]{0:T(512)} %param.28) | copy-start | bytes 6148
  164.6 9.5 %all-to-all-start.3 = ((f32[32,4,512]{2,0,1:T(8,128)}), f32[32,4,512]{2,0,1:T(8,128)S(1)}, u32[]{:S(2)}, u32[]{:S(2)}) async-start(f32[32,4,512]{2,0,1:T(8,128)} %bitcast.111), calls=%async_computation.3 | async-start | bytes 524288 | tf_op jit(solution)/shard_map/all_to_all | solution.py:56
  168.1 77.8 %all-gather.3.cloned.1.call-start = ((), (), s32[]{:S(2)}) async-start(), calls=%async_computation.7 | async-start | bytes 1966080 | tf_op jit(solution)/shard_map/all_gather | solution.py:240
  174.2 13.3 %copy-start.4 = (bf16[32,512]{1,0:T(8,128)(2,1)}, bf16[32,512]{1,0:T(8,128)(2,1)S(1)}, u32[]{:S(2)}) copy-start(bf16[32,512]{1,0:T(8,128)(2,1)S(1)} %get-tuple-element.26) | copy-start | bytes 98308
  257.7 4.5 %copy-start.6 = (s32[32,6]{1,0:T(8,128)S(1)}, s32[32,6]{1,0:T(8,128)}, u32[]{:S(2)}) copy-start(s32[32,6]{1,0:T(8,128)} %get-tuple-element.23) | copy-start | bytes 2308
  257.7 24.5 %all-to-all-start.5 = ((bf16[384,4,512]{2,0,1:T(8,128)(2,1)}), bf16[384,4,512]{2,0,1:T(8,128)(2,1)}, u32[]{:S(2)}, u32[]{:S(2)}) async-start(bf16[384,4,512]{2,0,1:T(8,128)(2,1)} %bitcast.101), calls=%async_computation.5 | async-start | bytes 3145728 | tf_op jit(solution)/shard_map/all_to_all | solution.py:56
  284.9 29.1 %all-to-all-start.6 = ((bf16[64,6,512]{2,1,0:T(8,128)(2,1)}), bf16[64,6,512]{2,1,0:T(8,128)(2,1)}, u32[]{:S(2)}, u32[]{:S(2)}) async-start(bf16[64,6,512]{2,1,0:T(8,128)(2,1)} %reshape.522), calls=%async_computation.6 | async-start | bytes 1048576 | tf_op jit(solution)/shard_map/all_to_all | solution.py:250
Sparse Core Ops, SparseCore 0:
  221.6 24.2 all-gather.2

commit v10 on v4

--- a/solution.py
+++ b/solution.py
@@ -175,15 +175,18 @@
     numerator, denominator = owner_attend(
         all_heads, owner_lengths, latent_cache, head_index, factor
     )
-    joined = head_sum_scatter(jnp.concatenate([numerator, denominator[:, :, None]], axis=2), 1)
+    den_row = jnp.zeros((1, denominator.shape[1], LATENT), jnp.float32)
+    den_row = den_row.at[0, :, : denominator.shape[0]].set(denominator.T)
+    joined = head_sum_scatter(jnp.concatenate([numerator, den_row], axis=0), 1)
+    group_den = joined[local_rows, :, :local_rows].T
     self_score = factor * jnp.einsum(
         "bhc,bc->bh", owner_probes, owner_new, preferred_element_type=jnp.float32
     )
     self_weight = jnp.exp(self_score).astype(jnp.bfloat16).astype(jnp.float32)
-    total_num = joined[:, :, :LATENT] + self_weight[:, :, None] * owner_new[:, None, :LATENT].astype(
+    total_num = joined[:local_rows] + self_weight[:, :, None] * owner_new[:, None, :LATENT].astype(
         jnp.float32
     )
-    total_den = joined[:, :, LATENT] + self_weight
+    total_den = group_den + self_weight
     mixed_latent = (total_num / total_den[:, :, None]).astype(jnp.bfloat16)
     owner_out = jnp.einsum(
         "bhl,hld->bhd", mixed_latent, w_value_up, preferred_element_type=jnp.float32

time: 311 us -> 307 us (0.987)
  transfers between devices with their start and end apart: 6 -> 6, of which waited for: 6 -> 6; matrix products, arithmetic and copies ran while one was open for 3% -> 2% of each run, Pallas kernels for 0% -> 0%
where the time goes in v10:
time: 307 us; the launch traced here: 305 us
  blocking collectives  87.3 us (28%)
  waiting for transfers between devices  80.7 us (26%)
  local copies, waits for them, and re-layouts  47.4 us (15%)
  starting transfers between devices  43.3 us (14%)
  matrix products  23.8 us (8%)
  other arithmetic  21.8 us (7%)
    all_to_all x3, waiting for transfers between devices, head_sum_scatter(): lax.all_to_all(values, 'head', split_axis=axis, concat_axis=0, tiled=True)  35.8 us
    all_to_all x1, blocking collectives, body(): lax.all_to_all(padded_rows[source_token].reshape(expert_count, capacity,...  27.4 us
    all_to_all x1, blocking collectives, body(): lax.all_to_all(jnp.broadcast_to(arrived.reshape(1, peer_count * capacity,...  23 us
    all_to_all x1, waiting for transfers between devices, body(): got_packed = lax.all_to_all(packed, 'tok', 0, 0, tiled=True)  19.9 us
    all_to_all x1, waiting for transfers between devices, body(): lax.all_to_all(expert_share.reshape(peer_count, capacity, quarter_width),...  15.5 us
    all_to_all x1, starting transfers between devices, body(): got_packed = lax.all_to_all(packed, 'tok', 0, 0, tiled=True)  14.2 us
    all_gather x1, blocking collectives, body(): got_rows = lax.all_gather(send_rows, 'head', axis=0, tiled=False)  12.5 us
    psum x1, blocking collectives, body(): lax.psum((jnp.sum(attended_wide * attended_wide, axis=1), jnp.dot(gained,...  12.3 us
  transfers between devices with their start and end apart: 6, of which 6 were waited for; matrix products, arithmetic and copies ran while one was open for 2% of the time, Pallas kernels for 0%

profile of v10, /device:TPU:1, one launch (start us, length us, event | category | flops | bytes accessed | tf_op | source)
XLA Modules:
  0.0 305.5 jit_solution(9807414722102676474)
XLA Ops:
  3.0 1.2 compare_select_fusion.5
  4.6 1.4 gather_fusion.3
  6.0 1.4 gather_fusion.2
  8.9 1.4 fusion.42
  10.4 12.5 %all-gather = bf16[128,2432]{1,0:T(8,128)(2,1)S(1)} all-gather(bf16[32,2432]{1,0:T(8,128)(2,1)S(1)} %concatenate.35), channel_id=2, replica_groups=mesh['tok'=64,'head'=4] {'head'}, dimensions={0}, use_global_device_ids=true | all-gather | bytes 778240 | tf_op jit(solution)/shard_map/all_gather | solution.py:112
  27.9 1.4 multiply_cosine_fusion
  30.9 1.3 fusion.16
  33.1 1.6 gather_fusion
  34.7 2.5 pad_maximum_fusion
  37.2 14.2 %all-to-all-start = ((bf16[64,6,576]{2,1,0:T(8,128)(2,1)}), bf16[64,6,576]{2,1,0:T(8,128)(2,1)}, u32[]{:S(2)}, u32[]{:S(2)}) async-start(bf16[64,6,576]{2,1,0:T(8,128)(2,1)} %pad_maximum_fusion), calls=%async_computation | async-start | bytes 1310720 | tf_op jit(solution)/shard_map/all_to_all | solution.py:164
  51.5 19.9 %all-to-all-done = bf16[64,6,576]{2,1,0:T(8,128)(2,1)} async-done(((bf16[64,6,576]{2,1,0:T(8,128)(2,1)}), bf16[64,6,576]{2,1,0:T(8,128)(2,1)}, u32[]{:S(2)}, u32[]{:S(2)}) %all-to-all-start) | async-done | bytes 442400 | tf_op jit(solution)/shard_map/all_to_all | solution.py:164
  73.8 1.9 copy.311
  75.7 2.1 gather_fusion.5
  77.8 12.1 %all_gather.11 = bf16[32,16,576]{2,0,1:T(8,128)(2,1)S(1)} all-gather(bf16[32,4,576]{2,0,1:T(8,128)(2,1)S(1)} %gather_fusion.5), channel_id=1, replica_groups=mesh['tok'=64,'head'=4] {'head'}, dimensions={1}, use_global_device_ids=true | all-gather | bytes 737280 | tf_op jit(solution)/shard_map/all_gather | solution.py:174
  90.7 1.4 copy.315
  92.1 4.5 %convert_reduce_fusion = (f32[512]{0:T(512)S(1)}, bf16[512,2496]{0,1:T(8,128)(2,1)}) fusion(pred[512,2496]{0,1:T(32,128)(4,1)S(1)} %copy.315, bf16[512,576]{1,0:T(8,128)(2,1)S(1)} %bitcast.123, bf16[2496,576]{0,1:T(8,128)(2,1)S(1)} %copy-done.10), kind=kOutput, calls=%fused_computation.13 | convolution fusion | flops 1478589952 | bytes 7301120 | tf_op jit(solution)/shard_map/qc,pc->qp/dot_general | solution.py:39
  96.8 4.4 %copy.313 = bf16[512,2496]{1,0:T(8,128)(2,1)} copy(bf16[512,2496]{0,1:T(8,128)(2,1)} %get-tuple-element.64) | data formatting | bytes 5111808 | tf_op jit(solution)/shard_map/exp | solution.py:46
  101.2 4.1 %fusion = f32[32,16,512]{2,1,0:T(8,128)S(1)} fusion(bf16[32,16,2496]{2,1,0:T(8,128)(2,1)} %bitcast.115, bf16[2496,576]{0,1:T(8,128)(2,1)} %param.27, pred[32,2496]{1,0:T(8,128)(4,1)S(1)} %compare_and_fusion), kind=kOutput, calls=%fused_computation.17 | convolution fusion | flops 1309900800 | bytes 6371328 | tf_op jit(solution)/shard_map/khp,pl->khl/dot_general | solution.py:47
  105.4 1.7 copy.317
  107.1 4.3 %all-to-all-start.1 = ((f32[33,16,512]{2,0,1:T(8,128)}), f32[33,16,512]{2,0,1:T(8,128)}, u32[]{:S(2)}, u32[]{:S(2)}) async-start(f32[33,16,512]{2,0,1:T(8,128)} %copy.317), calls=%async_computation.1 | async-start | bytes 2621440 | tf_op jit(solution)/shard_map/all_to_all | solution.py:56
  111.7 1.6 gather_fusion.11
  114.0 1.8 gather_fusion.6
  116.8 10.2 %all-to-all-done.1 = f32[33,16,512]{2,0,1:T(8,128)} async-done(((f32[33,16,512]{2,0,1:T(8,128)}), f32[33,16,512]{2,0,1:T(8,128)}, u32[]{:S(2)}, u32[]{:S(2)}) %all-to-all-start.1) | async-done | bytes 1081376 | tf_op jit(solution)/shard_map/all_to_all | solution.py:56
  127.1 1.5 reduce_sum.144
  128.6 1.3 fusion.18
  132.5 8.9 %all-to-all-start.2 = ((bf16[64,2,256]{2,1,0:T(2,128)(2,1)}), bf16[64,2,256]{2,1,0:T(2,128)(2,1)S(1)}, u32[]{:S(2)}, u32[]{:S(2)}) async-start(bf16[64,2,256]{2,1,0:T(2,128)(2,1)} %reshape.673), calls=%async_computation.2 | async-start | bytes 131072 | tf_op jit(solution)/shard_map/all_to_all | solution.py:200
  141.6 9.5 %all-to-all-done.2 = bf16[64,2,256]{2,1,0:T(2,128)(2,1)S(1)} async-done(((bf16[64,2,256]{2,1,0:T(2,128)(2,1)}), bf16[64,2,256]{2,1,0:T(2,128)(2,1)S(1)}, u32[]{:S(2)}, u32[]{:S(2)}) %all-to-all-start.2) | async-done | bytes 65568 | tf_op jit(solution)/shard_map/all_to_all | solution.py:200
  151.9 2.1 fusion.77
  154.7 3.4 %all-to-all-start.3 = ((f32[32,4,512]{2,0,1:T(8,128)}), f32[32,4,512]{2,0,1:T(8,128)S(1)}, u32[]{:S(2)}, u32[]{:S(2)}) async-start(f32[32,4,512]{2,0,1:T(8,128)} %bitcast.122), calls=%async_computation.3 | async-start | bytes 524288 | tf_op jit(solution)/shard_map/all_to_all | solution.py:56
  158.1 6.0 %all-to-all-done.3 = f32[32,4,512]{2,0,1:T(8,128)S(1)} async-done(((f32[32,4,512]{2,0,1:T(8,128)}), f32[32,4,512]{2,0,1:T(8,128)S(1)}, u32[]{:S(2)}, u32[]{:S(2)}) %all-to-all-start.3) | async-done | bytes 262176 | tf_op jit(solution)/shard_map/all_to_all | solution.py:56
  165.3 12.3 %all-reduce.6 = (f32[32]{0:T(128)S(1)}, f32[32,64]{1,0:T(8,128)}) all-reduce(f32[32]{0:T(128)S(1)} %get-tuple-element.37, f32[32,64]{1,0:T(8,128)S(1)} %fusion.52), channel_id=1, replica_groups=mesh['tok'=64,'head'=4] {'head'}, use_global_device_ids=true, to_apply=%region_13.14 | all-reduce | flops 2080 | bytes 16640 | tf_op jit(solution)/shard_map/psum | solution.py:206
  177.6 2.6 gather_fusion.9
  180.2 1.9 reshape.559
  182.1 27.4 %all_to_all.80 = bf16[64,6,512]{2,1,0:T(8,128)(2,1)} all-to-all(bf16[64,6,512]{2,1,0:T(8,128)(2,1)} %reshape.559), channel_id=1, replica_groups=mesh['tok'=64,'head'=4] {'tok'}, dimensions={0} | all-to-all | bytes 786432 | tf_op jit(solution)/shard_map/all_to_all | solution.py:236
  209.6 1.2 broadcast_in_dim.156
  212.8 23.0 %all_to_all.81 = bf16[4,384,512]{1,2,0:T(8,128)(2,1)S(1)} all-to-all(bf16[4,384,512]{1,2,0:T(8,128)(2,1)S(1)} %broadcast_in_dim.157), channel_id=1, replica_groups=mesh['tok'=64,'head'=4] {'head'}, dimensions={0} | all-to-all | bytes 3145728 | tf_op jit(solution)/shard_map/all_to_all | solution.py:243
  237.0 1.7 fusion.8
  238.7 5.5 %convolution_convert_fusion = bf16[384,2048]{1,0:T(8,128)(2,1)} fusion(bf16[1,352,2048]{2,1,0:T(8,128)(2,1)} %param.35, bf16[384,2048]{0,1:T(8,128)(2,1)} %bitcast.118, bf16[1,2048,352]{1,2,0:T(8,128)(2,1)} %param.34, f32[384,352]{0,1:T(8,128)} %fusion.8), kind=kOutput, calls=%fused_computation.16 | convolution fusion | flops 1108893696 | bytes 6569984 | tf_op jit(solution)/shard_map/dot_general | solution.py:257
  244.1 2.7 copy.353
  246.8 4.5 %all-to-all-start.6 = ((bf16[384,4,512]{2,0,1:T(8,128)(2,1)}), bf16[384,4,512]{2,0,1:T(8,128)(2,1)}, u32[]{:S(2)}, u32[]{:S(2)}) async-start(bf16[384,4,512]{2,0,1:T(8,128)(2,1)} %bitcast.110), calls=%async_computation.6 | async-start | bytes 3145728 | tf_op jit(solution)/shard_map/all_to_all | solution.py:56
  251.4 19.5 %all-to-all-done.6 = bf16[384,4,512]{2,0,1:T(8,128)(2,1)} async-done(((bf16[384,4,512]{2,0,1:T(8,128)(2,1)}), bf16[384,4,512]{2,0,1:T(8,128)(2,1)}, u32[]{:S(2)}, u32[]{:S(2)}) %all-to-all-start.6) | async-done | bytes 1572896 | tf_op jit(solution)/shard_map/all_to_all | solution.py:56
  270.9 1.8 reduce_sum.150
  273.7 8.1 %all-to-all-start.7 = ((bf16[64,6,512]{2,1,0:T(8,128)(2,1)}), bf16[64,6,512]{2,1,0:T(8,128)(2,1)}, u32[]{:S(2)}, u32[]{:S(2)}) async-start(bf16[64,6,512]{2,1,0:T(8,128)(2,1)} %reshape.561), calls=%async_computation.7 | async-start | bytes 1048576 | tf_op jit(solution)/shard_map/all_to_all | solution.py:260
  283.5 15.5 %all-to-all-done.7 = bf16[64,6,512]{2,1,0:T(8,128)(2,1)} async-done(((bf16[64,6,512]{2,1,0:T(8,128)(2,1)}), bf16[64,6,512]{2,1,0:T(8,128)(2,1)}, u32[]{:S(2)}, u32[]{:S(2)}) %all-to-all-start.7) | async-done | bytes 393248 | tf_op jit(solution)/shard_map/all_to_all | solution.py:260
  299.0 1.2 reshape.562
  300.2 1.7 gather_fusion.10
  301.8 1.8 reshape.657
  303.6 1.9 multiply_reduce_fusion
  (129 shorter events, 28.5 us)
Async XLA Ops:
  0.6 23.1 %copy-start = (bf16[2048,768]{1,0:T(8,128)(2,1)S(1)}, bf16[2048,768]{1,0:T(8,128)(2,1)}, u32[]{:S(2)}) copy-start(bf16[2048,768]{1,0:T(8,128)(2,1)} %param.22) | copy-start | bytes 9437188
  0.6 9.6 %copy-start.4 = (bf16[32,512]{1,0:T(8,128)(2,1)S(1)}, bf16[32,512]{1,0:T(8,128)(2,1)}, u32[]{:S(2)}) copy-start(bf16[32,512]{1,0:T(8,128)(2,1)} %param.20) | copy-start | bytes 98308
  23.7 4.1 %copy-start.9 = (f32[32]{0:T(128)S(1)}, f32[32]{0:T(128)}, u32[]{:S(2)}) copy-start(f32[32]{0:T(128)} %multiply_power_fusion) | copy-start | bytes 388
  29.4 5.4 %copy-start.1 = (bf16[32,576]{1,0:T(8,128)(2,1)}, bf16[32,576]{1,0:T(8,128)(2,1)S(1)}, u32[]{:S(2)}) copy-start(bf16[32,576]{1,0:T(8,128)(2,1)S(1)} %pad_maximum_fusion.2) | copy-start | bytes 110596
  33.1 18.2 %copy-start.6 = (s32[32,6]{0,1:T(8,128)S(1)}, s32[32,6]{0,1:T(8,128)}, u32[]{:S(2)}) copy-start(s32[32,6]{0,1:T(8,128)} %param.32) | copy-start | bytes 2308
  37.2 34.2 %all-to-all-start = ((bf16[64,6,576]{2,1,0:T(8,128)(2,1)}), bf16[64,6,576]{2,1,0:T(8,128)(2,1)}, u32[]{:S(2)}, u32[]{:S(2)}) async-start(bf16[64,6,576]{2,1,0:T(8,128)(2,1)} %pad_maximum_fusion), calls=%async_computation | async-start | bytes 1310720 | tf_op jit(solution)/shard_map/all_to_all | solution.py:164
  90.3 1.8 copy-start.10
  107.1 19.9 %all-to-all-start.1 = ((f32[33,16,512]{2,0,1:T(8,128)}), f32[33,16,512]{2,0,1:T(8,128)}, u32[]{:S(2)}, u32[]{:S(2)}) async-start(f32[33,16,512]{2,0,1:T(8,128)} %copy.317), calls=%async_computation.1 | async-start | bytes 2621440 | tf_op jit(solution)/shard_map/all_to_all | solution.py:56
  128.6 12.8 %copy-start.8 = (s32[32]{0:T(128)S(1)}, s32[32]{0:T(128)}, u32[]{:S(2)}) copy-start(s32[32]{0:T(128)} %get-tuple-element.39) | copy-start | bytes 388
  132.5 18.7 %all-to-all-start.2 = ((bf16[64,2,256]{2,1,0:T(2,128)(2,1)}), bf16[64,2,256]{2,1,0:T(2,128)(2,1)S(1)}, u32[]{:S(2)}, u32[]{:S(2)}) async-start(bf16[64,2,256]{2,1,0:T(2,128)(2,1)} %reshape.673), calls=%async_computation.2 | async-start | bytes 131072 | tf_op jit(solution)/shard_map/all_to_all | solution.py:200
  151.9 12.4 %copy-start.7 = (f32[512]{0:T(512)S(1)}, f32[512]{0:T(512)}, u32[]{:S(2)}) copy-start(f32[512]{0:T(512)} %param.30) | copy-start | bytes 6148
  154.7 9.5 %all-to-all-start.3 = ((f32[32,4,512]{2,0,1:T(8,128)}), f32[32,4,512]{2,0,1:T(8,128)S(1)}, u32[]{:S(2)}, u32[]{:S(2)}) async-start(f32[32,4,512]{2,0,1:T(8,128)} %bitcast.122), calls=%async_computation.3 | async-start | bytes 524288 | tf_op jit(solution)/shard_map/all_to_all | solution.py:56
  164.3 13.3 %copy-start.3 = (bf16[32,512]{1,0:T(8,128)(2,1)}, bf16[32,512]{1,0:T(8,128)(2,1)S(1)}, u32[]{:S(2)}) copy-start(bf16[32,512]{1,0:T(8,128)(2,1)S(1)} %get-tuple-element.38) | copy-start | bytes 98308
  212.8 24.2 %copy-start.11 = (bf16[1,2048,352]{1,2,0:T(8,128)(2,1)S(1)}, bf16[1,2048,352]{1,2,0:T(8,128)(2,1)}, u32[]{:S(2)}) copy-start(bf16[1,2048,352]{1,2,0:T(8,128)(2,1)} %param.33) | copy-start | bytes 4325380
  235.8 1.1 copy-start.2
  246.8 4.5 %copy-start.5 = (s32[32,6]{1,0:T(8,128)S(1)}, s32[32,6]{1,0:T(8,128)}, u32[]{:S(2)}) copy-start(s32[32,6]{1,0:T(8,128)} %get-tuple-element.35) | copy-start | bytes 2308
  246.8 24.1 %all-to-all-start.6 = ((bf16[384,4,512]{2,0,1:T(8,128)(2,1)}), bf16[384,4,512]{2,0,1:T(8,128)(2,1)}, u32[]{:S(2)}, u32[]{:S(2)}) async-start(bf16[384,4,512]{2,0,1:T(8,128)(2,1)} %bitcast.110), calls=%async_computation.6 | async-start | bytes 3145728 | tf_op jit(solution)/shard_map/all_to_all | solution.py:56
  273.7 25.3 %all-to-all-start.7 = ((bf16[64,6,512]{2,1,0:T(8,128)(2,1)}), bf16[64,6,512]{2,1,0:T(8,128)(2,1)}, u32[]{:S(2)}, u32[]{:S(2)}) async-start(bf16[64,6,512]{2,1,0:T(8,128)(2,1)} %reshape.561), calls=%async_computation.7 | async-start | bytes 1048576 | tf_op jit(solution)/shard_map/all_to_all | solution.py:260

commit v11 on v10

--- a/solution.py
+++ b/solution.py
@@ -234,7 +234,7 @@
         [normed_ffn, jnp.zeros((1, normed_ffn.shape[1]), jnp.bfloat16)], axis=0
     )
     arrived = lax.all_to_all(
-        padded_rows[source_token].reshape(expert_count, capacity, quarter_width),
+        padded_rows[source_token].reshape(expert_count, capacity * quarter_width),
         "tok",
         split_axis=0,
         concat_axis=0,
@@ -258,7 +258,7 @@
         1,
     ).astype(jnp.bfloat16)
     returned = lax.all_to_all(
-        expert_share.reshape(peer_count, capacity, quarter_width),
+        expert_share.reshape(peer_count, capacity * quarter_width),
         "tok",
         split_axis=0,
         concat_axis=0,

time: 307 us -> 332 us (1.081); the launches traced: 305 us -> 325 us
  other arithmetic: 21.8 us -> 38.5 us
  local copies, waits for them, and re-layouts: 47.4 us -> 56.2 us
    all_to_all x0 -> x4, other arithmetic: none -> 16.7 us  [the longest x2 8.73 us: body(): lax.all_to_all(padded_rows[source_token].reshape(expert_count, capacity *...]
    unnamed x28 -> x32, local copies, waits for them, and re-layouts: 2.06 us -> 8.94 us
    all_to_all x0 -> x2, local copies, waits for them, and re-layouts: none -> 4.37 us  [the longest x1 3.37 us: body(): lax.all_to_all(padded_rows[source_token].reshape(expert_count, capacity *...]
    all_to_all x1, blocking collectives: 27.4 us -> 23.6 us  [body(): lax.all_to_all(padded_rows[source_token].reshape(expert_count, capacity *...]
where the time goes in v11:
time: 332 us; the launch traced here: 325 us
  blocking collectives  84 us (25%)
  waiting for transfers between devices  77.9 us (23%)
  local copies, waits for them, and re-layouts  56.2 us (17%)
  starting transfers between devices  43.3 us (13%)
  other arithmetic  38.5 us (12%)
  matrix products  23.8 us (7%)
    all_to_all x3, waiting for transfers between devices, head_sum_scatter(): lax.all_to_all(values, 'head', split_axis=axis, concat_axis=0, tiled=True)  35.6 us
    all_to_all x1, blocking collectives, body(): lax.all_to_all(padded_rows[source_token].reshape(expert_count, capacity *...  23.6 us
    all_to_all x1, blocking collectives, body(): lax.all_to_all(jnp.broadcast_to(arrived.reshape(1, peer_count * capacity,...  22.9 us
    all_to_all x1, waiting for transfers between devices, body(): got_packed = lax.all_to_all(packed, 'tok', 0, 0, tiled=True)  19.9 us
    all_to_all x1, starting transfers between devices, body(): got_packed = lax.all_to_all(packed, 'tok', 0, 0, tiled=True)  14.2 us
    psum x1, blocking collectives, body(): lax.psum((jnp.sum(attended_wide * attended_wide, axis=1), jnp.dot(gained,...  12.9 us
    all_to_all x1, waiting for transfers between devices, body(): lax.all_to_all(expert_share.reshape(peer_count, capacity * quarter_width)...  12.8 us
    all_gather x1, blocking collectives, body(): got_rows = lax.all_gather(send_rows, 'head', axis=0, tiled=False)  12.5 us
  transfers between devices with their start and end apart: 6, of which 6 were waited for; matrix products, arithmetic and copies ran while one was open for 2% of the time, Pallas kernels for 0%

profile of v11, /device:TPU:1, one launch (start us, length us, event | category | flops | bytes accessed | tf_op | source)
XLA Modules:
  0.0 325.3 jit_solution(7551771236461916471)
XLA Ops:
  4.6 1.4 gather_fusion.3
  6.0 1.4 gather_fusion.2
  8.9 1.4 fusion.42
  10.4 12.5 %all-gather = bf16[128,2432]{1,0:T(8,128)(2,1)S(1)} all-gather(bf16[32,2432]{1,0:T(8,128)(2,1)S(1)} %concatenate.35), channel_id=2, replica_groups=mesh['tok'=64,'head'=4] {'head'}, dimensions={0}, use_global_device_ids=true | all-gather | bytes 778240 | tf_op jit(solution)/shard_map/all_gather | solution.py:112
  27.9 1.4 multiply_cosine_fusion
  33.1 1.6 gather_fusion
  34.7 2.5 pad_maximum_fusion
  37.2 14.2 %all-to-all-start = ((bf16[64,6,576]{2,1,0:T(8,128)(2,1)}), bf16[64,6,576]{2,1,0:T(8,128)(2,1)}, u32[]{:S(2)}, u32[]{:S(2)}) async-start(bf16[64,6,576]{2,1,0:T(8,128)(2,1)} %pad_maximum_fusion), calls=%async_computation | async-start | bytes 1310720 | tf_op jit(solution)/shard_map/all_to_all | solution.py:164
  51.5 19.9 %all-to-all-done = bf16[64,6,576]{2,1,0:T(8,128)(2,1)} async-done(((bf16[64,6,576]{2,1,0:T(8,128)(2,1)}), bf16[64,6,576]{2,1,0:T(8,128)(2,1)}, u32[]{:S(2)}, u32[]{:S(2)}) %all-to-all-start) | async-done | bytes 442400 | tf_op jit(solution)/shard_map/all_to_all | solution.py:164
  73.8 1.9 copy.318
  75.7 2.1 gather_fusion.5
  77.8 12.1 %all_gather.11 = bf16[32,16,576]{2,0,1:T(8,128)(2,1)S(1)} all-gather(bf16[32,4,576]{2,0,1:T(8,128)(2,1)S(1)} %gather_fusion.5), channel_id=1, replica_groups=mesh['tok'=64,'head'=4] {'head'}, dimensions={1}, use_global_device_ids=true | all-gather | bytes 737280 | tf_op jit(solution)/shard_map/all_gather | solution.py:174
  90.7 1.4 copy.322
  92.1 4.5 %convert_reduce_fusion = (f32[512]{0:T(512)S(1)}, bf16[512,2496]{0,1:T(8,128)(2,1)}) fusion(pred[512,2496]{0,1:T(32,128)(4,1)S(1)} %copy.322, bf16[512,576]{1,0:T(8,128)(2,1)S(1)} %bitcast.123, bf16[2496,576]{0,1:T(8,128)(2,1)S(1)} %copy-done.10), kind=kOutput, calls=%fused_computation.13 | convolution fusion | flops 1478589952 | bytes 7301120 | tf_op jit(solution)/shard_map/qc,pc->qp/dot_general | solution.py:39
  96.8 4.4 %copy.320 = bf16[512,2496]{1,0:T(8,128)(2,1)} copy(bf16[512,2496]{0,1:T(8,128)(2,1)} %get-tuple-element.64) | data formatting | bytes 5111808 | tf_op jit(solution)/shard_map/exp | solution.py:46
  101.2 4.1 %fusion = f32[32,16,512]{2,1,0:T(8,128)S(1)} fusion(bf16[32,16,2496]{2,1,0:T(8,128)(2,1)} %bitcast.115, bf16[2496,576]{0,1:T(8,128)(2,1)} %param.27, pred[32,2496]{1,0:T(8,128)(4,1)S(1)} %compare_and_fusion), kind=kOutput, calls=%fused_computation.17 | convolution fusion | flops 1309900800 | bytes 6371328 | tf_op jit(solution)/shard_map/khp,pl->khl/dot_general | solution.py:47
  105.4 1.7 copy.324
  107.1 4.3 %all-to-all-start.1 = ((f32[33,16,512]{2,0,1:T(8,128)}), f32[33,16,512]{2,0,1:T(8,128)}, u32[]{:S(2)}, u32[]{:S(2)}) async-start(f32[33,16,512]{2,0,1:T(8,128)} %copy.324), calls=%async_computation.1 | async-start | bytes 2621440 | tf_op jit(solution)/shard_map/all_to_all | solution.py:56
  111.7 1.6 gather_fusion.11
  114.0 1.8 gather_fusion.6
  116.8 10.2 %all-to-all-done.1 = f32[33,16,512]{2,0,1:T(8,128)} async-done(((f32[33,16,512]{2,0,1:T(8,128)}), f32[33,16,512]{2,0,1:T(8,128)}, u32[]{:S(2)}, u32[]{:S(2)}) %all-to-all-start.1) | async-done | bytes 1081376 | tf_op jit(solution)/shard_map/all_to_all | solution.py:56
  127.1 1.5 reduce_sum.144
  132.5 8.9 %all-to-all-start.2 = ((bf16[64,2,256]{2,1,0:T(2,128)(2,1)}), bf16[64,2,256]{2,1,0:T(2,128)(2,1)S(1)}, u32[]{:S(2)}, u32[]{:S(2)}) async-start(bf16[64,2,256]{2,1,0:T(2,128)(2,1)} %reshape.677), calls=%async_computation.2 | async-start | bytes 131072 | tf_op jit(solution)/shard_map/all_to_all | solution.py:200
  141.7 9.5 %all-to-all-done.2 = bf16[64,2,256]{2,1,0:T(2,128)(2,1)S(1)} async-done(((bf16[64,2,256]{2,1,0:T(2,128)(2,1)}), bf16[64,2,256]{2,1,0:T(2,128)(2,1)S(1)}, u32[]{:S(2)}, u32[]{:S(2)}) %all-to-all-start.2) | async-done | bytes 65568 | tf_op jit(solution)/shard_map/all_to_all | solution.py:200
  151.9 2.1 fusion.77
  154.7 3.4 %all-to-all-start.3 = ((f32[32,4,512]{2,0,1:T(8,128)}), f32[32,4,512]{2,0,1:T(8,128)S(1)}, u32[]{:S(2)}, u32[]{:S(2)}) async-start(f32[32,4,512]{2,0,1:T(8,128)} %bitcast.122), calls=%async_computation.3 | async-start | bytes 524288 | tf_op jit(solution)/shard_map/all_to_all | solution.py:56
  158.2 6.0 %all-to-all-done.3 = f32[32,4,512]{2,0,1:T(8,128)S(1)} async-done(((f32[32,4,512]{2,0,1:T(8,128)}), f32[32,4,512]{2,0,1:T(8,128)S(1)}, u32[]{:S(2)}, u32[]{:S(2)}) %all-to-all-start.3) | async-done | bytes 262176 | tf_op jit(solution)/shard_map/all_to_all | solution.py:56
  165.3 12.9 %all-reduce.6 = (f32[32]{0:T(128)S(1)}, f32[32,64]{1,0:T(8,128)}) all-reduce(f32[32]{0:T(128)S(1)} %get-tuple-element.37, f32[32,64]{1,0:T(8,128)S(1)} %fusion.52), channel_id=1, replica_groups=mesh['tok'=64,'head'=4] {'head'}, use_global_device_ids=true, to_apply=%region_13.14 | all-reduce | flops 2080 | bytes 16640 | tf_op jit(solution)/shard_map/psum | solution.py:206
  178.3 2.6 gather_fusion.9
  180.9 3.4 %all_to_all.80 = bf16[64,1,3072]{2,1,0:T(2,128)(2,1)} reshape(bf16[384,512]{1,0:T(8,128)(2,1)} %gather_fusion.9) | data formatting | bytes 786432 | tf_op jit(solution)/shard_map/all_to_all | solution.py:236
  184.2 4.7 %reduce.32 = bf16[64,3072]{1,0:T(8,128)(2,1)} reduce(bf16[64,1,3072]{2,1,0:T(2,128)(2,1)} %all_to_all.80, bf16[]{:T(256)} %broadcast.654), dimensions={1}, to_apply=%all_to_all.80.reduce_sub_computation | reduce | bytes 786434 | tf_op jit(solution)/shard_map/all_to_all | solution.py:236
  190.2 23.6 %all_to_all.90 = bf16[64,2,1536]{2,1,0:T(2,128)(2,1)} all-to-all(bf16[64,2,1536]{2,1,0:T(2,128)(2,1)S(1)} %reshape.679), channel_id=1, replica_groups=mesh['tok'=64,'head'=4] {'tok'}, dimensions={0} | all-to-all | bytes 786432 | tf_op jit(solution)/shard_map/all_to_all | solution.py:236
  213.8 3.5 %reshape.680 = bf16[64,1,3072]{2,1,0:T(2,128)(2,1)} reshape(bf16[64,2,1536]{2,1,0:T(2,128)(2,1)} %all_to_all.90) | data formatting | bytes 786432
  217.3 4.0 %reduce.23 = bf16[64,3072]{1,0:T(8,128)(2,1)} reduce(bf16[64,1,3072]{2,1,0:T(2,128)(2,1)} %reshape.680, bf16[]{:T(256)} %constant.265), dimensions={1}, to_apply=%all_to_all.72.reduce_sub_computation | reduce | bytes 786434 | tf_op jit(solution)/shard_map/all_to_all | solution.py:236
  224.8 22.9 %all_to_all.91 = bf16[4,384,512]{1,2,0:T(8,128)(2,1)S(1)} all-to-all(bf16[4,384,512]{1,2,0:T(8,128)(2,1)S(1)} %broadcast_in_dim.157), channel_id=1, replica_groups=mesh['tok'=64,'head'=4] {'head'}, dimensions={0} | all-to-all | bytes 3145728 | tf_op jit(solution)/shard_map/all_to_all | solution.py:243
  248.8 1.7 fusion.8
  250.5 5.5 %convolution_convert_fusion = bf16[384,2048]{1,0:T(8,128)(2,1)} fusion(bf16[1,352,2048]{2,1,0:T(8,128)(2,1)} %param.35, bf16[384,2048]{0,1:T(8,128)(2,1)} %bitcast.118, bf16[1,2048,352]{1,2,0:T(8,128)(2,1)} %param.34, f32[384,352]{0,1:T(8,128)} %fusion.8), kind=kOutput, calls=%fused_computation.16 | convolution fusion | flops 1108893696 | bytes 6569984 | tf_op jit(solution)/shard_map/dot_general | solution.py:257
  256.0 2.7 copy.362
  258.7 4.7 %all-to-all-start.6 = ((bf16[384,4,512]{2,0,1:T(8,128)(2,1)}), bf16[384,4,512]{2,0,1:T(8,128)(2,1)}, u32[]{:S(2)}, u32[]{:S(2)}) async-start(bf16[384,4,512]{2,0,1:T(8,128)(2,1)} %bitcast.110), calls=%async_computation.6 | async-start | bytes 3145728 | tf_op jit(solution)/shard_map/all_to_all | solution.py:56
  263.5 19.4 %all-to-all-done.6 = bf16[384,4,512]{2,0,1:T(8,128)(2,1)} async-done(((bf16[384,4,512]{2,0,1:T(8,128)(2,1)}), bf16[384,4,512]{2,0,1:T(8,128)(2,1)}, u32[]{:S(2)}, u32[]{:S(2)}) %all-to-all-start.6) | async-done | bytes 1572896 | tf_op jit(solution)/shard_map/all_to_all | solution.py:56
  282.9 1.8 reduce_sum.150
  285.7 3.9 %reduce.33 = bf16[64,3072]{1,0:T(8,128)(2,1)S(1)} reduce(bf16[64,1,3072]{2,1,0:T(2,128)(2,1)} %all_to_all.81, bf16[]{:T(256)} %broadcast.654), dimensions={1}, to_apply=%all_to_all.81.reduce_sub_computation | reduce | bytes 786434 | tf_op jit(solution)/shard_map/all_to_all | solution.py:260
  290.7 7.8 %all-to-all-start.7 = ((bf16[64,2,1536]{2,1,0:T(2,128)(2,1)}), bf16[64,2,1536]{2,1,0:T(2,128)(2,1)S(1)}, u32[]{:S(2)}, u32[]{:S(2)}) async-start(bf16[64,2,1536]{2,1,0:T(2,128)(2,1)} %reshape.681), calls=%async_computation.7 | async-start | bytes 786432 | tf_op jit(solution)/shard_map/all_to_all | solution.py:260
  300.2 12.8 %all-to-all-done.7 = bf16[64,2,1536]{2,1,0:T(2,128)(2,1)S(1)} async-done(((bf16[64,2,1536]{2,1,0:T(2,128)(2,1)}), bf16[64,2,1536]{2,1,0:T(2,128)(2,1)S(1)}, u32[]{:S(2)}, u32[]{:S(2)}) %all-to-all-start.7) | async-done | bytes 393248 | tf_op jit(solution)/shard_map/all_to_all | solution.py:260
  314.1 4.0 %reduce.24 = bf16[64,3072]{1,0:T(8,128)(2,1)} reduce(bf16[64,1,3072]{2,1,0:T(2,128)(2,1)} %reshape.682, bf16[]{:T(256)} %constant.265), dimensions={1}, to_apply=%all_to_all.79.reduce_sub_computation | reduce | bytes 786434 | tf_op jit(solution)/shard_map/all_to_all | solution.py:260
  319.5 1.7 gather_fusion.10
  321.2 1.8 reshape.659
  323.0 1.9 multiply_reduce_fusion
  (137 shorter events, 38.5 us)
Async XLA Ops:
  0.6 23.1 %copy-start = (bf16[2048,768]{1,0:T(8,128)(2,1)S(1)}, bf16[2048,768]{1,0:T(8,128)(2,1)}, u32[]{:S(2)}) copy-start(bf16[2048,768]{1,0:T(8,128)(2,1)} %param.22) | copy-start | bytes 9437188
  0.6 9.6 %copy-start.4 = (bf16[32,512]{1,0:T(8,128)(2,1)S(1)}, bf16[32,512]{1,0:T(8,128)(2,1)}, u32[]{:S(2)}) copy-start(bf16[32,512]{1,0:T(8,128)(2,1)} %param.20) | copy-start | bytes 98308
  23.7 4.1 %copy-start.9 = (f32[32]{0:T(128)S(1)}, f32[32]{0:T(128)}, u32[]{:S(2)}) copy-start(f32[32]{0:T(128)} %multiply_power_fusion) | copy-start | bytes 388
  29.3 5.4 %copy-start.1 = (bf16[32,576]{1,0:T(8,128)(2,1)}, bf16[32,576]{1,0:T(8,128)(2,1)S(1)}, u32[]{:S(2)}) copy-start(bf16[32,576]{1,0:T(8,128)(2,1)S(1)} %pad_maximum_fusion.2) | copy-start | bytes 110596
  33.1 18.2 %copy-start.6 = (s32[32,6]{0,1:T(8,128)S(1)}, s32[32,6]{0,1:T(8,128)}, u32[]{:S(2)}) copy-start(s32[32,6]{0,1:T(8,128)} %param.32) | copy-start | bytes 2308
  37.2 34.2 %all-to-all-start = ((bf16[64,6,576]{2,1,0:T(8,128)(2,1)}), bf16[64,6,576]{2,1,0:T(8,128)(2,1)}, u32[]{:S(2)}, u32[]{:S(2)}) async-start(bf16[64,6,576]{2,1,0:T(8,128)(2,1)} %pad_maximum_fusion), calls=%async_computation | async-start | bytes 1310720 | tf_op jit(solution)/shard_map/all_to_all | solution.py:164
  90.3 1.8 copy-start.10
  107.1 19.9 %all-to-all-start.1 = ((f32[33,16,512]{2,0,1:T(8,128)}), f32[33,16,512]{2,0,1:T(8,128)}, u32[]{:S(2)}, u32[]{:S(2)}) async-start(f32[33,16,512]{2,0,1:T(8,128)} %copy.324), calls=%async_computation.1 | async-start | bytes 2621440 | tf_op jit(solution)/shard_map/all_to_all | solution.py:56
  128.5 12.9 %copy-start.8 = (s32[32]{0:T(128)S(1)}, s32[32]{0:T(128)}, u32[]{:S(2)}) copy-start(s32[32]{0:T(128)} %get-tuple-element.39) | copy-start | bytes 388
  132.5 18.7 %all-to-all-start.2 = ((bf16[64,2,256]{2,1,0:T(2,128)(2,1)}), bf16[64,2,256]{2,1,0:T(2,128)(2,1)S(1)}, u32[]{:S(2)}, u32[]{:S(2)}) async-start(bf16[64,2,256]{2,1,0:T(2,128)(2,1)} %reshape.677), calls=%async_computation.2 | async-start | bytes 131072 | tf_op jit(solution)/shard_map/all_to_all | solution.py:200
  151.9 12.4 %copy-start.7 = (f32[512]{0:T(512)S(1)}, f32[512]{0:T(512)}, u32[]{:S(2)}) copy-start(f32[512]{0:T(512)} %param.30) | copy-start | bytes 6148
  154.7 9.5 %all-to-all-start.3 = ((f32[32,4,512]{2,0,1:T(8,128)}), f32[32,4,512]{2,0,1:T(8,128)S(1)}, u32[]{:S(2)}, u32[]{:S(2)}) async-start(f32[32,4,512]{2,0,1:T(8,128)} %bitcast.122), calls=%async_computation.3 | async-start | bytes 524288 | tf_op jit(solution)/shard_map/all_to_all | solution.py:56
  164.3 13.9 %copy-start.3 = (bf16[32,512]{1,0:T(8,128)(2,1)}, bf16[32,512]{1,0:T(8,128)(2,1)S(1)}, u32[]{:S(2)}) copy-start(bf16[32,512]{1,0:T(8,128)(2,1)S(1)} %get-tuple-element.38) | copy-start | bytes 98308
  224.8 24.1 %copy-start.11 = (bf16[1,2048,352]{1,2,0:T(8,128)(2,1)S(1)}, bf16[1,2048,352]{1,2,0:T(8,128)(2,1)}, u32[]{:S(2)}) copy-start(bf16[1,2048,352]{1,2,0:T(8,128)(2,1)} %param.33) | copy-start | bytes 4325380
  247.7 1.1 copy-start.2
  258.7 4.7 %copy-start.5 = (s32[32,6]{1,0:T(8,128)S(1)}, s32[32,6]{1,0:T(8,128)}, u32[]{:S(2)}) copy-start(s32[32,6]{1,0:T(8,128)} %get-tuple-element.35) | copy-start | bytes 2308
  258.7 24.2 %all-to-all-start.6 = ((bf16[384,4,512]{2,0,1:T(8,128)(2,1)}), bf16[384,4,512]{2,0,1:T(8,128)(2,1)}, u32[]{:S(2)}, u32[]{:S(2)}) async-start(bf16[384,4,512]{2,0,1:T(8,128)(2,1)} %bitcast.110), calls=%async_computation.6 | async-start | bytes 3145728 | tf_op jit(solution)/shard_map/all_to_all | solution.py:56
  290.7 22.4 %all-to-all-start.7 = ((bf16[64,2,1536]{2,1,0:T(2,128)(2,1)}), bf16[64,2,1536]{2,1,0:T(2,128)(2,1)S(1)}, u32[]{:S(2)}, u32[]{:S(2)}) async-start(bf16[64,2,1536]{2,1,0:T(2,128)(2,1)} %reshape.681), calls=%async_computation.7 | async-start | bytes 786432 | tf_op jit(solution)/shard_map/all_to_all | solution.py:260

commit v12 on v10

--- a/solution.py
+++ b/solution.py
@@ -175,10 +175,24 @@
     numerator, denominator = owner_attend(
         all_heads, owner_lengths, latent_cache, head_index, factor
     )
-    den_row = jnp.zeros((1, denominator.shape[1], LATENT), jnp.float32)
-    den_row = den_row.at[0, :, : denominator.shape[0]].set(denominator.T)
-    joined = head_sum_scatter(jnp.concatenate([numerator, den_row], axis=0), 1)
-    group_den = joined[local_rows, :, :local_rows].T
+    den_t = denominator.T
+    den_hi = lax.reduce_precision(den_t, exponent_bits=8, mantissa_bits=7)
+    den_rest = den_t - den_hi
+    den_mid = lax.reduce_precision(den_rest, exponent_bits=8, mantissa_bits=7)
+    den_lo = den_rest - den_mid
+    den_row = jnp.zeros((3, denominator.shape[1], LATENT), jnp.float32)
+    den_row = den_row.at[:, :, : denominator.shape[0]].set(jnp.stack([den_hi, den_mid, den_lo]))
+    moved = lax.all_to_all(
+        jnp.concatenate([numerator, den_row], axis=0).astype(jnp.bfloat16),
+        "head",
+        split_axis=1,
+        concat_axis=0,
+        tiled=True,
+    ).astype(jnp.float32)
+    moved = moved.reshape((head_count, local_rows + 3) + moved.shape[1:])
+    joined = jnp.sum(moved[:, :local_rows], axis=0)
+    den_parts = moved[:, local_rows:, :, :local_rows]
+    group_den = jnp.sum((den_parts[:, 0] + den_parts[:, 1]) + den_parts[:, 2], axis=0).T
     self_score = factor * jnp.einsum(
         "bhc,bc->bh", owner_probes, owner_new, preferred_element_type=jnp.float32
     )

time: 307 us -> 302 us (0.984)
  waiting for transfers between devices: 80.7 us -> 73.7 us
    all_to_all x3 -> x2, waiting for transfers between devices: 35.8 us -> 25.5 us  [head_sum_scatter(): lax.all_to_all(values, 'head', split_axis=axis, concat_axis=0, tiled=True)]
    all_to_all x0 -> x1, waiting for transfers between devices: none -> 7.21 us  [body(): lax.all_to_all(jnp.concatenate([numerator, den_row], axis=0).astype(jnp.b...]
    all_to_all x3 -> x2, starting transfers between devices: 12.1 us -> 7.87 us  [head_sum_scatter(): lax.all_to_all(values, 'head', split_axis=axis, concat_axis=0, tiled=True)]
    all_to_all x0 -> x1, starting transfers between devices: none -> 4.15 us  [body(): lax.all_to_all(jnp.concatenate([numerator, den_row], axis=0).astype(jnp.b...]
where the time goes in v12:
time: 302 us; the launch traced here: 300 us
  blocking collectives  87.5 us (29%)
  waiting for transfers between devices  73.7 us (24%)
  local copies, waits for them, and re-layouts  49.2 us (16%)
  starting transfers between devices  43.6 us (14%)
  matrix products  23.7 us (8%)
  other arithmetic  21.4 us (7%)
    all_to_all x1, blocking collectives, body(): lax.all_to_all(padded_rows[source_token].reshape(expert_count, capacity,...  27.4 us
    all_to_all x2, waiting for transfers between devices, head_sum_scatter(): lax.all_to_all(values, 'head', split_axis=axis, concat_axis=0, tiled=True)  25.5 us
    all_to_all x1, blocking collectives, body(): lax.all_to_all(jnp.broadcast_to(arrived.reshape(1, peer_count * capacity,...  23 us
    all_to_all x1, waiting for transfers between devices, body(): got_packed = lax.all_to_all(packed, 'tok', 0, 0, tiled=True)  17.3 us
    all_to_all x1, waiting for transfers between devices, body(): lax.all_to_all(expert_share.reshape(peer_count, capacity, quarter_width),...  15.5 us
    all_to_all x1, starting transfers between devices, body(): got_packed = lax.all_to_all(packed, 'tok', 0, 0, tiled=True)  14.2 us
    psum x1, blocking collectives, body(): lax.psum((jnp.sum(attended_wide * attended_wide, axis=1), jnp.dot(gained,...  12.5 us
    all_gather x1, blocking collectives, body(): got_rows = lax.all_gather(send_rows, 'head', axis=0, tiled=False)  12.5 us
  transfers between devices with their start and end apart: 6, of which 6 were waited for; matrix products, arithmetic and copies ran while one was open for 2% of the time, Pallas kernels for 0%

profile of v12, /device:TPU:1, one launch (start us, length us, event | category | flops | bytes accessed | tf_op | source)
XLA Modules:
  0.0 300.2 jit_solution(15096290623887668666)
XLA Ops:
  3.0 1.2 compare_select_fusion.5
  4.6 1.4 gather_fusion.3
  6.0 1.4 gather_fusion.2
  8.9 1.4 fusion.44
  10.4 12.5 %all-gather = bf16[128,2432]{1,0:T(8,128)(2,1)S(1)} all-gather(bf16[32,2432]{1,0:T(8,128)(2,1)S(1)} %concatenate.36), channel_id=2, replica_groups=mesh['tok'=64,'head'=4] {'head'}, dimensions={0}, use_global_device_ids=true | all-gather | bytes 778240 | tf_op jit(solution)/shard_map/all_gather | solution.py:112
  27.9 1.4 multiply_cosine_fusion
  30.9 1.3 fusion.19
  33.1 1.6 gather_fusion
  34.7 2.5 pad_maximum_fusion
  37.2 14.2 %all-to-all-start = ((bf16[64,6,576]{2,1,0:T(8,128)(2,1)}), bf16[64,6,576]{2,1,0:T(8,128)(2,1)}, u32[]{:S(2)}, u32[]{:S(2)}) async-start(bf16[64,6,576]{2,1,0:T(8,128)(2,1)} %pad_maximum_fusion), calls=%async_computation | async-start | bytes 1310720 | tf_op jit(solution)/shard_map/all_to_all | solution.py:164
  51.7 1.6 gather_fusion.11
  54.1 17.3 %all-to-all-done = bf16[64,6,576]{2,1,0:T(8,128)(2,1)} async-done(((bf16[64,6,576]{2,1,0:T(8,128)(2,1)}), bf16[64,6,576]{2,1,0:T(8,128)(2,1)}, u32[]{:S(2)}, u32[]{:S(2)}) %all-to-all-start) | async-done | bytes 442400 | tf_op jit(solution)/shard_map/all_to_all | solution.py:164
  73.8 1.9 copy.308
  75.7 1.8 gather_fusion.6
  77.5 2.1 gather_fusion.5
  79.6 12.1 %all_gather.11 = bf16[32,16,576]{2,0,1:T(8,128)(2,1)S(1)} all-gather(bf16[32,4,576]{2,0,1:T(8,128)(2,1)S(1)} %gather_fusion.5), channel_id=1, replica_groups=mesh['tok'=64,'head'=4] {'head'}, dimensions={1}, use_global_device_ids=true | all-gather | bytes 737280 | tf_op jit(solution)/shard_map/all_gather | solution.py:174
  92.4 1.4 copy.312
  93.9 4.5 %convert_reduce_fusion = (f32[512]{0:T(512)S(1)}, bf16[512,2496]{0,1:T(8,128)(2,1)}) fusion(pred[512,2496]{0,1:T(32,128)(4,1)S(1)} %copy.312, bf16[512,576]{1,0:T(8,128)(2,1)S(1)} %bitcast.146, bf16[2496,576]{0,1:T(8,128)(2,1)S(1)} %copy-done.9), kind=kOutput, calls=%fused_computation.13 | convolution fusion | flops 1478589952 | bytes 7301120 | tf_op jit(solution)/shard_map/qc,pc->qp/dot_general | solution.py:39
  98.6 4.4 %copy.310 = bf16[512,2496]{1,0:T(8,128)(2,1)} copy(bf16[512,2496]{0,1:T(8,128)(2,1)} %get-tuple-element.67) | data formatting | bytes 5111808 | tf_op jit(solution)/shard_map/exp | solution.py:46
  103.0 4.1 %fusion.10 = bf16[32,16,512]{2,1,0:T(8,128)(2,1)S(1)} fusion(bf16[2496,576]{0,1:T(8,128)(2,1)} %param.27, bf16[32,16,2496]{2,1,0:T(8,128)(2,1)} %bitcast.138, pred[32,2496]{1,0:T(8,128)(4,1)S(1)} %compare_and_fusion), kind=kOutput, calls=%fused_computation.28 | convolution fusion | flops 1310162944 | bytes 5847040 | tf_op jit(solution)/shard_map/khp,pl->khl/dot_general | solution.py:47
  107.1 1.2 copy.314
  108.3 4.2 %all-to-all-start.1 = ((bf16[35,16,512]{2,0,1:T(8,128)(2,1)}), bf16[35,16,512]{2,0,1:T(8,128)(2,1)}, u32[]{:S(2)}, u32[]{:S(2)}) async-start(bf16[35,16,512]{2,0,1:T(8,128)(2,1)} %copy.314), calls=%async_computation.1 | async-start | bytes 1310720 | tf_op jit(solution)/shard_map/all_to_all | solution.py:185
  113.5 7.2 %all-to-all-done.1 = bf16[35,16,512]{2,0,1:T(8,128)(2,1)} async-done(((bf16[35,16,512]{2,0,1:T(8,128)(2,1)}), bf16[35,16,512]{2,0,1:T(8,128)(2,1)}, u32[]{:S(2)}, u32[]{:S(2)}) %all-to-all-start.1) | async-done | bytes 573472 | tf_op jit(solution)/shard_map/all_to_all | solution.py:185
  120.7 1.4 copy.358
  122.7 1.2 fusion.21
  126.6 9.3 %all-to-all-start.2 = ((bf16[64,2,256]{2,1,0:T(2,128)(2,1)}), bf16[64,2,256]{2,1,0:T(2,128)(2,1)S(1)}, u32[]{:S(2)}, u32[]{:S(2)}) async-start(bf16[64,2,256]{2,1,0:T(2,128)(2,1)} %reshape.670), calls=%async_computation.2 | async-start | bytes 131072 | tf_op jit(solution)/shard_map/all_to_all | solution.py:214
  137.5 8.2 %all-to-all-done.2 = bf16[64,2,256]{2,1,0:T(2,128)(2,1)S(1)} async-done(((bf16[64,2,256]{2,1,0:T(2,128)(2,1)}), bf16[64,2,256]{2,1,0:T(2,128)(2,1)S(1)}, u32[]{:S(2)}, u32[]{:S(2)}) %all-to-all-start.2) | async-done | bytes 65568 | tf_op jit(solution)/shard_map/all_to_all | solution.py:214
  146.4 2.1 fusion.85
  149.2 3.4 %all-to-all-start.3 = ((f32[32,4,512]{2,0,1:T(8,128)}), f32[32,4,512]{2,0,1:T(8,128)S(1)}, u32[]{:S(2)}, u32[]{:S(2)}) async-start(f32[32,4,512]{2,0,1:T(8,128)} %bitcast.145), calls=%async_computation.3 | async-start | bytes 524288 | tf_op jit(solution)/shard_map/all_to_all | solution.py:56
  152.6 6.0 %all-to-all-done.3 = f32[32,4,512]{2,0,1:T(8,128)S(1)} async-done(((f32[32,4,512]{2,0,1:T(8,128)}), f32[32,4,512]{2,0,1:T(8,128)S(1)}, u32[]{:S(2)}, u32[]{:S(2)}) %all-to-all-start.3) | async-done | bytes 262176 | tf_op jit(solution)/shard_map/all_to_all | solution.py:56
  159.8 12.5 %all-reduce.6 = (f32[32]{0:T(128)S(1)}, f32[32,64]{1,0:T(8,128)}) all-reduce(f32[32]{0:T(128)S(1)} %get-tuple-element.37, f32[32,64]{1,0:T(8,128)S(1)} %fusion.56), channel_id=1, replica_groups=mesh['tok'=64,'head'=4] {'head'}, use_global_device_ids=true, to_apply=%region_14.15 | all-reduce | flops 2080 | bytes 16640 | tf_op jit(solution)/shard_map/psum | solution.py:220
  172.4 2.6 gather_fusion.9
  175.0 1.9 reshape.555
  176.9 27.4 %all_to_all.77 = bf16[64,6,512]{2,1,0:T(8,128)(2,1)} all-to-all(bf16[64,6,512]{2,1,0:T(8,128)(2,1)} %reshape.555), channel_id=1, replica_groups=mesh['tok'=64,'head'=4] {'tok'}, dimensions={0} | all-to-all | bytes 786432 | tf_op jit(solution)/shard_map/all_to_all | solution.py:250
  204.3 1.2 broadcast_in_dim.156
  207.5 23.0 %all_to_all.78 = bf16[4,384,512]{1,2,0:T(8,128)(2,1)S(1)} all-to-all(bf16[4,384,512]{1,2,0:T(8,128)(2,1)S(1)} %broadcast_in_dim.157), channel_id=1, replica_groups=mesh['tok'=64,'head'=4] {'head'}, dimensions={0} | all-to-all | bytes 3145728 | tf_op jit(solution)/shard_map/all_to_all | solution.py:257
  231.7 1.7 fusion.8
  233.4 5.5 %convolution_convert_fusion = bf16[384,2048]{1,0:T(8,128)(2,1)} fusion(bf16[1,352,2048]{2,1,0:T(8,128)(2,1)} %param.35, bf16[384,2048]{0,1:T(8,128)(2,1)} %bitcast.141, bf16[1,2048,352]{1,2,0:T(8,128)(2,1)} %param.34, f32[384,352]{0,1:T(8,128)} %fusion.8), kind=kOutput, calls=%fused_computation.16 | convolution fusion | flops 1108893696 | bytes 6569984 | tf_op jit(solution)/shard_map/dot_general | solution.py:271
  238.8 2.7 copy.357
  241.5 4.5 %all-to-all-start.6 = ((bf16[384,4,512]{2,0,1:T(8,128)(2,1)}), bf16[384,4,512]{2,0,1:T(8,128)(2,1)}, u32[]{:S(2)}, u32[]{:S(2)}) async-start(bf16[384,4,512]{2,0,1:T(8,128)(2,1)} %bitcast.131), calls=%async_computation.6 | async-start | bytes 3145728 | tf_op jit(solution)/shard_map/all_to_all | solution.py:56
  246.1 19.5 %all-to-all-done.6 = bf16[384,4,512]{2,0,1:T(8,128)(2,1)} async-done(((bf16[384,4,512]{2,0,1:T(8,128)(2,1)}), bf16[384,4,512]{2,0,1:T(8,128)(2,1)}, u32[]{:S(2)}, u32[]{:S(2)}) %all-to-all-start.6) | async-done | bytes 1572896 | tf_op jit(solution)/shard_map/all_to_all | solution.py:56
  265.6 1.8 reduce_sum.160
  268.4 8.1 %all-to-all-start.7 = ((bf16[64,6,512]{2,1,0:T(8,128)(2,1)}), bf16[64,6,512]{2,1,0:T(8,128)(2,1)}, u32[]{:S(2)}, u32[]{:S(2)}) async-start(bf16[64,6,512]{2,1,0:T(8,128)(2,1)} %reshape.557), calls=%async_computation.7 | async-start | bytes 1048576 | tf_op jit(solution)/shard_map/all_to_all | solution.py:274
  278.2 15.5 %all-to-all-done.7 = bf16[64,6,512]{2,1,0:T(8,128)(2,1)} async-done(((bf16[64,6,512]{2,1,0:T(8,128)(2,1)}), bf16[64,6,512]{2,1,0:T(8,128)(2,1)}, u32[]{:S(2)}, u32[]{:S(2)}) %all-to-all-start.7) | async-done | bytes 393248 | tf_op jit(solution)/shard_map/all_to_all | solution.py:274
  293.7 1.2 reshape.558
  294.8 1.7 gather_fusion.10
  296.5 1.8 reshape.654
  298.3 1.9 multiply_reduce_fusion
  (133 shorter events, 30.6 us)
Async XLA Ops:
  0.6 23.1 %copy-start = (bf16[2048,768]{1,0:T(8,128)(2,1)S(1)}, bf16[2048,768]{1,0:T(8,128)(2,1)}, u32[]{:S(2)}) copy-start(bf16[2048,768]{1,0:T(8,128)(2,1)} %param.22) | copy-start | bytes 9437188
  0.6 9.6 %copy-start.4 = (bf16[32,512]{1,0:T(8,128)(2,1)S(1)}, bf16[32,512]{1,0:T(8,128)(2,1)}, u32[]{:S(2)}) copy-start(bf16[32,512]{1,0:T(8,128)(2,1)} %param.20) | copy-start | bytes 98308
  23.7 4.1 %copy-start.8 = (f32[32]{0:T(128)S(1)}, f32[32]{0:T(128)}, u32[]{:S(2)}) copy-start(f32[32]{0:T(128)} %multiply_power_fusion) | copy-start | bytes 388
  29.3 5.4 %copy-start.1 = (bf16[32,576]{1,0:T(8,128)(2,1)}, bf16[32,576]{1,0:T(8,128)(2,1)S(1)}, u32[]{:S(2)}) copy-start(bf16[32,576]{1,0:T(8,128)(2,1)S(1)} %pad_maximum_fusion.3) | copy-start | bytes 110596
  33.1 18.2 %copy-start.6 = (s32[32,6]{0,1:T(8,128)S(1)}, s32[32,6]{0,1:T(8,128)}, u32[]{:S(2)}) copy-start(s32[32,6]{0,1:T(8,128)} %param.32) | copy-start | bytes 2308
  37.2 34.2 %all-to-all-start = ((bf16[64,6,576]{2,1,0:T(8,128)(2,1)}), bf16[64,6,576]{2,1,0:T(8,128)(2,1)}, u32[]{:S(2)}, u32[]{:S(2)}) async-start(bf16[64,6,576]{2,1,0:T(8,128)(2,1)} %pad_maximum_fusion), calls=%async_computation | async-start | bytes 1310720 | tf_op jit(solution)/shard_map/all_to_all | solution.py:164
  92.1 1.8 copy-start.9
  108.3 12.4 %all-to-all-start.1 = ((bf16[35,16,512]{2,0,1:T(8,128)(2,1)}), bf16[35,16,512]{2,0,1:T(8,128)(2,1)}, u32[]{:S(2)}, u32[]{:S(2)}) async-start(bf16[35,16,512]{2,0,1:T(8,128)(2,1)} %copy.314), calls=%async_computation.1 | async-start | bytes 1310720 | tf_op jit(solution)/shard_map/all_to_all | solution.py:185
  126.6 19.1 %all-to-all-start.2 = ((bf16[64,2,256]{2,1,0:T(2,128)(2,1)}), bf16[64,2,256]{2,1,0:T(2,128)(2,1)S(1)}, u32[]{:S(2)}, u32[]{:S(2)}) async-start(bf16[64,2,256]{2,1,0:T(2,128)(2,1)} %reshape.670), calls=%async_computation.2 | async-start | bytes 131072 | tf_op jit(solution)/shard_map/all_to_all | solution.py:214
  146.4 12.4 %copy-start.7 = (f32[512]{0:T(512)S(1)}, f32[512]{0:T(512)}, u32[]{:S(2)}) copy-start(f32[512]{0:T(512)} %param.30) | copy-start | bytes 6148
  149.2 9.5 %all-to-all-start.3 = ((f32[32,4,512]{2,0,1:T(8,128)}), f32[32,4,512]{2,0,1:T(8,128)S(1)}, u32[]{:S(2)}, u32[]{:S(2)}) async-start(f32[32,4,512]{2,0,1:T(8,128)} %bitcast.145), calls=%async_computation.3 | async-start | bytes 524288 | tf_op jit(solution)/shard_map/all_to_all | solution.py:56
  158.8 13.5 %copy-start.3 = (bf16[32,512]{1,0:T(8,128)(2,1)}, bf16[32,512]{1,0:T(8,128)(2,1)S(1)}, u32[]{:S(2)}) copy-start(bf16[32,512]{1,0:T(8,128)(2,1)S(1)} %get-tuple-element.38) | copy-start | bytes 98308
  207.5 24.2 %copy-start.10 = (bf16[1,2048,352]{1,2,0:T(8,128)(2,1)S(1)}, bf16[1,2048,352]{1,2,0:T(8,128)(2,1)}, u32[]{:S(2)}) copy-start(bf16[1,2048,352]{1,2,0:T(8,128)(2,1)} %param.33) | copy-start | bytes 4325380
  230.5 1.1 copy-start.2
  241.5 4.5 %copy-start.5 = (s32[32,6]{1,0:T(8,128)S(1)}, s32[32,6]{1,0:T(8,128)}, u32[]{:S(2)}) copy-start(s32[32,6]{1,0:T(8,128)} %get-tuple-element.35) | copy-start | bytes 2308
  241.5 24.1 %all-to-all-start.6 = ((bf16[384,4,512]{2,0,1:T(8,128)(2,1)}), bf16[384,4,512]{2,0,1:T(8,128)(2,1)}, u32[]{:S(2)}, u32[]{:S(2)}) async-start(bf16[384,4,512]{2,0,1:T(8,128)(2,1)} %bitcast.131), calls=%async_computation.6 | async-start | bytes 3145728 | tf_op jit(solution)/shard_map/all_to_all | solution.py:56
  268.4 25.3 %all-to-all-start.7 = ((bf16[64,6,512]{2,1,0:T(8,128)(2,1)}), bf16[64,6,512]{2,1,0:T(8,128)(2,1)}, u32[]{:S(2)}, u32[]{:S(2)}) async-start(bf16[64,6,512]{2,1,0:T(8,128)(2,1)} %reshape.557), calls=%async_computation.7 | async-start | bytes 1048576 | tf_op jit(solution)/shard_map/all_to_all | solution.py:274

commit v13 on v12

--- a/solution.py
+++ b/solution.py
@@ -213,7 +213,9 @@
     back_row = jnp.where(back_valid, local_slot, local_rows)
     head_out = lax.all_to_all(owner_out[back_row], "tok", 0, 0, tiled=True)[dest_owner]
     head_out = head_out.reshape(local_rows, local_heads * NOPE)
-    attn_piece = head_sum_scatter(jnp.dot(head_out, w_out, preferred_element_type=jnp.float32), 1)
+    attn_piece = head_sum_scatter(
+        jnp.dot(head_out, w_out, preferred_element_type=jnp.float32).astype(jnp.bfloat16), 1
+    )
     attended = (hidden.astype(jnp.float32) + attn_piece).astype(jnp.bfloat16)
     attended_wide = attended.astype(jnp.float32)
     gained = (attended_wide * ffn_gain).astype(jnp.bfloat16)

time: 302 us -> 301 us (level)
  transfers between devices with their start and end apart: 6 -> 6, of which waited for: 6 -> 6; matrix products, arithmetic and copies ran while one was open for 2% -> 3% of each run, Pallas kernels for 0% -> 0%
where the time goes in v13:
time: 301 us; the launch traced here: 299 us
  blocking collectives  87.5 us (29%)
  waiting for transfers between devices  72 us (24%)
  local copies, waits for them, and re-layouts  49.7 us (17%)
  starting transfers between devices  43.5 us (14%)
  matrix products  22.8 us (8%)
  other arithmetic  22.5 us (7%)
    all_to_all x1, blocking collectives, body(): lax.all_to_all(padded_rows[source_token].reshape(expert_count, capacity,...  27.4 us
    all_to_all x2, waiting for transfers between devices, head_sum_scatter(): lax.all_to_all(values, 'head', split_axis=axis, concat_axis=0, tiled=True)  24.3 us
    all_to_all x1, blocking collectives, body(): lax.all_to_all(jnp.broadcast_to(arrived.reshape(1, peer_count * capacity,...  23 us
    all_to_all x1, waiting for transfers between devices, body(): got_packed = lax.all_to_all(packed, 'tok', 0, 0, tiled=True)  16.5 us
    all_to_all x1, waiting for transfers between devices, body(): lax.all_to_all(expert_share.reshape(peer_count, capacity, quarter_width),...  15.5 us
    all_to_all x1, starting transfers between devices, body(): got_packed = lax.all_to_all(packed, 'tok', 0, 0, tiled=True)  14.2 us
    psum x1, blocking collectives, body(): lax.psum((jnp.sum(attended_wide * attended_wide, axis=1), jnp.dot(gained,...  12.5 us
    all_gather x1, blocking collectives, body(): got_rows = lax.all_gather(send_rows, 'head', axis=0, tiled=False)  12.5 us
  transfers between devices with their start and end apart: 6, of which 6 were waited for; matrix products, arithmetic and copies ran while one was open for 3% of the time, Pallas kernels for 0%

profile of v13, /device:TPU:1, one launch (start us, length us, event | category | flops | bytes accessed | tf_op | source)
XLA Modules:
  0.0 299.2 jit_solution(14646686963028986328)
XLA Ops:
  3.0 1.2 compare_select_fusion.5
  4.5 1.4 gather_fusion.3
  6.0 1.4 gather_fusion.2
  8.9 1.4 fusion.44
  10.4 12.5 %all-gather = bf16[128,2432]{1,0:T(8,128)(2,1)S(1)} all-gather(bf16[32,2432]{1,0:T(8,128)(2,1)S(1)} %concatenate.36), channel_id=2, replica_groups=mesh['tok'=64,'head'=4] {'head'}, dimensions={0}, use_global_device_ids=true | all-gather | bytes 778240 | tf_op jit(solution)/shard_map/all_gather | solution.py:112
  27.8 1.4 multiply_cosine_fusion
  30.8 1.3 fusion.19
  33.1 1.6 gather_fusion
  34.7 2.5 pad_maximum_fusion
  37.2 14.2 %all-to-all-start = ((bf16[64,6,576]{2,1,0:T(8,128)(2,1)}), bf16[64,6,576]{2,1,0:T(8,128)(2,1)}, u32[]{:S(2)}, u32[]{:S(2)}) async-start(bf16[64,6,576]{2,1,0:T(8,128)(2,1)} %pad_maximum_fusion), calls=%async_computation | async-start | bytes 1310720 | tf_op jit(solution)/shard_map/all_to_all | solution.py:164
  51.7 1.6 gather_fusion.11
  54.8 16.5 %all-to-all-done = bf16[64,6,576]{2,1,0:T(8,128)(2,1)} async-done(((bf16[64,6,576]{2,1,0:T(8,128)(2,1)}), bf16[64,6,576]{2,1,0:T(8,128)(2,1)}, u32[]{:S(2)}, u32[]{:S(2)}) %all-to-all-start) | async-done | bytes 442400 | tf_op jit(solution)/shard_map/all_to_all | solution.py:164
  73.7 1.9 copy.308
  75.7 1.8 gather_fusion.6
  77.4 2.1 gather_fusion.5
  79.6 12.1 %all_gather.11 = bf16[32,16,576]{2,0,1:T(8,128)(2,1)S(1)} all-gather(bf16[32,4,576]{2,0,1:T(8,128)(2,1)S(1)} %gather_fusion.5), channel_id=1, replica_groups=mesh['tok'=64,'head'=4] {'head'}, dimensions={1}, use_global_device_ids=true | all-gather | bytes 737280 | tf_op jit(solution)/shard_map/all_gather | solution.py:174
  92.4 1.4 copy.312
  93.9 4.5 %convert_reduce_fusion = (f32[512]{0:T(512)S(1)}, bf16[512,2496]{0,1:T(8,128)(2,1)}) fusion(pred[512,2496]{0,1:T(32,128)(4,1)S(1)} %copy.312, bf16[512,576]{1,0:T(8,128)(2,1)S(1)} %bitcast.144, bf16[2496,576]{0,1:T(8,128)(2,1)S(1)} %copy-done.12), kind=kOutput, calls=%fused_computation.13 | convolution fusion | flops 1478589952 | bytes 7301120 | tf_op jit(solution)/shard_map/qc,pc->qp/dot_general | solution.py:39
  98.6 4.4 %copy.310 = bf16[512,2496]{1,0:T(8,128)(2,1)} copy(bf16[512,2496]{0,1:T(8,128)(2,1)} %get-tuple-element.67) | data formatting | bytes 5111808 | tf_op jit(solution)/shard_map/exp | solution.py:46
  102.9 4.1 %fusion.10 = bf16[32,16,512]{2,1,0:T(8,128)(2,1)S(1)} fusion(bf16[2496,576]{0,1:T(8,128)(2,1)} %param.27, bf16[32,16,2496]{2,1,0:T(8,128)(2,1)} %bitcast.138, pred[32,2496]{1,0:T(8,128)(4,1)S(1)} %compare_and_fusion), kind=kOutput, calls=%fused_computation.29 | convolution fusion | flops 1310162944 | bytes 5847040 | tf_op jit(solution)/shard_map/khp,pl->khl/dot_general | solution.py:47
  107.1 1.2 copy.314
  108.3 4.2 %all-to-all-start.1 = ((bf16[35,16,512]{2,0,1:T(8,128)(2,1)}), bf16[35,16,512]{2,0,1:T(8,128)(2,1)}, u32[]{:S(2)}, u32[]{:S(2)}) async-start(bf16[35,16,512]{2,0,1:T(8,128)(2,1)} %copy.314), calls=%async_computation.1 | async-start | bytes 1310720 | tf_op jit(solution)/shard_map/all_to_all | solution.py:185
  114.0 6.6 %all-to-all-done.1 = bf16[35,16,512]{2,0,1:T(8,128)(2,1)} async-done(((bf16[35,16,512]{2,0,1:T(8,128)(2,1)}), bf16[35,16,512]{2,0,1:T(8,128)(2,1)}, u32[]{:S(2)}, u32[]{:S(2)}) %all-to-all-start.1) | async-done | bytes 573472 | tf_op jit(solution)/shard_map/all_to_all | solution.py:185
  120.6 1.4 copy.358
  123.9 1.2 fusion.21
  127.8 9.3 %all-to-all-start.2 = ((bf16[64,2,256]{2,1,0:T(2,128)(2,1)}), bf16[64,2,256]{2,1,0:T(2,128)(2,1)S(1)}, u32[]{:S(2)}, u32[]{:S(2)}) async-start(bf16[64,2,256]{2,1,0:T(2,128)(2,1)} %reshape.670), calls=%async_computation.2 | async-start | bytes 131072 | tf_op jit(solution)/shard_map/all_to_all | solution.py:214
  137.9 9.1 %all-to-all-done.2 = bf16[64,2,256]{2,1,0:T(2,128)(2,1)S(1)} async-done(((bf16[64,2,256]{2,1,0:T(2,128)(2,1)}), bf16[64,2,256]{2,1,0:T(2,128)(2,1)S(1)}, u32[]{:S(2)}, u32[]{:S(2)}) %all-to-all-start.2) | async-done | bytes 65568 | tf_op jit(solution)/shard_map/all_to_all | solution.py:214
  147.7 2.1 convolution_convert_fusion.1
  150.4 3.3 %all-to-all-start.3 = ((bf16[32,4,512]{2,0,1:T(8,128)(2,1)}), bf16[32,4,512]{2,0,1:T(8,128)(2,1)S(1)}, u32[]{:S(2)}, u32[]{:S(2)}) async-start(bf16[32,4,512]{2,0,1:T(8,128)(2,1)} %bitcast.127), calls=%async_computation.3 | async-start | bytes 262144 | tf_op jit(solution)/shard_map/all_to_all | solution.py:56
  153.7 4.8 %all-to-all-done.3 = bf16[32,4,512]{2,0,1:T(8,128)(2,1)S(1)} async-done(((bf16[32,4,512]{2,0,1:T(8,128)(2,1)}), bf16[32,4,512]{2,0,1:T(8,128)(2,1)S(1)}, u32[]{:S(2)}, u32[]{:S(2)}) %all-to-all-start.3) | async-done | bytes 131104 | tf_op jit(solution)/shard_map/all_to_all | solution.py:56
  158.8 12.5 %all-reduce.6 = (f32[32]{0:T(128)S(1)}, f32[32,64]{1,0:T(8,128)}) all-reduce(f32[32]{0:T(128)S(1)} %get-tuple-element.37, f32[32,64]{1,0:T(8,128)S(1)} %fusion.56), channel_id=1, replica_groups=mesh['tok'=64,'head'=4] {'head'}, use_global_device_ids=true, to_apply=%region_14.15 | all-reduce | flops 2080 | bytes 16640 | tf_op jit(solution)/shard_map/psum | solution.py:222
  171.5 2.6 gather_fusion.9
  174.0 1.9 reshape.555
  175.9 27.4 %all_to_all.77 = bf16[64,6,512]{2,1,0:T(8,128)(2,1)} all-to-all(bf16[64,6,512]{2,1,0:T(8,128)(2,1)} %reshape.555), channel_id=1, replica_groups=mesh['tok'=64,'head'=4] {'tok'}, dimensions={0} | all-to-all | bytes 786432 | tf_op jit(solution)/shard_map/all_to_all | solution.py:252
  203.3 1.2 broadcast_in_dim.156
  206.5 23.0 %all_to_all.78 = bf16[4,384,512]{1,2,0:T(8,128)(2,1)S(1)} all-to-all(bf16[4,384,512]{1,2,0:T(8,128)(2,1)S(1)} %broadcast_in_dim.157), channel_id=1, replica_groups=mesh['tok'=64,'head'=4] {'head'}, dimensions={0} | all-to-all | bytes 3145728 | tf_op jit(solution)/shard_map/all_to_all | solution.py:259
  230.7 1.7 fusion.8
  232.4 5.5 %convolution_convert_fusion = bf16[384,2048]{1,0:T(8,128)(2,1)} fusion(bf16[1,352,2048]{2,1,0:T(8,128)(2,1)} %param.35, bf16[384,2048]{0,1:T(8,128)(2,1)} %bitcast.141, bf16[1,2048,352]{1,2,0:T(8,128)(2,1)} %param.34, f32[384,352]{0,1:T(8,128)} %fusion.8), kind=kOutput, calls=%fused_computation.16 | convolution fusion | flops 1108893696 | bytes 6569984 | tf_op jit(solution)/shard_map/dot_general | solution.py:273
  237.9 2.7 copy.357
  240.6 4.5 %all-to-all-start.6 = ((bf16[384,4,512]{2,0,1:T(8,128)(2,1)}), bf16[384,4,512]{2,0,1:T(8,128)(2,1)}, u32[]{:S(2)}, u32[]{:S(2)}) async-start(bf16[384,4,512]{2,0,1:T(8,128)(2,1)} %bitcast.131), calls=%async_computation.6 | async-start | bytes 3145728 | tf_op jit(solution)/shard_map/all_to_all | solution.py:56
  245.2 19.5 %all-to-all-done.6 = bf16[384,4,512]{2,0,1:T(8,128)(2,1)} async-done(((bf16[384,4,512]{2,0,1:T(8,128)(2,1)}), bf16[384,4,512]{2,0,1:T(8,128)(2,1)}, u32[]{:S(2)}, u32[]{:S(2)}) %all-to-all-start.6) | async-done | bytes 1572896 | tf_op jit(solution)/shard_map/all_to_all | solution.py:56
  264.7 1.8 reduce_sum.160
  267.4 8.1 %all-to-all-start.7 = ((bf16[64,6,512]{2,1,0:T(8,128)(2,1)}), bf16[64,6,512]{2,1,0:T(8,128)(2,1)}, u32[]{:S(2)}, u32[]{:S(2)}) async-start(bf16[64,6,512]{2,1,0:T(8,128)(2,1)} %reshape.557), calls=%async_computation.7 | async-start | bytes 1048576 | tf_op jit(solution)/shard_map/all_to_all | solution.py:276
  277.2 15.5 %all-to-all-done.7 = bf16[64,6,512]{2,1,0:T(8,128)(2,1)} async-done(((bf16[64,6,512]{2,1,0:T(8,128)(2,1)}), bf16[64,6,512]{2,1,0:T(8,128)(2,1)}, u32[]{:S(2)}, u32[]{:S(2)}) %all-to-all-start.7) | async-done | bytes 393248 | tf_op jit(solution)/shard_map/all_to_all | solution.py:276
  292.7 1.2 reshape.558
  293.9 1.7 gather_fusion.10
  295.6 1.8 reshape.654
  297.3 1.9 multiply_reduce_fusion
  (139 shorter events, 31.3 us)
Async XLA Ops:
  0.6 23.1 %copy-start = (bf16[2048,768]{1,0:T(8,128)(2,1)S(1)}, bf16[2048,768]{1,0:T(8,128)(2,1)}, u32[]{:S(2)}) copy-start(bf16[2048,768]{1,0:T(8,128)(2,1)} %param.22) | copy-start | bytes 9437188
  0.6 9.6 %copy-start.4 = (bf16[32,512]{1,0:T(8,128)(2,1)S(1)}, bf16[32,512]{1,0:T(8,128)(2,1)}, u32[]{:S(2)}) copy-start(bf16[32,512]{1,0:T(8,128)(2,1)} %param.20) | copy-start | bytes 98308
  23.7 4.1 %copy-start.11 = (f32[32]{0:T(128)S(1)}, f32[32]{0:T(128)}, u32[]{:S(2)}) copy-start(f32[32]{0:T(128)} %multiply_power_fusion) | copy-start | bytes 388
  29.3 5.4 %copy-start.1 = (bf16[32,576]{1,0:T(8,128)(2,1)}, bf16[32,576]{1,0:T(8,128)(2,1)S(1)}, u32[]{:S(2)}) copy-start(bf16[32,576]{1,0:T(8,128)(2,1)S(1)} %pad_maximum_fusion.3) | copy-start | bytes 110596
  33.1 18.2 %copy-start.7 = (s32[32,6]{0,1:T(8,128)S(1)}, s32[32,6]{0,1:T(8,128)}, u32[]{:S(2)}) copy-start(s32[32,6]{0,1:T(8,128)} %param.32) | copy-start | bytes 2308
  37.2 34.2 %all-to-all-start = ((bf16[64,6,576]{2,1,0:T(8,128)(2,1)}), bf16[64,6,576]{2,1,0:T(8,128)(2,1)}, u32[]{:S(2)}, u32[]{:S(2)}) async-start(bf16[64,6,576]{2,1,0:T(8,128)(2,1)} %pad_maximum_fusion), calls=%async_computation | async-start | bytes 1310720 | tf_op jit(solution)/shard_map/all_to_all | solution.py:164
  92.0 1.8 copy-start.12
  108.3 12.4 %all-to-all-start.1 = ((bf16[35,16,512]{2,0,1:T(8,128)(2,1)}), bf16[35,16,512]{2,0,1:T(8,128)(2,1)}, u32[]{:S(2)}, u32[]{:S(2)}) async-start(bf16[35,16,512]{2,0,1:T(8,128)(2,1)} %copy.314), calls=%async_computation.1 | async-start | bytes 1310720 | tf_op jit(solution)/shard_map/all_to_all | solution.py:185
  114.0 8.3 %copy-start.10 = (f32[32,1,4]{0,2,1:T(4,128)S(1)}, f32[32,1,4]{0,2,1:T(4,128)}, u32[]{:S(2)}) copy-start(f32[32,1,4]{0,2,1:T(4,128)} %copy.333) | copy-start | bytes 1540
  122.1 15.1 %copy-start.9 = (s32[384]{0:T(512)S(1)}, s32[384]{0:T(512)}, u32[]{:S(2)}) copy-start(s32[384]{0:T(512)} %get-tuple-element.30) | copy-start | bytes 4612
  127.8 19.1 %all-to-all-start.2 = ((bf16[64,2,256]{2,1,0:T(2,128)(2,1)}), bf16[64,2,256]{2,1,0:T(2,128)(2,1)S(1)}, u32[]{:S(2)}, u32[]{:S(2)}) async-start(bf16[64,2,256]{2,1,0:T(2,128)(2,1)} %reshape.670), calls=%async_computation.2 | async-start | bytes 131072 | tf_op jit(solution)/shard_map/all_to_all | solution.py:214
  147.6 11.1 %copy-start.5 = (bf16[512,64]{0,1:T(8,128)(2,1)S(1)}, bf16[512,64]{0,1:T(8,128)(2,1)}, u32[]{:S(2)}) copy-start(bf16[512,64]{0,1:T(8,128)(2,1)} %param.31) | copy-start | bytes 196612
  147.6 11.0 %copy-start.8 = (f32[512]{0:T(512)S(1)}, f32[512]{0:T(512)}, u32[]{:S(2)}) copy-start(f32[512]{0:T(512)} %param.30) | copy-start | bytes 6148
  150.4 8.1 %all-to-all-start.3 = ((bf16[32,4,512]{2,0,1:T(8,128)(2,1)}), bf16[32,4,512]{2,0,1:T(8,128)(2,1)S(1)}, u32[]{:S(2)}, u32[]{:S(2)}) async-start(bf16[32,4,512]{2,0,1:T(8,128)(2,1)} %bitcast.127), calls=%async_computation.3 | async-start | bytes 262144 | tf_op jit(solution)/shard_map/all_to_all | solution.py:56
  158.7 12.7 %copy-start.3 = (bf16[32,512]{1,0:T(8,128)(2,1)}, bf16[32,512]{1,0:T(8,128)(2,1)S(1)}, u32[]{:S(2)}) copy-start(bf16[32,512]{1,0:T(8,128)(2,1)S(1)} %get-tuple-element.38) | copy-start | bytes 98308
  206.5 24.2 %copy-start.13 = (bf16[1,2048,352]{1,2,0:T(8,128)(2,1)S(1)}, bf16[1,2048,352]{1,2,0:T(8,128)(2,1)}, u32[]{:S(2)}) copy-start(bf16[1,2048,352]{1,2,0:T(8,128)(2,1)} %param.33) | copy-start | bytes 4325380
  229.6 1.1 copy-start.2
  240.6 4.5 %copy-start.6 = (s32[32,6]{1,0:T(8,128)S(1)}, s32[32,6]{1,0:T(8,128)}, u32[]{:S(2)}) copy-start(s32[32,6]{1,0:T(8,128)} %get-tuple-element.35) | copy-start | bytes 2308
  240.6 24.1 %all-to-all-start.6 = ((bf16[384,4,512]{2,0,1:T(8,128)(2,1)}), bf16[384,4,512]{2,0,1:T(8,128)(2,1)}, u32[]{:S(2)}, u32[]{:S(2)}) async-start(bf16[384,4,512]{2,0,1:T(8,128)(2,1)} %bitcast.131), calls=%async_computation.6 | async-start | bytes 3145728 | tf_op jit(solution)/shard_map/all_to_all | solution.py:56
  267.4 25.3 %all-to-all-start.7 = ((bf16[64,6,512]{2,1,0:T(8,128)(2,1)}), bf16[64,6,512]{2,1,0:T(8,128)(2,1)}, u32[]{:S(2)}, u32[]{:S(2)}) async-start(bf16[64,6,512]{2,1,0:T(8,128)(2,1)} %reshape.557), calls=%async_computation.7 | async-start | bytes 1048576 | tf_op jit(solution)/shard_map/all_to_all | solution.py:276
